TPU v7x, 256 devices: a whole 4x4x8 slice. The times are simulated.
256 devices in a mesh: seq: 64 (over z, x, core), head: 4 (over y).
Axes of the slice: x: 4, y: 4, z: 8, core: 2. Of those that a mesh axis runs over, the one named last changes fastest.
Arguments:
- queries: bfloat16 [32768, 1536], P('seq', 'head'), may hold values from -6 to 6
- keys: bfloat16 [32768, 1536], P('seq', 'head'), may hold values from -6 to 6
- values: bfloat16 [32768, 1536], P('seq', 'head'), may hold values from -6 to 6
- out_weight: bfloat16 [1536, 1536], P('head'), may hold values from -0.625 to 0.625
- cotangent: bfloat16 [32768, 1536], P('seq', 'head'), may hold values from -6 to 6
- routes: int32 [64, 2], replicated, may hold values from 0 to 63, as said below
- shot_ids: int32 [32768], P('seq'), may hold values from 0 to 31, never falling along the last dimension, each value on 1 to 2048 neighbouring positions
Outputs:
- attn_out: bfloat16 [32768, 1536], P('seq', 'head')
- grad_queries: bfloat16 [32768, 1536], P('seq', 'head')
- grad_keys: bfloat16 [32768, 1536], P('seq', 'head')
- grad_values: bfloat16 [32768, 1536], P('seq', 'head')
Inputs may be any that keep to these rules, and one draw needn't show every extreme that they name: routes[c, j] names a block of another device whose index of seq differs from that of block c by at most 2; the 2 routes of the blocks of one device name blocks of distinct devices.
All inputs are finite; a program needn't handle non-finite values.
Results may differ from a plain program's by a relative error of at most 0.025.
Values may be sent and summed in bfloat16 or wider, within the bound.
No kernel may reach another device: no remote copies, remote signals or barrier semaphores. Data moves between devices by JAX's collectives and lax.ppermute only.
A program may use at most 64 MiB of HBM per device.

v0:
```python
import jax
import jax.numpy as jnp
from jax import lax
from jax.experimental import pallas as pl
from jax.experimental.pallas import tpu as pltpu
from jax.sharding import PartitionSpec as P


HEAD_DIM = 128
NEG_BIG = -1e30
INTERPRET = None


def shifted(block, axis, distance):
    devices = range(lax.axis_size(axis))
    route = [(i - distance, i) for i in devices if i - distance in devices]
    return lax.ppermute(block, axis, route)


def ring_shift(block, axis, distance):
    size = lax.axis_size(axis)
    return lax.ppermute(block, axis, [(i, (i + distance) % size) for i in range(size)])


def head_slice(array, group, width):
    return lax.dynamic_slice_in_dim(array, group * width, width, 1)


def fold_cotangent(cotangent, out_weight):
    groups = lax.axis_size("head")
    me = lax.axis_index("head")
    rows, width = cotangent.shape
    half = rows // 2
    from_prev = ring_shift(cotangent, "head", 1)
    from_next = ring_shift(cotangent, "head", -1)
    far_a = ring_shift(cotangent[:half], "head", 2)
    far_b = ring_shift(cotangent[half:], "head", -2)
    far = jnp.concatenate([far_a, far_b], axis=0)
    nt = (((1,), (1,)), ((), ()))
    acc = None
    for piece, group in ((cotangent, me), (from_prev, me - 1), (from_next, me + 1), (far, me + 2)):
        w_cols = head_slice(out_weight, group % groups, width)
        part = lax.dot_general(piece, w_cols, nt, preferred_element_type=jnp.float32)
        acc = part if acc is None else acc + part
    return acc.astype(jnp.bfloat16)


def project_out(attn, out_weight):
    groups = lax.axis_size("head")
    me = lax.axis_index("head")
    rows, width = attn.shape
    half = rows // 2

    def part(group):
        w_cols = head_slice(out_weight, group % groups, width)
        return jnp.dot(attn, w_cols, preferred_element_type=jnp.float32).astype(jnp.bfloat16)

    far = part(me + 2)
    near_up = part(me + 1)
    near_down = part(me - 1)
    got_a = ring_shift(far[:half], "head", 2)
    got_b = ring_shift(far[half:], "head", -2)
    from_prev = ring_shift(near_up, "head", 1)
    from_next = ring_shift(near_down, "head", -1)
    total = (
        jnp.dot(attn, head_slice(out_weight, me, width), preferred_element_type=jnp.float32)
        + from_prev.astype(jnp.float32)
        + from_next.astype(jnp.float32)
        + jnp.concatenate([got_a, got_b], axis=0).astype(jnp.float32)
    )
    return total.astype(jnp.bfloat16)


def partner_swap(block, axis):
    size = lax.axis_size(axis)
    return lax.ppermute(block, axis, [(i, i ^ 1) for i in range(size)])


def even_to_odd(block, axis):
    size = lax.axis_size(axis)
    return lax.ppermute(block, axis, [(i, i + 1) for i in range(0, size - 1, 2)])


def odd_to_even(block, axis):
    size = lax.axis_size(axis)
    return lax.ppermute(block, axis, [(i, i - 1) for i in range(1, size, 2)])


def attn_kernel(sel_ref, q_ref, k0_ref, v0_ref, *refs):
    n_cand = 5
    cand_k = refs[0:2 * n_cand:2]
    cand_v = refs[1:2 * n_cand:2]
    g_ref, srow_ref, scol_ref, attn_ref, dq_ref, self_ref, pa_ref, pb_ref, far_ref = refs[2 * n_cand:]
    scale = HEAD_DIM ** (-0.5)
    d = HEAD_DIM
    h = pl.program_id(0)

    @pl.when(h == 0)
    def _():
        pa_ref[...] = jnp.zeros_like(pa_ref)
        pb_ref[...] = jnp.zeros_like(pb_ref)
        far_ref[...] = jnp.zeros_like(far_ref)

    def pick(cands, slot):
        idx = sel_ref[slot]
        out = cands[0][...]
        for c in range(1, n_cand):
            out = jnp.where(idx == c, cands[c][...], out)
        return out

    ks = [k0_ref[...], pick(cand_k, 0), pick(cand_k, 1)]
    vs = [v0_ref[...], pick(cand_v, 0), pick(cand_v, 1)]
    q = q_ref[...]
    g = g_ref[...]
    nt = (((1,), (1,)), ((), ()))
    tn = (((0,), (0,)), ((), ()))
    scores = [lax.dot_general(q, k, nt, preferred_element_type=jnp.float32) * scale for k in ks]
    visible = srow_ref[...] == scol_ref[...]
    scores[0] = jnp.where(visible, scores[0], NEG_BIG)
    top = jnp.max(scores[0], axis=1, keepdims=True)
    for s in scores[1:]:
        top = jnp.maximum(top, jnp.max(s, axis=1, keepdims=True))
    weights = [jnp.exp(s - top) for s in scores]
    weights[0] = jnp.where(visible, weights[0], 0.0)
    total = weights[0].sum(axis=1, keepdims=True)
    for w in weights[1:]:
        total = total + w.sum(axis=1, keepdims=True)
    inv = 1.0 / total
    probs = [w * inv for w in weights]
    low = [p.astype(jnp.bfloat16) for p in probs]
    acc = jnp.dot(low[0], vs[0], preferred_element_type=jnp.float32)
    for j in (1, 2):
        acc = acc + jnp.dot(low[j], vs[j], preferred_element_type=jnp.float32)
    attn = acc.astype(jnp.bfloat16)
    attn_ref[...] = attn
    gf = g.astype(jnp.float32)
    delta = jnp.sum(attn.astype(jnp.float32) * gf, axis=1, keepdims=True)
    dq = None
    cols = pl.ds(pl.multiple_of(h * d, d), d)
    for j in range(3):
        dp = lax.dot_general(g, vs[j], nt, preferred_element_type=jnp.float32)
        ds = (probs[j] * (dp - delta) * scale).astype(jnp.bfloat16)
        part = jnp.dot(ds, ks[j], preferred_element_type=jnp.float32)
        dq = part if dq is None else dq + part
        dk = lax.dot_general(ds, q, tn, preferred_element_type=jnp.float32)
        dv = lax.dot_general(low[j], g, tn, preferred_element_type=jnp.float32)
        if j == 0:
            self_ref[0] = dk
            self_ref[1] = dv
            continue
        dk = dk.astype(jnp.bfloat16)
        dv = dv.astype(jnp.bfloat16)
        off = sel_ref[2 + j]
        for value, dests in ((-2, ((far_ref, 0),)), (2, ((far_ref, 1),)),
                             (1, ((pa_ref, 0), (pb_ref, 1))), (-1, ((pa_ref, 1), (pb_ref, 0)))):
            @pl.when(off == value)
            def _():
                for ref, slot in dests:
                    ref[slot, 0, :, cols] = dk
                    ref[slot, 1, :, cols] = dv
    dq_ref[...] = dq.astype(jnp.bfloat16)


def attention(sel, queries, keys, values, cands, grad_attn, shot_ids):
    rows, columns = queries.shape
    heads = columns // HEAD_DIM
    d = HEAD_DIM
    spec_q = pl.BlockSpec((rows, d), lambda h, s: (0, h))
    spec_ck = pl.BlockSpec((None, rows, d), lambda h, s: (0, 0, h))
    spec_cv = pl.BlockSpec((None, rows, d), lambda h, s: (1, 0, h))
    spec_self = pl.BlockSpec((2, rows, d), lambda h, s: (0, 0, h))
    spec_pair = pl.BlockSpec((2, 2, rows, columns), lambda h, s: (0, 0, 0, 0))
    cand_specs = []
    cand_args = []
    for c in cands:
        cand_specs += [spec_ck, spec_cv]
        cand_args += [c, c]
    grid_spec = pltpu.PrefetchScalarGridSpec(
        num_scalar_prefetch=1,
        grid=(heads,),
        in_specs=[spec_q, spec_q, spec_q] + cand_specs + [spec_q,
                  pl.BlockSpec((rows, 1), lambda h, s: (0, 0)),
                  pl.BlockSpec((1, rows), lambda h, s: (0, 0))],
        out_specs=[spec_q, spec_q, spec_self, spec_pair, spec_pair, spec_pair],
    )
    pair_shape = jax.ShapeDtypeStruct((2, 2, rows, columns), jnp.bfloat16)
    out_shape = [
        jax.ShapeDtypeStruct((rows, columns), jnp.bfloat16),
        jax.ShapeDtypeStruct((rows, columns), jnp.bfloat16),
        jax.ShapeDtypeStruct((2, rows, columns), jnp.float32),
        pair_shape,
        pair_shape,
        pair_shape,
    ]
    kwargs = {}
    if INTERPRET is not None:
        kwargs["interpret"] = INTERPRET
    return pl.pallas_call(
        attn_kernel,
        grid_spec=grid_spec,
        out_shape=out_shape,
        compiler_params=pltpu.CompilerParams(vmem_limit_bytes=48 * 1024 * 1024),
        **kwargs,
    )(sel, queries, keys, values, *cand_args, grad_attn, shot_ids.reshape(rows, 1), shot_ids.reshape(1, rows))


def on_device(queries, keys, values, out_weight, cotangent, routes, shot_ids):
    seq_index = lax.axis_index("seq")
    parity = seq_index % 2
    grad_attn = fold_cotangent(cotangent, out_weight)
    own_kv = jnp.stack([keys, values])
    from_left2 = shifted(own_kv, "seq", 2)
    from_right2 = shifted(own_kv, "seq", -2)
    partner_own = partner_swap(own_kv, "seq")
    relay_to_odd = even_to_odd(from_right2, "seq")
    relay_to_even = odd_to_even(from_left2, "seq")
    partner_off = 1 - 2 * parity
    offs = (routes[seq_index] - seq_index).astype(jnp.int32)
    relay_idx = jnp.where(parity == 1, 2, 3)
    pick = jnp.where(offs == -2, 0, jnp.where(offs == 2, 4, jnp.where(offs == partner_off, 1, relay_idx)))
    sel = jnp.concatenate([pick.astype(jnp.int32), jnp.zeros((1,), jnp.int32), offs])
    cands = (from_left2, partner_own, relay_to_odd, relay_to_even, from_right2)
    attn, grad_q, self_term, pair_a, pair_b, far = attention(
        sel, queries, keys, values, cands, grad_attn, shot_ids
    )
    attn_out = project_out(attn, out_weight)
    got_a = even_to_odd(pair_a, "seq")
    got_b = odd_to_even(pair_b, "seq")
    up_plus = (far[1].astype(jnp.float32) + got_b[1].astype(jnp.float32)).astype(jnp.bfloat16)
    up_minus = (far[0].astype(jnp.float32) + got_a[1].astype(jnp.float32)).astype(jnp.bfloat16)
    got_from_left = shifted(up_plus, "seq", 2)
    got_from_right = shifted(up_minus, "seq", -2)
    total = (
        self_term
        + got_a[0].astype(jnp.float32)
        + got_b[0].astype(jnp.float32)
        + got_from_left.astype(jnp.float32)
        + got_from_right.astype(jnp.float32)
    )
    rounded = total.astype(jnp.bfloat16)
    return (attn_out, grad_q, rounded[0], rounded[1])


def solution(mesh):
    in_specs = (
        P("seq", "head"),
        P("seq", "head"),
        P("seq", "head"),
        P("head", None),
        P("seq", "head"),
        P(),
        P("seq"),
    )
    out_specs = (P("seq", "head"), P("seq", "head"), P("seq", "head"), P("seq", "head"))

    return jax.shard_map(on_device, mesh=mesh, in_specs=in_specs, out_specs=out_specs, check_vma=False)
```

profile of v0, /device:TPU:126, one launch (start us, length us, event | category | flops | bytes accessed | tf_op | source)
XLA Modules:
  0.0 108.1 jit_solution(16362346489416187812)
XLA Ops:
  0.7 2.2 %pad_maximum_fusion = bf16[2,512,384]{2,1,0:T(8,128)(2,1)} fusion(bf16[1,512,384]{2,1,0:T(8,128)(2,1)} %bitcast.36, bf16[1,512,384]{2,1,0:T(8,128)(2,1)} %bitcast.35), kind=kLoop, calls=%fused_computation.23 | loop fusion | flops 393216 | bytes 1572864 | tf_op jit(solution)/shard_map/stack | solution.py:211
  2.9 2.9 %collective-permute-start.2 = (bf16[2,512,384]{2,1,0:T(8,128)(2,1)}, bf16[2,512,384]{2,1,0:T(8,128)(2,1)S(1)}, u32[]{:S(2)}, u32[]{:S(2)}) collective-permute-start(bf16[2,512,384]{2,1,0:T(8,128)(2,1)} %pad_maximum_fusion), channel_id=1, source_target_pairs={{8,0},{12,4},{16,8},{20,12},{24,16},{28,20},{32,24},{36,28},{40,32... | collective-permute-start | bytes 2359304 | tf_op jit(solution)/shard_map/ppermute | solution.py:17
  5.7 6.4 %collective-permute-start = (bf16[2,512,384]{2,1,0:T(8,128)(2,1)}, bf16[2,512,384]{2,1,0:T(8,128)(2,1)S(1)}, u32[]{:S(2)}, u32[]{:S(2)}) collective-permute-start(bf16[2,512,384]{2,1,0:T(8,128)(2,1)} %pad_maximum_fusion), channel_id=1, source_target_pairs={{0,8},{4,12},{8,16},{12,20},{16,24},{20,28},{24,32},{28,36},{32,40... | collective-permute-start | bytes 2359304 | tf_op jit(solution)/shard_map/ppermute | solution.py:17
  12.5 0.8 fusion.36
  13.3 2.6 %collective-permute-start.7 = (bf16[256,384]{1,0:T(8,128)(2,1)}, bf16[256,384]{1,0:T(8,128)(2,1)}, u32[]{:S(2)}, u32[]{:S(2)}) collective-permute-start(bf16[256,384]{1,0:T(8,128)(2,1)} %get-tuple-element.22), channel_id=1, source_target_pairs={{0,2},{1,3},{2,0},{3,1},{4,6},{5,7},{6,4},{7,5},{8,10},{9,11},{10,... | collective-permute-start | bytes 589832 | tf_op jit(solution)/shard_map/ppermute | solution.py:22
  15.9 0.9 collective-permute-start.8
  17.0 1.4 %fusion.16 = f32[384,512]{0,1:T(8,128)} fusion(bf16[512,384]{1,0:T(8,128)(2,1)S(1)} %copy-done.6, bf16[384,1536]{1,0:T(8,128)(2,1)S(1)} %copy-done, s32[]{:T(128)S(6)} %select_n.72), kind=kOutput, calls=%fused_computation.31 | convolution fusion | flops 150994944 | bytes 1474564 | tf_op jit(solution)/shard_map/dot_general | solution.py:43
  18.5 4.3 %collective-permute-done.7 = bf16[256,384]{1,0:T(8,128)(2,1)} collective-permute-done((bf16[256,384]{1,0:T(8,128)(2,1)}, bf16[256,384]{1,0:T(8,128)(2,1)}, u32[]{:S(2)}, u32[]{:S(2)}) %collective-permute-start.7) | collective-permute-done | bytes 196640 | tf_op jit(solution)/shard_map/ppermute | solution.py:22
  22.9 4.8 %collective-permute-done.2.refs_8_.refs_9_ = bf16[2,512,384]{2,1,0:T(8,128)(2,1)S(1)} collective-permute-done((bf16[2,512,384]{2,1,0:T(8,128)(2,1)}, bf16[2,512,384]{2,1,0:T(8,128)(2,1)S(1)}, u32[]{:S(2)}, u32[]{:S(2)}) %collective-permute-start.2) | collective-permute-done | bytes 786464 | tf_op jit(solution)/shard_map/ppermute | solution.py:17
  27.7 1.3 %collective-permute-start.3 = (bf16[2,512,384]{2,1,0:T(8,128)(2,1)S(1)}, bf16[2,512,384]{2,1,0:T(8,128)(2,1)S(1)}, u32[]{:S(2)}, u32[]{:S(2)}) collective-permute-start(bf16[2,512,384]{2,1,0:T(8,128)(2,1)S(1)} %collective-permute-done.2.refs_8_.refs_9_), channel_id=1, source_target_pairs={{0,4},{8,12},{16,20},{24,28},{32,36},{40,44},{48,52},{56,60},{64,6... | collective-permute-start | bytes 2359304 | tf_op jit(solution)/shard_map/ppermute | solution.py:81
  29.1 1.3 %collective-permute-start.4 = (bf16[2,512,384]{2,1,0:T(8,128)(2,1)S(1)}, bf16[2,512,384]{2,1,0:T(8,128)(2,1)S(1)}, u32[]{:S(2)}, u32[]{:S(2)}) collective-permute-start(bf16[2,512,384]{2,1,0:T(8,128)(2,1)S(1)} %collective-permute-done.refs_0_.refs_1_), channel_id=1, source_target_pairs={{4,0},{12,8},{20,16},{28,24},{36,32},{44,40},{52,48},{60,56},{68,6... | collective-permute-start | bytes 2359304 | tf_op jit(solution)/shard_map/ppermute | solution.py:86
  30.4 2.8 %collective-permute-start.6 = (bf16[512,384]{1,0:T(8,128)(2,1)S(1)}, bf16[512,384]{1,0:T(8,128)(2,1)S(1)}, u32[]{:S(2)}, u32[]{:S(2)}) collective-permute-start(bf16[512,384]{1,0:T(8,128)(2,1)S(1)} %copy-done.6), channel_id=1, source_target_pairs={{0,3},{1,0},{2,1},{3,2},{4,7},{5,4},{6,5},{7,6},{8,11},{9,8},{10,9... | collective-permute-start | bytes 1179656 | tf_op jit(solution)/shard_map/ppermute | solution.py:22
  33.2 1.4 %fusion.11 = f32[512,384]{1,0:T(8,128)S(1)} fusion(bf16[256,384]{1,0:T(8,128)(2,1)} %collective-permute-done.8, bf16[256,384]{1,0:T(8,128)(2,1)} %collective-permute-done.7, bf16[384,1536]{1,0:T(8,128)(2,1)S(1)} %copy-done, s32[]{:T(128)S(6)} %select_n.78), kind=kOutput, calls=%fused_computation.26 | convolution fusion | flops 151781376 | bytes 1474564 | tf_op jit(solution)/shard_map/dot_general | solution.py:43
  34.6 1.4 %convolution_add_fusion.2 = f32[384,512]{0,1:T(8,128)S(1)} fusion(f32[384,512]{0,1:T(8,128)S(1)} %copy-done.5, bf16[512,384]{1,0:T(8,128)(2,1)} %collective-permute-done.5, bf16[384,1536]{1,0:T(8,128)(2,1)S(1)} %copy-done, s32[]{:T(128)S(6)} %select_n.74), kind=kOutput, calls=%fused_computation.10 | convolution fusion | flops 151191552 | bytes 2260996 | tf_op jit(solution)/shard_map/dot_general | solution.py:43
  36.1 8.5 %collective-permute-done.6 = bf16[512,384]{1,0:T(8,128)(2,1)S(1)} collective-permute-done((bf16[512,384]{1,0:T(8,128)(2,1)S(1)}, bf16[512,384]{1,0:T(8,128)(2,1)S(1)}, u32[]{:S(2)}, u32[]{:S(2)}) %collective-permute-start.6) | collective-permute-done | bytes 393248 | tf_op jit(solution)/shard_map/ppermute | solution.py:22
  45.1 19.2 %shard_map.102 = (bf16[512,384]{1,0:T(8,128)(2,1)S(1)}, bf16[512,384]{1,0:T(8,128)(2,1)}, f32[2,512,384]{2,1,0:T(8,128)}, bf16[2,2,512,384]{3,2,1,0:T(8,128)(2,1...) custom-call(s32[5]{0:T(128)S(1)} %pad_add_fusion.sel_ref, bf16[512,384]{1,0:T(8,128)(2,1)S(1)} %copy-done.3, ...), custom_call_target="tpu_custom_call" | custom-call | tf_op jit(solution)/shard_map/pallas_call | solution.py:198
  64.3 2.4 %collective-permute-start.13 = (bf16[2,2,512,384]{3,2,1,0:T(8,128)(2,1)}, bf16[2,2,512,384]{3,2,1,0:T(8,128)(2,1)S(1)}, u32[]{:S(2)}, u32[]{:S(2)}) collective-permute-start(bf16[2,2,512,384]{3,2,1,0:T(8,128)(2,1)} %get-tuple-element.13), channel_id=1, source_target_pairs={{0,4},{8,12},{16,20},{24,28},{32,36},{40,44},{48,52},{56,60},{64,6... | collective-permute-start | bytes 4718600 | tf_op jit(solution)/shard_map/ppermute | solution.py:81
  66.7 1.3 %collective-permute-start.14 = (bf16[2,2,512,384]{3,2,1,0:T(8,128)(2,1)}, bf16[2,2,512,384]{3,2,1,0:T(8,128)(2,1)S(1)}, u32[]{:S(2)}, u32[]{:S(2)}) collective-permute-start(bf16[2,2,512,384]{3,2,1,0:T(8,128)(2,1)} %get-tuple-element.14), channel_id=1, source_target_pairs={{4,0},{12,8},{20,16},{28,24},{36,32},{44,40},{52,48},{60,56},{68,6... | collective-permute-start | bytes 4718600 | tf_op jit(solution)/shard_map/ppermute | solution.py:86
  68.4 0.7 fusion.35
  69.1 1.3 %collective-permute-start.11 = (bf16[256,384]{1,0:T(8,128)(2,1)S(1)}, bf16[256,384]{1,0:T(8,128)(2,1)}, u32[]{:S(2)}, u32[]{:S(2)}) collective-permute-start(bf16[256,384]{1,0:T(8,128)(2,1)S(1)} %get-tuple-element.20), channel_id=1, source_target_pairs={{0,2},{1,3},{2,0},{3,1},{4,6},{5,7},{6,4},{7,5},{8,10},{9,11},{10,... | collective-permute-start | bytes 589832 | tf_op jit(solution)/shard_map/ppermute | solution.py:22
  70.9 1.4 %collective-permute-done.14 = bf16[2,2,512,384]{3,2,1,0:T(8,128)(2,1)S(1)} collective-permute-done((bf16[2,2,512,384]{3,2,1,0:T(8,128)(2,1)}, bf16[2,2,512,384]{3,2,1,0:T(8,128)(2,1)S(1)}, u32[]{:S(2)}, u32[]{:S(2)}) %collective-permute-start.14) | collective-permute-done | bytes 1572896 | tf_op jit(solution)/shard_map/ppermute | solution.py:86
  72.2 1.6 %fusion.9 = (bf16[2,512,384]{2,1,0:T(8,128)(2,1)}, bf16[2,512,384]{2,1,0:T(8,128)(2,1)}) fusion(bf16[2,2,512,384]{3,2,1,0:T(8,128)(2,1)S(1)} %collective-permute-done.14, bf16[2,2,512,384]{3,2,1,0:T(8,128)(2,1)S(1)} %copy-done.11, bf16[2,2,512,384]{3,2,1,0:T(8,128)(2,1)S(1)} %collective-permute-done.13), kind=kLoop, calls=%fused_computation.19 | loop fusion | flops 3145728 | bytes 4718592 | tf_op jit(solution)/shard_map/convert_element_type | solution.py:229
  73.9 6.2 %collective-permute-start.15 = (bf16[2,512,384]{2,1,0:T(8,128)(2,1)}, bf16[2,512,384]{2,1,0:T(8,128)(2,1)}, u32[]{:S(2)}, u32[]{:S(2)}) collective-permute-start(bf16[2,512,384]{2,1,0:T(8,128)(2,1)} %get-tuple-element.16), channel_id=1, source_target_pairs={{0,8},{4,12},{8,16},{12,20},{16,24},{20,28},{24,32},{28,36},{32,40... | collective-permute-start | bytes 2359304 | tf_op jit(solution)/shard_map/ppermute | solution.py:17
  80.1 2.1 %collective-permute-start.16 = (bf16[2,512,384]{2,1,0:T(8,128)(2,1)}, bf16[2,512,384]{2,1,0:T(8,128)(2,1)}, u32[]{:S(2)}, u32[]{:S(2)}) collective-permute-start(bf16[2,512,384]{2,1,0:T(8,128)(2,1)} %get-tuple-element.17), channel_id=1, source_target_pairs={{8,0},{12,4},{16,8},{20,12},{24,16},{28,20},{32,24},{36,28},{40,32... | collective-permute-start | bytes 2359304 | tf_op jit(solution)/shard_map/ppermute | solution.py:17
  82.1 1.1 %convolution_convert_fusion.2 = bf16[512,384]{1,0:T(8,128)(2,1)} fusion(bf16[512,384]{1,0:T(8,128)(2,1)S(1)} %get-tuple-element.10, bf16[384,1536]{1,0:T(8,128)(2,1)S(1)} %copy-done, s32[]{:T(128)S(6)} %select_n.76), kind=kOutput, calls=%fused_computation.18 | convolution fusion | flops 151191552 | bytes 1081348 | tf_op jit(solution)/shard_map/dot_general | solution.py:56
  83.3 2.0 %collective-permute-start.10 = (bf16[512,384]{1,0:T(8,128)(2,1)S(1)}, bf16[512,384]{1,0:T(8,128)(2,1)}, u32[]{:S(2)}, u32[]{:S(2)}) collective-permute-start(bf16[512,384]{1,0:T(8,128)(2,1)S(1)} %convolution_convert_fusion.1), channel_id=1, source_target_pairs={{0,3},{1,0},{2,1},{3,2},{4,7},{5,4},{6,5},{7,6},{8,11},{9,8},{10,9... | collective-permute-start | bytes 1179656 | tf_op jit(solution)/shard_map/ppermute | solution.py:22
  85.3 1.3 %collective-permute-start.12 = (bf16[256,384]{1,0:T(8,128)(2,1)}, bf16[256,384]{1,0:T(8,128)(2,1)}, u32[]{:S(2)}, u32[]{:S(2)}) collective-permute-start(bf16[256,384]{1,0:T(8,128)(2,1)} %get-tuple-element.21), channel_id=1, source_target_pairs={{0,2},{1,3},{2,0},{3,1},{4,6},{5,7},{6,4},{7,5},{8,10},{9,11},{10,... | collective-permute-start | bytes 589832 | tf_op jit(solution)/shard_map/ppermute | solution.py:22
  86.6 13.7 %collective-permute-done.12 = bf16[256,384]{1,0:T(8,128)(2,1)} collective-permute-done((bf16[256,384]{1,0:T(8,128)(2,1)}, bf16[256,384]{1,0:T(8,128)(2,1)}, u32[]{:S(2)}, u32[]{:S(2)}) %collective-permute-start.12) | collective-permute-done | bytes 196640 | tf_op jit(solution)/shard_map/ppermute | solution.py:22
  100.3 2.4 %fusion.7 = bf16[512,384]{1,0:T(8,128)(2,1)} fusion(bf16[512,384]{1,0:T(8,128)(2,1)S(1)} %get-tuple-element.10, bf16[512,384]{1,0:T(8,128)(2,1)} %collective-permute-done.10, bf16[512,384]{1,0:T(8,128)(2,1)} %collective-permute-done.9, bf16[256,384]{1,0:T(8,128)(2,1)} %collective-permute-done.12, bf16[256,384]{1,0:T(8,128)(2,1)} %collective-permute-done.11, ...), kind=kOutput, calls=%fused_computation.14 | convolution fusion | flops 152961024 | bytes 2260996 | tf_op jit(solution)/shard_map/dot_general | solution.py:66
  102.8 2.3 %collective-permute-done.16 = bf16[2,512,384]{2,1,0:T(8,128)(2,1)} collective-permute-done((bf16[2,512,384]{2,1,0:T(8,128)(2,1)}, bf16[2,512,384]{2,1,0:T(8,128)(2,1)}, u32[]{:S(2)}, u32[]{:S(2)}) %collective-permute-start.16) | collective-permute-done | bytes 786464 | tf_op jit(solution)/shard_map/ppermute | solution.py:17
  105.0 2.1 %fusion.2 = bf16[2,512,384]{2,1,0:T(8,128)(2,1)S(1)} fusion(f32[2,512,384]{2,1,0:T(8,128)S(1)} %copy-done.7, bf16[2,512,384]{2,1,0:T(8,128)(2,1)} %collective-permute-done.16, bf16[2,512,384]{2,1,0:T(8,128)(2,1)} %collective-permute-done.15, bf16[2,2,512,384]{3,2,1,0:T(8,128)(2,1)} %copy-done.10, bf16[2,2,512,384]{3,2,1,0:T(8,128)(2,1)S(1)} %copy-done.9), kind=kLoop, calls=%fused_computation.3 | loop fusion | flops 3538944 | bytes 5505024 | tf_op jit(solution)/shard_map/convert_element_type | solution.py:240
  107.1 1.0 slice_bitcast_fusion.2
  (47 shorter events, 2.0 us)
Async XLA Ops:
  0.6 16.4 %copy-start = (bf16[384,1536]{1,0:T(8,128)(2,1)S(1)}, bf16[384,1536]{1,0:T(8,128)(2,1)}, u32[]{:S(2)}) copy-start(bf16[384,1536]{1,0:T(8,128)(2,1)} %param.10) | copy-start | bytes 3538948
  0.6 11.5 %copy-start.6 = (bf16[512,384]{1,0:T(8,128)(2,1)S(1)}, bf16[512,384]{1,0:T(8,128)(2,1)}, u32[]{:S(2)}) copy-start(bf16[512,384]{1,0:T(8,128)(2,1)} %param.11) | copy-start | bytes 1179652
  0.7 16.1 %copy-start.12 = (s32[64,2]{0,1:T(2,128)S(1)}, s32[64,2]{0,1:T(2,128)}, u32[]{:S(2)}) copy-start(s32[64,2]{0,1:T(2,128)} %param.12) | copy-start | bytes 1540
  2.9 15.5 %copy-start.4 = (s32[512]{0:T(512)S(1)}, s32[512]{0:T(512)}, u32[]{:S(2)}) copy-start(s32[512]{0:T(512)} %param.13) | copy-start | bytes 6148
  2.9 24.8 %collective-permute-start.2 = (bf16[2,512,384]{2,1,0:T(8,128)(2,1)}, bf16[2,512,384]{2,1,0:T(8,128)(2,1)S(1)}, u32[]{:S(2)}, u32[]{:S(2)}) collective-permute-start(bf16[2,512,384]{2,1,0:T(8,128)(2,1)} %pad_maximum_fusion), channel_id=1, source_target_pairs={{8,0},{12,4},{16,8},{20,12},{24,16},{28,20},{32,24},{36,28},{40,32... | collective-permute-start | bytes 2359304 | tf_op jit(solution)/shard_map/ppermute | solution.py:17
  5.7 23.3 %collective-permute-start = (bf16[2,512,384]{2,1,0:T(8,128)(2,1)}, bf16[2,512,384]{2,1,0:T(8,128)(2,1)S(1)}, u32[]{:S(2)}, u32[]{:S(2)}) collective-permute-start(bf16[2,512,384]{2,1,0:T(8,128)(2,1)} %pad_maximum_fusion), channel_id=1, source_target_pairs={{0,8},{4,12},{8,16},{12,20},{16,24},{20,28},{24,32},{28,36},{32,40... | collective-permute-start | bytes 2359304 | tf_op jit(solution)/shard_map/ppermute | solution.py:17
  12.2 22.4 %collective-permute-start.5 = (bf16[512,384]{1,0:T(8,128)(2,1)S(1)}, bf16[512,384]{1,0:T(8,128)(2,1)}, u32[]{:S(2)}, u32[]{:S(2)}) collective-permute-start(bf16[512,384]{1,0:T(8,128)(2,1)S(1)} %copy-done.6), channel_id=1, source_target_pairs={{0,1},{1,2},{2,3},{3,0},{4,5},{5,6},{6,7},{7,4},{8,9},{9,10},{10,1... | collective-permute-start | bytes 1179656 | tf_op jit(solution)/shard_map/ppermute | solution.py:22
  13.3 9.6 %collective-permute-start.7 = (bf16[256,384]{1,0:T(8,128)(2,1)}, bf16[256,384]{1,0:T(8,128)(2,1)}, u32[]{:S(2)}, u32[]{:S(2)}) collective-permute-start(bf16[256,384]{1,0:T(8,128)(2,1)} %get-tuple-element.22), channel_id=1, source_target_pairs={{0,2},{1,3},{2,0},{3,1},{4,6},{5,7},{6,4},{7,5},{8,10},{9,11},{10,... | collective-permute-start | bytes 589832 | tf_op jit(solution)/shard_map/ppermute | solution.py:22
  15.9 14.6 %collective-permute-start.8 = (bf16[256,384]{1,0:T(8,128)(2,1)}, bf16[256,384]{1,0:T(8,128)(2,1)}, u32[]{:S(2)}, u32[]{:S(2)}) collective-permute-start(bf16[256,384]{1,0:T(8,128)(2,1)} %get-tuple-element.23), channel_id=1, source_target_pairs={{0,2},{1,3},{2,0},{3,1},{4,6},{5,7},{6,4},{7,5},{8,10},{9,11},{10,... | collective-permute-start | bytes 589832 | tf_op jit(solution)/shard_map/ppermute | solution.py:22
  18.5 16.1 %copy-start.5 = (f32[384,512]{0,1:T(8,128)S(1)}, f32[384,512]{0,1:T(8,128)}, u32[]{:S(2)}) copy-start(f32[384,512]{0,1:T(8,128)} %fusion.16) | copy-start | bytes 2359300
  22.9 22.2 %collective-permute-start.1 = (bf16[2,512,384]{2,1,0:T(8,128)(2,1)}, bf16[2,512,384]{2,1,0:T(8,128)(2,1)S(1)}, u32[]{:S(2)}, u32[]{:S(2)}) collective-permute-start(bf16[2,512,384]{2,1,0:T(8,128)(2,1)} %pad_maximum_fusion), channel_id=1, source_target_pairs={{0,4},{4,0},{8,12},{12,8},{16,20},{20,16},{24,28},{28,24},{32,36},... | collective-permute-start | bytes 2359304 | tf_op jit(solution)/shard_map/ppermute | solution.py:76
  27.7 17.3 %collective-permute-start.3 = (bf16[2,512,384]{2,1,0:T(8,128)(2,1)S(1)}, bf16[2,512,384]{2,1,0:T(8,128)(2,1)S(1)}, u32[]{:S(2)}, u32[]{:S(2)}) collective-permute-start(bf16[2,512,384]{2,1,0:T(8,128)(2,1)S(1)} %collective-permute-done.2.refs_8_.refs_9_), channel_id=1, source_target_pairs={{0,4},{8,12},{16,20},{24,28},{32,36},{40,44},{48,52},{56,60},{64,6... | collective-permute-start | bytes 2359304 | tf_op jit(solution)/shard_map/ppermute | solution.py:81
  29.1 16.0 %collective-permute-start.4 = (bf16[2,512,384]{2,1,0:T(8,128)(2,1)S(1)}, bf16[2,512,384]{2,1,0:T(8,128)(2,1)S(1)}, u32[]{:S(2)}, u32[]{:S(2)}) collective-permute-start(bf16[2,512,384]{2,1,0:T(8,128)(2,1)S(1)} %collective-permute-done.refs_0_.refs_1_), channel_id=1, source_target_pairs={{4,0},{12,8},{20,16},{28,24},{36,32},{44,40},{52,48},{60,56},{68,6... | collective-permute-start | bytes 2359304 | tf_op jit(solution)/shard_map/ppermute | solution.py:86
  30.4 14.2 %collective-permute-start.6 = (bf16[512,384]{1,0:T(8,128)(2,1)S(1)}, bf16[512,384]{1,0:T(8,128)(2,1)S(1)}, u32[]{:S(2)}, u32[]{:S(2)}) collective-permute-start(bf16[512,384]{1,0:T(8,128)(2,1)S(1)} %copy-done.6), channel_id=1, source_target_pairs={{0,3},{1,0},{2,1},{3,2},{4,7},{5,4},{6,5},{7,6},{8,11},{9,8},{10,9... | collective-permute-start | bytes 1179656 | tf_op jit(solution)/shard_map/ppermute | solution.py:22
  36.1 9.0 %copy-start.1 = (bf16[512,384]{1,0:T(8,128)(2,1)S(1)}, bf16[512,384]{1,0:T(8,128)(2,1)}, u32[]{:S(2)}) copy-start(bf16[512,384]{1,0:T(8,128)(2,1)} %k0_ref.1) | copy-start | bytes 1179652
  36.1 9.0 %copy-start.2 = (bf16[512,384]{1,0:T(8,128)(2,1)S(1)}, bf16[512,384]{1,0:T(8,128)(2,1)}, u32[]{:S(2)}) copy-start(bf16[512,384]{1,0:T(8,128)(2,1)} %v0_ref.1) | copy-start | bytes 1179652
  36.1 9.0 %copy-start.3 = (bf16[512,384]{1,0:T(8,128)(2,1)S(1)}, bf16[512,384]{1,0:T(8,128)(2,1)}, u32[]{:S(2)}) copy-start(bf16[512,384]{1,0:T(8,128)(2,1)} %q_ref.1) | copy-start | bytes 1179652
  64.3 7.9 %copy-start.11 = (bf16[2,2,512,384]{3,2,1,0:T(8,128)(2,1)S(1)}, bf16[2,2,512,384]{3,2,1,0:T(8,128)(2,1)}, u32[]{:S(2)}) copy-start(bf16[2,2,512,384]{3,2,1,0:T(8,128)(2,1)} %get-tuple-element.15) | copy-start | bytes 4718596
  64.3 6.5 %collective-permute-start.13 = (bf16[2,2,512,384]{3,2,1,0:T(8,128)(2,1)}, bf16[2,2,512,384]{3,2,1,0:T(8,128)(2,1)S(1)}, u32[]{:S(2)}, u32[]{:S(2)}) collective-permute-start(bf16[2,2,512,384]{3,2,1,0:T(8,128)(2,1)} %get-tuple-element.13), channel_id=1, source_target_pairs={{0,4},{8,12},{16,20},{24,28},{32,36},{40,44},{48,52},{56,60},{64,6... | collective-permute-start | bytes 4718600 | tf_op jit(solution)/shard_map/ppermute | solution.py:81
  66.7 5.5 %collective-permute-start.14 = (bf16[2,2,512,384]{3,2,1,0:T(8,128)(2,1)}, bf16[2,2,512,384]{3,2,1,0:T(8,128)(2,1)S(1)}, u32[]{:S(2)}, u32[]{:S(2)}) collective-permute-start(bf16[2,2,512,384]{3,2,1,0:T(8,128)(2,1)} %get-tuple-element.14), channel_id=1, source_target_pairs={{4,0},{12,8},{20,16},{28,24},{36,32},{44,40},{52,48},{60,56},{68,6... | collective-permute-start | bytes 4718600 | tf_op jit(solution)/shard_map/ppermute | solution.py:86
  69.1 16.2 %collective-permute-start.11 = (bf16[256,384]{1,0:T(8,128)(2,1)S(1)}, bf16[256,384]{1,0:T(8,128)(2,1)}, u32[]{:S(2)}, u32[]{:S(2)}) collective-permute-start(bf16[256,384]{1,0:T(8,128)(2,1)S(1)} %get-tuple-element.20), channel_id=1, source_target_pairs={{0,2},{1,3},{2,0},{3,1},{4,6},{5,7},{6,4},{7,5},{8,10},{9,11},{10,... | collective-permute-start | bytes 589832 | tf_op jit(solution)/shard_map/ppermute | solution.py:22
  70.9 3.0 %copy-start.8 = (bf16[2,2,512,384]{3,2,1,0:T(8,128)(2,1)}, bf16[2,2,512,384]{3,2,1,0:T(8,128)(2,1)S(1)}, u32[]{:S(2)}) copy-start(bf16[2,2,512,384]{3,2,1,0:T(8,128)(2,1)S(1)} %collective-permute-done.13) | copy-start | bytes 4718596
  72.2 1.7 %copy-start.10 = (bf16[2,2,512,384]{3,2,1,0:T(8,128)(2,1)}, bf16[2,2,512,384]{3,2,1,0:T(8,128)(2,1)S(1)}, u32[]{:S(2)}) copy-start(bf16[2,2,512,384]{3,2,1,0:T(8,128)(2,1)S(1)} %collective-permute-done.14) | copy-start | bytes 4718596
  73.9 28.9 %collective-permute-start.15 = (bf16[2,512,384]{2,1,0:T(8,128)(2,1)}, bf16[2,512,384]{2,1,0:T(8,128)(2,1)}, u32[]{:S(2)}, u32[]{:S(2)}) collective-permute-start(bf16[2,512,384]{2,1,0:T(8,128)(2,1)} %get-tuple-element.16), channel_id=1, source_target_pairs={{0,8},{4,12},{8,16},{12,20},{16,24},{20,28},{24,32},{28,36},{32,40... | collective-permute-start | bytes 2359304 | tf_op jit(solution)/shard_map/ppermute | solution.py:17
  80.1 25.0 %copy-start.7 = (f32[2,512,384]{2,1,0:T(8,128)S(1)}, f32[2,512,384]{2,1,0:T(8,128)}, u32[]{:S(2)}) copy-start(f32[2,512,384]{2,1,0:T(8,128)} %get-tuple-element.12) | copy-start | bytes 4718596
  80.1 25.0 %collective-permute-start.16 = (bf16[2,512,384]{2,1,0:T(8,128)(2,1)}, bf16[2,512,384]{2,1,0:T(8,128)(2,1)}, u32[]{:S(2)}, u32[]{:S(2)}) collective-permute-start(bf16[2,512,384]{2,1,0:T(8,128)(2,1)} %get-tuple-element.17), channel_id=1, source_target_pairs={{8,0},{12,4},{16,8},{20,12},{24,16},{28,20},{32,24},{36,28},{40,32... | collective-permute-start | bytes 2359304 | tf_op jit(solution)/shard_map/ppermute | solution.py:17
  83.3 17.0 %collective-permute-start.9 = (bf16[512,384]{1,0:T(8,128)(2,1)}, bf16[512,384]{1,0:T(8,128)(2,1)}, u32[]{:S(2)}, u32[]{:S(2)}) collective-permute-start(bf16[512,384]{1,0:T(8,128)(2,1)} %convolution_convert_fusion.2), channel_id=1, source_target_pairs={{0,1},{1,2},{2,3},{3,0},{4,5},{5,6},{6,7},{7,4},{8,9},{9,10},{10,1... | collective-permute-start | bytes 1179656 | tf_op jit(solution)/shard_map/ppermute | solution.py:22
  83.3 17.0 %collective-permute-start.10 = (bf16[512,384]{1,0:T(8,128)(2,1)S(1)}, bf16[512,384]{1,0:T(8,128)(2,1)}, u32[]{:S(2)}, u32[]{:S(2)}) collective-permute-start(bf16[512,384]{1,0:T(8,128)(2,1)S(1)} %convolution_convert_fusion.1), channel_id=1, source_target_pairs={{0,3},{1,0},{2,1},{3,2},{4,7},{5,4},{6,5},{7,6},{8,11},{9,8},{10,9... | collective-permute-start | bytes 1179656 | tf_op jit(solution)/shard_map/ppermute | solution.py:22
  85.3 15.0 %collective-permute-start.12 = (bf16[256,384]{1,0:T(8,128)(2,1)}, bf16[256,384]{1,0:T(8,128)(2,1)}, u32[]{:S(2)}, u32[]{:S(2)}) collective-permute-start(bf16[256,384]{1,0:T(8,128)(2,1)} %get-tuple-element.21), channel_id=1, source_target_pairs={{0,2},{1,3},{2,0},{3,1},{4,6},{5,7},{6,4},{7,5},{8,10},{9,11},{10,... | collective-permute-start | bytes 589832 | tf_op jit(solution)/shard_map/ppermute | solution.py:22
  86.6 18.4 %copy-start.9 = (bf16[2,2,512,384]{3,2,1,0:T(8,128)(2,1)S(1)}, bf16[2,2,512,384]{3,2,1,0:T(8,128)(2,1)}, u32[]{:S(2)}) copy-start(bf16[2,2,512,384]{3,2,1,0:T(8,128)(2,1)} %copy-done.8) | copy-start | bytes 4718596
where the time goes:
time: 109 us; the launch traced here: 108 us
  waiting for transfers between devices  35.1 us (32%)
  starting transfers between devices  35 us (32%)
  Pallas kernels  19.2 us (18%)
  matrix products  8.98 us (8%)
  other arithmetic  6.19 us (6%)
  local copies, waits for them, and re-layouts  2.66 us (2%)
    ppermute x8, waiting for transfers between devices, ring_shift(): lax.ppermute(block, axis, [(i, (i + distance) % size) for i in range(size)])  26.5 us
    pallas_call x1, Pallas kernels, attention(): pl.pallas_call(attn_kernel, grid_spec=grid_spec, out_shape=out_shape, com...  19.2 us
    ppermute x4, starting transfers between devices, shifted(): return lax.ppermute(block, axis, route)  17.5 us
    ppermute x8, starting transfers between devices, ring_shift(): lax.ppermute(block, axis, [(i, (i + distance) % size) for i in range(size)])  11.2 us
    ppermute x4, waiting for transfers between devices, shifted(): return lax.ppermute(block, axis, route)  7.12 us
    dot_general x4, matrix products, fold_cotangent(): lax.dot_general(piece, w_cols, nt, preferred_element_type=jnp.float32)  4.6 us
    ppermute x2, starting transfers between devices, even_to_odd(): lax.ppermute(block, axis, [(i, i + 1) for i in range(0, size - 1, 2)])  3.7 us
    ppermute x2, starting transfers between devices, odd_to_even(): return lax.ppermute(block, axis, [(i, i - 1) for i in range(1, size, 2)])  2.58 us
  transfers between devices with their start and end apart: 17, of which 6 were waited for; matrix products, arithmetic and copies ran while one was open for 12% of the time, Pallas kernels for 0%

commit v1 on v0

--- a/solution.py
+++ b/solution.py
@@ -90,16 +90,8 @@
     n_cand = 5
     cand_k = refs[0:2 * n_cand:2]
     cand_v = refs[1:2 * n_cand:2]
-    g_ref, srow_ref, scol_ref, attn_ref, dq_ref, self_ref, pa_ref, pb_ref, far_ref = refs[2 * n_cand:]
+    g_ref, srow_ref, scol_ref, attn_ref, dq_ref, self_ref, terms_ref = refs[2 * n_cand:]
     scale = HEAD_DIM ** (-0.5)
-    d = HEAD_DIM
-    h = pl.program_id(0)
-
-    @pl.when(h == 0)
-    def _():
-        pa_ref[...] = jnp.zeros_like(pa_ref)
-        pb_ref[...] = jnp.zeros_like(pb_ref)
-        far_ref[...] = jnp.zeros_like(far_ref)
 
     def pick(cands, slot):
         idx = sel_ref[slot]
@@ -136,7 +128,7 @@
     gf = g.astype(jnp.float32)
     delta = jnp.sum(attn.astype(jnp.float32) * gf, axis=1, keepdims=True)
     dq = None
-    cols = pl.ds(pl.multiple_of(h * d, d), d)
+    routed = []
     for j in range(3):
         dp = lax.dot_general(g, vs[j], nt, preferred_element_type=jnp.float32)
         ds = (probs[j] * (dp - delta) * scale).astype(jnp.bfloat16)
@@ -147,17 +139,13 @@
         if j == 0:
             self_ref[0] = dk
             self_ref[1] = dv
-            continue
-        dk = dk.astype(jnp.bfloat16)
-        dv = dv.astype(jnp.bfloat16)
-        off = sel_ref[2 + j]
-        for value, dests in ((-2, ((far_ref, 0),)), (2, ((far_ref, 1),)),
-                             (1, ((pa_ref, 0), (pb_ref, 1))), (-1, ((pa_ref, 1), (pb_ref, 0)))):
-            @pl.when(off == value)
-            def _():
-                for ref, slot in dests:
-                    ref[slot, 0, :, cols] = dk
-                    ref[slot, 1, :, cols] = dv
+        else:
+            routed.append((sel_ref[2 + j], dk.astype(jnp.bfloat16), dv.astype(jnp.bfloat16)))
+    (off1, dk1, dv1), (off2, dk2, dv2) = routed
+    zero = jnp.zeros_like(dk1)
+    for slot, value in enumerate((-2, -1, 1, 2)):
+        terms_ref[slot, 0] = jnp.where(off1 == value, dk1, jnp.where(off2 == value, dk2, zero))
+        terms_ref[slot, 1] = jnp.where(off1 == value, dv1, jnp.where(off2 == value, dv2, zero))
     dq_ref[...] = dq.astype(jnp.bfloat16)
 
 
@@ -169,7 +157,7 @@
     spec_ck = pl.BlockSpec((None, rows, d), lambda h, s: (0, 0, h))
     spec_cv = pl.BlockSpec((None, rows, d), lambda h, s: (1, 0, h))
     spec_self = pl.BlockSpec((2, rows, d), lambda h, s: (0, 0, h))
-    spec_pair = pl.BlockSpec((2, 2, rows, columns), lambda h, s: (0, 0, 0, 0))
+    spec_terms = pl.BlockSpec((4, 2, rows, d), lambda h, s: (0, 0, 0, h))
     cand_specs = []
     cand_args = []
     for c in cands:
@@ -181,16 +169,13 @@
         in_specs=[spec_q, spec_q, spec_q] + cand_specs + [spec_q,
                   pl.BlockSpec((rows, 1), lambda h, s: (0, 0)),
                   pl.BlockSpec((1, rows), lambda h, s: (0, 0))],
-        out_specs=[spec_q, spec_q, spec_self, spec_pair, spec_pair, spec_pair],
-    )
-    pair_shape = jax.ShapeDtypeStruct((2, 2, rows, columns), jnp.bfloat16)
+        out_specs=[spec_q, spec_q, spec_self, spec_terms],
+    )
     out_shape = [
         jax.ShapeDtypeStruct((rows, columns), jnp.bfloat16),
         jax.ShapeDtypeStruct((rows, columns), jnp.bfloat16),
         jax.ShapeDtypeStruct((2, rows, columns), jnp.float32),
-        pair_shape,
-        pair_shape,
-        pair_shape,
+        jax.ShapeDtypeStruct((4, 2, rows, columns), jnp.bfloat16),
     ]
     kwargs = {}
     if INTERPRET is not None:
@@ -220,19 +205,18 @@
     pick = jnp.where(offs == -2, 0, jnp.where(offs == 2, 4, jnp.where(offs == partner_off, 1, relay_idx)))
     sel = jnp.concatenate([pick.astype(jnp.int32), jnp.zeros((1,), jnp.int32), offs])
     cands = (from_left2, partner_own, relay_to_odd, relay_to_even, from_right2)
-    attn, grad_q, self_term, pair_a, pair_b, far = attention(
-        sel, queries, keys, values, cands, grad_attn, shot_ids
-    )
+    attn, grad_q, self_term, terms = attention(sel, queries, keys, values, cands, grad_attn, shot_ids)
     attn_out = project_out(attn, out_weight)
-    got_a = even_to_odd(pair_a, "seq")
-    got_b = odd_to_even(pair_b, "seq")
-    up_plus = (far[1].astype(jnp.float32) + got_b[1].astype(jnp.float32)).astype(jnp.bfloat16)
-    up_minus = (far[0].astype(jnp.float32) + got_a[1].astype(jnp.float32)).astype(jnp.bfloat16)
+    near = terms[1:3]
+    got_a = even_to_odd(near, "seq")
+    got_b = odd_to_even(near, "seq")
+    up_plus = (terms[3].astype(jnp.float32) + got_b[1].astype(jnp.float32)).astype(jnp.bfloat16)
+    up_minus = (terms[0].astype(jnp.float32) + got_a[0].astype(jnp.float32)).astype(jnp.bfloat16)
     got_from_left = shifted(up_plus, "seq", 2)
     got_from_right = shifted(up_minus, "seq", -2)
     total = (
         self_term
-        + got_a[0].astype(jnp.float32)
+        + got_a[1].astype(jnp.float32)
         + got_b[0].astype(jnp.float32)
         + got_from_left.astype(jnp.float32)
         + got_from_right.astype(jnp.float32)

time: 109 us -> 108 us (level)
  Pallas kernels: 19.2 us -> 16.1 us
  waiting for transfers between devices: 35.1 us -> 32.7 us
  starting transfers between devices: 35 us -> 37 us
  local copies, waits for them, and re-layouts: 2.66 us -> 4.5 us
    pallas_call x1, Pallas kernels: 19.2 us -> 16.1 us  [attention(): pl.pallas_call(attn_kernel, grid_spec=grid_spec, out_shape=out_shape, com...]
    slice x0 -> x1, local copies, waits for them, and re-layouts: none -> 1.72 us  [on_device(): near = terms[1:3]]
    ppermute x8, waiting for transfers between devices: 26.5 us -> 24.9 us  [ring_shift(): lax.ppermute(block, axis, [(i, (i + distance) % size) for i in range(size)])]
    ppermute x2, waiting for transfers between devices: 1.38 us -> 0.01 us  [odd_to_even(): return lax.ppermute(block, axis, [(i, i - 1) for i in range(1, size, 2)])]
    ppermute x8, starting transfers between devices: 11.2 us -> 12.5 us  [ring_shift(): lax.ppermute(block, axis, [(i, (i + distance) % size) for i in range(size)])]
  transfers between devices with their start and end apart: 17 -> 17, of which waited for: 6 -> 7; matrix products, arithmetic and copies ran while one was open for 12% -> 12% of each run, Pallas kernels for 0% -> 0%
where the time goes in v1:
time: 108 us; the launch traced here: 107 us
  starting transfers between devices  37 us (34%)
  waiting for transfers between devices  32.7 us (30%)
  Pallas kernels  16.1 us (15%)
  matrix products  8.98 us (8%)
  other arithmetic  6.5 us (6%)
  local copies, waits for them, and re-layouts  4.5 us (4%)
    ppermute x8, waiting for transfers between devices, ring_shift(): lax.ppermute(block, axis, [(i, (i + distance) % size) for i in range(size)])  24.9 us
    ppermute x4, starting transfers between devices, shifted(): return lax.ppermute(block, axis, route)  17.3 us
    pallas_call x1, Pallas kernels, attention(): pl.pallas_call(attn_kernel, grid_spec=grid_spec, out_shape=out_shape, com...  16.1 us
    ppermute x8, starting transfers between devices, ring_shift(): lax.ppermute(block, axis, [(i, (i + distance) % size) for i in range(size)])  12.5 us
    ppermute x4, waiting for transfers between devices, shifted(): return lax.ppermute(block, axis, route)  7.76 us
    dot_general x4, matrix products, fold_cotangent(): lax.dot_general(piece, w_cols, nt, preferred_element_type=jnp.float32)  4.6 us
    ppermute x2, starting transfers between devices, even_to_odd(): lax.ppermute(block, axis, [(i, i + 1) for i in range(0, size - 1, 2)])  4.55 us
    ppermute x2, starting transfers between devices, odd_to_even(): return lax.ppermute(block, axis, [(i, i - 1) for i in range(1, size, 2)])  2.58 us
  transfers between devices with their start and end apart: 17, of which 7 were waited for; matrix products, arithmetic and copies ran while one was open for 12% of the time, Pallas kernels for 0%

profile of v1, /device:TPU:126, one launch (start us, length us, event | category | flops | bytes accessed | tf_op | source)
XLA Modules:
  0.0 106.7 jit_solution(11089689674894883586)
XLA Ops:
  0.7 2.2 %pad_maximum_fusion = bf16[2,512,384]{2,1,0:T(8,128)(2,1)} fusion(bf16[1,512,384]{2,1,0:T(8,128)(2,1)} %bitcast.36, bf16[1,512,384]{2,1,0:T(8,128)(2,1)} %bitcast.35), kind=kLoop, calls=%fused_computation.23 | loop fusion | flops 393216 | bytes 1572864 | tf_op jit(solution)/shard_map/stack | solution.py:196
  2.9 2.9 %collective-permute-start.2 = (bf16[2,512,384]{2,1,0:T(8,128)(2,1)}, bf16[2,512,384]{2,1,0:T(8,128)(2,1)S(1)}, u32[]{:S(2)}, u32[]{:S(2)}) collective-permute-start(bf16[2,512,384]{2,1,0:T(8,128)(2,1)} %pad_maximum_fusion), channel_id=1, source_target_pairs={{8,0},{12,4},{16,8},{20,12},{24,16},{28,20},{32,24},{36,28},{40,32... | collective-permute-start | bytes 2359304 | tf_op jit(solution)/shard_map/ppermute | solution.py:17
  5.7 6.4 %collective-permute-start = (bf16[2,512,384]{2,1,0:T(8,128)(2,1)}, bf16[2,512,384]{2,1,0:T(8,128)(2,1)S(1)}, u32[]{:S(2)}, u32[]{:S(2)}) collective-permute-start(bf16[2,512,384]{2,1,0:T(8,128)(2,1)} %pad_maximum_fusion), channel_id=1, source_target_pairs={{0,8},{4,12},{8,16},{12,20},{16,24},{20,28},{24,32},{28,36},{32,40... | collective-permute-start | bytes 2359304 | tf_op jit(solution)/shard_map/ppermute | solution.py:17
  12.5 0.8 fusion.36
  13.3 2.6 %collective-permute-start.7 = (bf16[256,384]{1,0:T(8,128)(2,1)}, bf16[256,384]{1,0:T(8,128)(2,1)}, u32[]{:S(2)}, u32[]{:S(2)}) collective-permute-start(bf16[256,384]{1,0:T(8,128)(2,1)} %get-tuple-element.18), channel_id=1, source_target_pairs={{0,2},{1,3},{2,0},{3,1},{4,6},{5,7},{6,4},{7,5},{8,10},{9,11},{10,... | collective-permute-start | bytes 589832 | tf_op jit(solution)/shard_map/ppermute | solution.py:22
  15.9 0.9 collective-permute-start.8
  17.0 1.4 %fusion.16 = f32[384,512]{0,1:T(8,128)} fusion(bf16[512,384]{1,0:T(8,128)(2,1)S(1)} %copy-done.7, bf16[384,1536]{1,0:T(8,128)(2,1)S(1)} %copy-done, s32[]{:T(128)S(6)} %select_n.72), kind=kOutput, calls=%fused_computation.31 | convolution fusion | flops 150994944 | bytes 1474564 | tf_op jit(solution)/shard_map/dot_general | solution.py:43
  18.5 4.3 %collective-permute-done.7 = bf16[256,384]{1,0:T(8,128)(2,1)} collective-permute-done((bf16[256,384]{1,0:T(8,128)(2,1)}, bf16[256,384]{1,0:T(8,128)(2,1)}, u32[]{:S(2)}, u32[]{:S(2)}) %collective-permute-start.7) | collective-permute-done | bytes 196640 | tf_op jit(solution)/shard_map/ppermute | solution.py:22
  22.9 4.8 %collective-permute-done.2.refs_8_.refs_9_ = bf16[2,512,384]{2,1,0:T(8,128)(2,1)S(1)} collective-permute-done((bf16[2,512,384]{2,1,0:T(8,128)(2,1)}, bf16[2,512,384]{2,1,0:T(8,128)(2,1)S(1)}, u32[]{:S(2)}, u32[]{:S(2)}) %collective-permute-start.2) | collective-permute-done | bytes 786464 | tf_op jit(solution)/shard_map/ppermute | solution.py:17
  27.7 1.3 %collective-permute-start.3 = (bf16[2,512,384]{2,1,0:T(8,128)(2,1)S(1)}, bf16[2,512,384]{2,1,0:T(8,128)(2,1)S(1)}, u32[]{:S(2)}, u32[]{:S(2)}) collective-permute-start(bf16[2,512,384]{2,1,0:T(8,128)(2,1)S(1)} %collective-permute-done.2.refs_8_.refs_9_), channel_id=1, source_target_pairs={{0,4},{8,12},{16,20},{24,28},{32,36},{40,44},{48,52},{56,60},{64,6... | collective-permute-start | bytes 2359304 | tf_op jit(solution)/shard_map/ppermute | solution.py:81
  29.1 1.3 %collective-permute-start.4 = (bf16[2,512,384]{2,1,0:T(8,128)(2,1)S(1)}, bf16[2,512,384]{2,1,0:T(8,128)(2,1)S(1)}, u32[]{:S(2)}, u32[]{:S(2)}) collective-permute-start(bf16[2,512,384]{2,1,0:T(8,128)(2,1)S(1)} %collective-permute-done.refs_0_.refs_1_), channel_id=1, source_target_pairs={{4,0},{12,8},{20,16},{28,24},{36,32},{44,40},{52,48},{60,56},{68,6... | collective-permute-start | bytes 2359304 | tf_op jit(solution)/shard_map/ppermute | solution.py:86
  30.4 2.8 %collective-permute-start.6 = (bf16[512,384]{1,0:T(8,128)(2,1)S(1)}, bf16[512,384]{1,0:T(8,128)(2,1)S(1)}, u32[]{:S(2)}, u32[]{:S(2)}) collective-permute-start(bf16[512,384]{1,0:T(8,128)(2,1)S(1)} %copy-done.7), channel_id=1, source_target_pairs={{0,3},{1,0},{2,1},{3,2},{4,7},{5,4},{6,5},{7,6},{8,11},{9,8},{10,9... | collective-permute-start | bytes 1179656 | tf_op jit(solution)/shard_map/ppermute | solution.py:22
  33.2 1.4 %fusion.11 = f32[512,384]{1,0:T(8,128)S(1)} fusion(bf16[256,384]{1,0:T(8,128)(2,1)} %collective-permute-done.8, bf16[256,384]{1,0:T(8,128)(2,1)} %collective-permute-done.7, bf16[384,1536]{1,0:T(8,128)(2,1)S(1)} %copy-done, s32[]{:T(128)S(6)} %select_n.78), kind=kOutput, calls=%fused_computation.26 | convolution fusion | flops 151781376 | bytes 1474564 | tf_op jit(solution)/shard_map/dot_general | solution.py:43
  34.6 1.4 %convolution_add_fusion.2 = f32[384,512]{0,1:T(8,128)S(1)} fusion(f32[384,512]{0,1:T(8,128)S(1)} %copy-done.5, bf16[512,384]{1,0:T(8,128)(2,1)} %collective-permute-done.5, bf16[384,1536]{1,0:T(8,128)(2,1)S(1)} %copy-done, s32[]{:T(128)S(6)} %select_n.74), kind=kOutput, calls=%fused_computation.10 | convolution fusion | flops 151191552 | bytes 2260996 | tf_op jit(solution)/shard_map/dot_general | solution.py:43
  36.1 8.5 %collective-permute-done.6 = bf16[512,384]{1,0:T(8,128)(2,1)S(1)} collective-permute-done((bf16[512,384]{1,0:T(8,128)(2,1)S(1)}, bf16[512,384]{1,0:T(8,128)(2,1)S(1)}, u32[]{:S(2)}, u32[]{:S(2)}) %collective-permute-start.6) | collective-permute-done | bytes 393248 | tf_op jit(solution)/shard_map/ppermute | solution.py:22
  45.1 16.1 %shard_map.102 = (bf16[512,384]{1,0:T(8,128)(2,1)S(1)}, bf16[512,384]{1,0:T(8,128)(2,1)}, f32[2,512,384]{2,1,0:T(8,128)}, bf16[4,2,512,384]{3,2,1,0:T(8,128)(2,1)}) custom-call(s32[5]{0:T(128)S(1)} %pad_add_fusion.sel_ref, bf16[512,384]{1,0:T(8,128)(2,1)S(1)} %copy-done.3, bf16[512,384]{1,0:T(8,128)(2,1)S(1)} %copy-done.1, bf16[512,384]{1,0:T(8,128)(2,1)S(1)} %copy-done.2, ...), custom_call_target="tpu_custom_call" | custom-call | tf_op jit(solution)/shard_map/pallas_call | solution.py:183
  61.2 1.7 %slice.43 = bf16[2,2,512,384]{3,2,1,0:T(8,128)(2,1)S(1)} slice(bf16[4,2,512,384]{3,2,1,0:T(8,128)(2,1)} %get-tuple-element.11), slice={[1:3], [0:2], [0:512], [0:384]} | slice | bytes 3145728 | tf_op jit(solution)/shard_map/slice | solution.py:210
  63.0 1.3 %collective-permute-start.14 = (bf16[2,2,512,384]{3,2,1,0:T(8,128)(2,1)S(1)}, bf16[2,2,512,384]{3,2,1,0:T(8,128)(2,1)S(1)}, u32[]{:S(2)}, u32[]{:S(2)}) collective-permute-start(bf16[2,2,512,384]{3,2,1,0:T(8,128)(2,1)S(1)} %slice.43), channel_id=1, source_target_pairs={{4,0},{12,8},{20,16},{28,24},{36,32},{44,40},{52,48},{60,56},{68,6... | collective-permute-start | bytes 4718600 | tf_op jit(solution)/shard_map/ppermute | solution.py:86
  64.3 3.2 %collective-permute-start.13 = (bf16[2,2,512,384]{3,2,1,0:T(8,128)(2,1)S(1)}, bf16[2,2,512,384]{3,2,1,0:T(8,128)(2,1)S(1)}, u32[]{:S(2)}, u32[]{:S(2)}) collective-permute-start(bf16[2,2,512,384]{3,2,1,0:T(8,128)(2,1)S(1)} %slice.43), channel_id=1, source_target_pairs={{0,4},{8,12},{16,20},{24,28},{32,36},{40,44},{48,52},{56,60},{64,6... | collective-permute-start | bytes 4718600 | tf_op jit(solution)/shard_map/ppermute | solution.py:81
  68.6 1.3 %collective-permute-start.11 = (bf16[256,384]{1,0:T(8,128)(2,1)S(1)}, bf16[256,384]{1,0:T(8,128)(2,1)}, u32[]{:S(2)}, u32[]{:S(2)}) collective-permute-start(bf16[256,384]{1,0:T(8,128)(2,1)S(1)} %get-tuple-element.16), channel_id=1, source_target_pairs={{0,2},{1,3},{2,0},{3,1},{4,6},{5,7},{6,4},{7,5},{8,10},{9,11},{10,... | collective-permute-start | bytes 589832 | tf_op jit(solution)/shard_map/ppermute | solution.py:22
  70.4 1.9 %fusion.9 = (bf16[2,512,384]{2,1,0:T(8,128)(2,1)}, bf16[2,512,384]{2,1,0:T(8,128)(2,1)}) fusion(bf16[2,2,512,384]{3,2,1,0:T(8,128)(2,1)S(1)} %collective-permute-done.14, bf16[4,2,512,384]{3,2,1,0:T(8,128)(2,1)S(1)} %copy-done.6, bf16[2,2,512,384]{3,2,1,0:T(8,128)(2,1)S(1)} %collective-permute-done.13), kind=kLoop, calls=%fused_computation.19 | loop fusion | flops 3145728 | bytes 4718592 | tf_op jit(solution)/shard_map/convert_element_type | solution.py:213
  72.5 6.0 %collective-permute-start.15 = (bf16[2,512,384]{2,1,0:T(8,128)(2,1)}, bf16[2,512,384]{2,1,0:T(8,128)(2,1)}, u32[]{:S(2)}, u32[]{:S(2)}) collective-permute-start(bf16[2,512,384]{2,1,0:T(8,128)(2,1)} %get-tuple-element.12), channel_id=1, source_target_pairs={{0,8},{4,12},{8,16},{12,20},{16,24},{20,28},{24,32},{28,36},{32,40... | collective-permute-start | bytes 2359304 | tf_op jit(solution)/shard_map/ppermute | solution.py:17
  78.5 2.1 %collective-permute-start.16 = (bf16[2,512,384]{2,1,0:T(8,128)(2,1)}, bf16[2,512,384]{2,1,0:T(8,128)(2,1)}, u32[]{:S(2)}, u32[]{:S(2)}) collective-permute-start(bf16[2,512,384]{2,1,0:T(8,128)(2,1)} %get-tuple-element.13), channel_id=1, source_target_pairs={{8,0},{12,4},{16,8},{20,12},{24,16},{28,20},{32,24},{36,28},{40,32... | collective-permute-start | bytes 2359304 | tf_op jit(solution)/shard_map/ppermute | solution.py:17
  80.6 1.1 %convolution_convert_fusion.2 = bf16[512,384]{1,0:T(8,128)(2,1)} fusion(bf16[512,384]{1,0:T(8,128)(2,1)S(1)} %get-tuple-element.8, bf16[384,1536]{1,0:T(8,128)(2,1)S(1)} %copy-done, s32[]{:T(128)S(6)} %select_n.76), kind=kOutput, calls=%fused_computation.18 | convolution fusion | flops 151191552 | bytes 1081348 | tf_op jit(solution)/shard_map/dot_general | solution.py:56
  81.7 1.3 %collective-permute-start.9 = (bf16[512,384]{1,0:T(8,128)(2,1)}, bf16[512,384]{1,0:T(8,128)(2,1)}, u32[]{:S(2)}, u32[]{:S(2)}) collective-permute-start(bf16[512,384]{1,0:T(8,128)(2,1)} %convolution_convert_fusion.2), channel_id=1, source_target_pairs={{0,1},{1,2},{2,3},{3,0},{4,5},{5,6},{6,7},{7,4},{8,9},{9,10},{10,1... | collective-permute-start | bytes 1179656 | tf_op jit(solution)/shard_map/ppermute | solution.py:22
  83.0 0.7 collective-permute-start.10
  83.7 2.6 %collective-permute-start.12 = (bf16[256,384]{1,0:T(8,128)(2,1)}, bf16[256,384]{1,0:T(8,128)(2,1)}, u32[]{:S(2)}, u32[]{:S(2)}) collective-permute-start(bf16[256,384]{1,0:T(8,128)(2,1)} %get-tuple-element.17), channel_id=1, source_target_pairs={{0,2},{1,3},{2,0},{3,1},{4,6},{5,7},{6,4},{7,5},{8,10},{9,11},{10,... | collective-permute-start | bytes 589832 | tf_op jit(solution)/shard_map/ppermute | solution.py:22
  86.4 11.9 %collective-permute-done.12 = bf16[256,384]{1,0:T(8,128)(2,1)} collective-permute-done((bf16[256,384]{1,0:T(8,128)(2,1)}, bf16[256,384]{1,0:T(8,128)(2,1)}, u32[]{:S(2)}, u32[]{:S(2)}) %collective-permute-start.12) | collective-permute-done | bytes 196640 | tf_op jit(solution)/shard_map/ppermute | solution.py:22
  98.4 2.4 %fusion.7 = bf16[512,384]{1,0:T(8,128)(2,1)} fusion(bf16[512,384]{1,0:T(8,128)(2,1)S(1)} %get-tuple-element.8, bf16[512,384]{1,0:T(8,128)(2,1)} %collective-permute-done.10, bf16[512,384]{1,0:T(8,128)(2,1)} %collective-permute-done.9, bf16[256,384]{1,0:T(8,128)(2,1)} %collective-permute-done.12, bf16[256,384]{1,0:T(8,128)(2,1)} %collective-permute-done.11, ...), kind=kOutput, calls=%fused_computation.14 | convolution fusion | flops 152961024 | bytes 2260996 | tf_op jit(solution)/shard_map/dot_general | solution.py:66
  100.8 2.9 %collective-permute-done.16 = bf16[2,512,384]{2,1,0:T(8,128)(2,1)} collective-permute-done((bf16[2,512,384]{2,1,0:T(8,128)(2,1)}, bf16[2,512,384]{2,1,0:T(8,128)(2,1)}, u32[]{:S(2)}, u32[]{:S(2)}) %collective-permute-start.16) | collective-permute-done | bytes 786464 | tf_op jit(solution)/shard_map/ppermute | solution.py:17
  103.7 2.1 %fusion.2 = bf16[2,512,384]{2,1,0:T(8,128)(2,1)S(1)} fusion(f32[2,512,384]{2,1,0:T(8,128)S(1)} %copy-done.8, bf16[2,512,384]{2,1,0:T(8,128)(2,1)} %collective-permute-done.16, bf16[2,512,384]{2,1,0:T(8,128)(2,1)} %collective-permute-done.15, bf16[2,2,512,384]{3,2,1,0:T(8,128)(2,1)S(1)} %copy-done.10, bf16[2,2,512,384]{3,2,1,0:T(8,128)(2,1)} %copy-done.11), kind=kLoop, calls=%fused_computation.3 | loop fusion | flops 3538944 | bytes 5505024 | tf_op jit(solution)/shard_map/convert_element_type | solution.py:224
  105.8 1.0 slice_bitcast_fusion.2
  (48 shorter events, 3.1 us)
Async XLA Ops:
  0.6 16.4 %copy-start = (bf16[384,1536]{1,0:T(8,128)(2,1)S(1)}, bf16[384,1536]{1,0:T(8,128)(2,1)}, u32[]{:S(2)}) copy-start(bf16[384,1536]{1,0:T(8,128)(2,1)} %param.10) | copy-start | bytes 3538948
  0.6 11.5 %copy-start.7 = (bf16[512,384]{1,0:T(8,128)(2,1)S(1)}, bf16[512,384]{1,0:T(8,128)(2,1)}, u32[]{:S(2)}) copy-start(bf16[512,384]{1,0:T(8,128)(2,1)} %param.11) | copy-start | bytes 1179652
  0.7 16.1 %copy-start.12 = (s32[64,2]{0,1:T(2,128)S(1)}, s32[64,2]{0,1:T(2,128)}, u32[]{:S(2)}) copy-start(s32[64,2]{0,1:T(2,128)} %param.12) | copy-start | bytes 1540
  2.9 15.5 %copy-start.4 = (s32[512]{0:T(512)S(1)}, s32[512]{0:T(512)}, u32[]{:S(2)}) copy-start(s32[512]{0:T(512)} %param.13) | copy-start | bytes 6148
  2.9 24.8 %collective-permute-start.2 = (bf16[2,512,384]{2,1,0:T(8,128)(2,1)}, bf16[2,512,384]{2,1,0:T(8,128)(2,1)S(1)}, u32[]{:S(2)}, u32[]{:S(2)}) collective-permute-start(bf16[2,512,384]{2,1,0:T(8,128)(2,1)} %pad_maximum_fusion), channel_id=1, source_target_pairs={{8,0},{12,4},{16,8},{20,12},{24,16},{28,20},{32,24},{36,28},{40,32... | collective-permute-start | bytes 2359304 | tf_op jit(solution)/shard_map/ppermute | solution.py:17
  5.7 23.3 %collective-permute-start = (bf16[2,512,384]{2,1,0:T(8,128)(2,1)}, bf16[2,512,384]{2,1,0:T(8,128)(2,1)S(1)}, u32[]{:S(2)}, u32[]{:S(2)}) collective-permute-start(bf16[2,512,384]{2,1,0:T(8,128)(2,1)} %pad_maximum_fusion), channel_id=1, source_target_pairs={{0,8},{4,12},{8,16},{12,20},{16,24},{20,28},{24,32},{28,36},{32,40... | collective-permute-start | bytes 2359304 | tf_op jit(solution)/shard_map/ppermute | solution.py:17
  12.2 22.4 %collective-permute-start.5 = (bf16[512,384]{1,0:T(8,128)(2,1)S(1)}, bf16[512,384]{1,0:T(8,128)(2,1)}, u32[]{:S(2)}, u32[]{:S(2)}) collective-permute-start(bf16[512,384]{1,0:T(8,128)(2,1)S(1)} %copy-done.7), channel_id=1, source_target_pairs={{0,1},{1,2},{2,3},{3,0},{4,5},{5,6},{6,7},{7,4},{8,9},{9,10},{10,1... | collective-permute-start | bytes 1179656 | tf_op jit(solution)/shard_map/ppermute | solution.py:22
  13.3 9.6 %collective-permute-start.7 = (bf16[256,384]{1,0:T(8,128)(2,1)}, bf16[256,384]{1,0:T(8,128)(2,1)}, u32[]{:S(2)}, u32[]{:S(2)}) collective-permute-start(bf16[256,384]{1,0:T(8,128)(2,1)} %get-tuple-element.18), channel_id=1, source_target_pairs={{0,2},{1,3},{2,0},{3,1},{4,6},{5,7},{6,4},{7,5},{8,10},{9,11},{10,... | collective-permute-start | bytes 589832 | tf_op jit(solution)/shard_map/ppermute | solution.py:22
  15.9 14.6 %collective-permute-start.8 = (bf16[256,384]{1,0:T(8,128)(2,1)}, bf16[256,384]{1,0:T(8,128)(2,1)}, u32[]{:S(2)}, u32[]{:S(2)}) collective-permute-start(bf16[256,384]{1,0:T(8,128)(2,1)} %get-tuple-element.19), channel_id=1, source_target_pairs={{0,2},{1,3},{2,0},{3,1},{4,6},{5,7},{6,4},{7,5},{8,10},{9,11},{10,... | collective-permute-start | bytes 589832 | tf_op jit(solution)/shard_map/ppermute | solution.py:22
  18.5 16.1 %copy-start.5 = (f32[384,512]{0,1:T(8,128)S(1)}, f32[384,512]{0,1:T(8,128)}, u32[]{:S(2)}) copy-start(f32[384,512]{0,1:T(8,128)} %fusion.16) | copy-start | bytes 2359300
  22.9 22.2 %collective-permute-start.1 = (bf16[2,512,384]{2,1,0:T(8,128)(2,1)}, bf16[2,512,384]{2,1,0:T(8,128)(2,1)S(1)}, u32[]{:S(2)}, u32[]{:S(2)}) collective-permute-start(bf16[2,512,384]{2,1,0:T(8,128)(2,1)} %pad_maximum_fusion), channel_id=1, source_target_pairs={{0,4},{4,0},{8,12},{12,8},{16,20},{20,16},{24,28},{28,24},{32,36},... | collective-permute-start | bytes 2359304 | tf_op jit(solution)/shard_map/ppermute | solution.py:76
  27.7 17.3 %collective-permute-start.3 = (bf16[2,512,384]{2,1,0:T(8,128)(2,1)S(1)}, bf16[2,512,384]{2,1,0:T(8,128)(2,1)S(1)}, u32[]{:S(2)}, u32[]{:S(2)}) collective-permute-start(bf16[2,512,384]{2,1,0:T(8,128)(2,1)S(1)} %collective-permute-done.2.refs_8_.refs_9_), channel_id=1, source_target_pairs={{0,4},{8,12},{16,20},{24,28},{32,36},{40,44},{48,52},{56,60},{64,6... | collective-permute-start | bytes 2359304 | tf_op jit(solution)/shard_map/ppermute | solution.py:81
  29.1 16.0 %collective-permute-start.4 = (bf16[2,512,384]{2,1,0:T(8,128)(2,1)S(1)}, bf16[2,512,384]{2,1,0:T(8,128)(2,1)S(1)}, u32[]{:S(2)}, u32[]{:S(2)}) collective-permute-start(bf16[2,512,384]{2,1,0:T(8,128)(2,1)S(1)} %collective-permute-done.refs_0_.refs_1_), channel_id=1, source_target_pairs={{4,0},{12,8},{20,16},{28,24},{36,32},{44,40},{52,48},{60,56},{68,6... | collective-permute-start | bytes 2359304 | tf_op jit(solution)/shard_map/ppermute | solution.py:86
  30.4 14.2 %collective-permute-start.6 = (bf16[512,384]{1,0:T(8,128)(2,1)S(1)}, bf16[512,384]{1,0:T(8,128)(2,1)S(1)}, u32[]{:S(2)}, u32[]{:S(2)}) collective-permute-start(bf16[512,384]{1,0:T(8,128)(2,1)S(1)} %copy-done.7), channel_id=1, source_target_pairs={{0,3},{1,0},{2,1},{3,2},{4,7},{5,4},{6,5},{7,6},{8,11},{9,8},{10,9... | collective-permute-start | bytes 1179656 | tf_op jit(solution)/shard_map/ppermute | solution.py:22
  36.1 9.0 %copy-start.1 = (bf16[512,384]{1,0:T(8,128)(2,1)S(1)}, bf16[512,384]{1,0:T(8,128)(2,1)}, u32[]{:S(2)}) copy-start(bf16[512,384]{1,0:T(8,128)(2,1)} %k0_ref.1) | copy-start | bytes 1179652
  36.1 9.0 %copy-start.2 = (bf16[512,384]{1,0:T(8,128)(2,1)S(1)}, bf16[512,384]{1,0:T(8,128)(2,1)}, u32[]{:S(2)}) copy-start(bf16[512,384]{1,0:T(8,128)(2,1)} %v0_ref.1) | copy-start | bytes 1179652
  36.1 9.0 %copy-start.3 = (bf16[512,384]{1,0:T(8,128)(2,1)S(1)}, bf16[512,384]{1,0:T(8,128)(2,1)}, u32[]{:S(2)}) copy-start(bf16[512,384]{1,0:T(8,128)(2,1)} %q_ref.1) | copy-start | bytes 1179652
  61.2 9.2 %copy-start.6 = (bf16[4,2,512,384]{3,2,1,0:T(8,128)(2,1)S(1)}, bf16[4,2,512,384]{3,2,1,0:T(8,128)(2,1)}, u32[]{:S(2)}) copy-start(bf16[4,2,512,384]{3,2,1,0:T(8,128)(2,1)} %get-tuple-element.11) | copy-start | bytes 9437188
  63.0 7.3 %collective-permute-start.14 = (bf16[2,2,512,384]{3,2,1,0:T(8,128)(2,1)S(1)}, bf16[2,2,512,384]{3,2,1,0:T(8,128)(2,1)S(1)}, u32[]{:S(2)}, u32[]{:S(2)}) collective-permute-start(bf16[2,2,512,384]{3,2,1,0:T(8,128)(2,1)S(1)} %slice.43), channel_id=1, source_target_pairs={{4,0},{12,8},{20,16},{28,24},{36,32},{44,40},{52,48},{60,56},{68,6... | collective-permute-start | bytes 4718600 | tf_op jit(solution)/shard_map/ppermute | solution.py:86
  64.3 6.2 %collective-permute-start.13 = (bf16[2,2,512,384]{3,2,1,0:T(8,128)(2,1)S(1)}, bf16[2,2,512,384]{3,2,1,0:T(8,128)(2,1)S(1)}, u32[]{:S(2)}, u32[]{:S(2)}) collective-permute-start(bf16[2,2,512,384]{3,2,1,0:T(8,128)(2,1)S(1)} %slice.43), channel_id=1, source_target_pairs={{0,4},{8,12},{16,20},{24,28},{32,36},{40,44},{48,52},{56,60},{64,6... | collective-permute-start | bytes 4718600 | tf_op jit(solution)/shard_map/ppermute | solution.py:81
  68.6 15.1 %collective-permute-start.11 = (bf16[256,384]{1,0:T(8,128)(2,1)S(1)}, bf16[256,384]{1,0:T(8,128)(2,1)}, u32[]{:S(2)}, u32[]{:S(2)}) collective-permute-start(bf16[256,384]{1,0:T(8,128)(2,1)S(1)} %get-tuple-element.16), channel_id=1, source_target_pairs={{0,2},{1,3},{2,0},{3,1},{4,6},{5,7},{6,4},{7,5},{8,10},{9,11},{10,... | collective-permute-start | bytes 589832 | tf_op jit(solution)/shard_map/ppermute | solution.py:22
  70.3 2.0 %copy-start.9 = (bf16[2,2,512,384]{3,2,1,0:T(8,128)(2,1)}, bf16[2,2,512,384]{3,2,1,0:T(8,128)(2,1)S(1)}, u32[]{:S(2)}) copy-start(bf16[2,2,512,384]{3,2,1,0:T(8,128)(2,1)S(1)} %collective-permute-done.14) | copy-start | bytes 4718596
  70.4 2.1 %copy-start.11 = (bf16[2,2,512,384]{3,2,1,0:T(8,128)(2,1)}, bf16[2,2,512,384]{3,2,1,0:T(8,128)(2,1)S(1)}, u32[]{:S(2)}) copy-start(bf16[2,2,512,384]{3,2,1,0:T(8,128)(2,1)S(1)} %collective-permute-done.13) | copy-start | bytes 4718596
  72.5 28.3 %collective-permute-start.15 = (bf16[2,512,384]{2,1,0:T(8,128)(2,1)}, bf16[2,512,384]{2,1,0:T(8,128)(2,1)}, u32[]{:S(2)}, u32[]{:S(2)}) collective-permute-start(bf16[2,512,384]{2,1,0:T(8,128)(2,1)} %get-tuple-element.12), channel_id=1, source_target_pairs={{0,8},{4,12},{8,16},{12,20},{16,24},{20,28},{24,32},{28,36},{32,40... | collective-permute-start | bytes 2359304 | tf_op jit(solution)/shard_map/ppermute | solution.py:17
  78.5 25.2 %copy-start.8 = (f32[2,512,384]{2,1,0:T(8,128)S(1)}, f32[2,512,384]{2,1,0:T(8,128)}, u32[]{:S(2)}) copy-start(f32[2,512,384]{2,1,0:T(8,128)} %get-tuple-element.10) | copy-start | bytes 4718596
  78.5 25.2 %collective-permute-start.16 = (bf16[2,512,384]{2,1,0:T(8,128)(2,1)}, bf16[2,512,384]{2,1,0:T(8,128)(2,1)}, u32[]{:S(2)}, u32[]{:S(2)}) collective-permute-start(bf16[2,512,384]{2,1,0:T(8,128)(2,1)} %get-tuple-element.13), channel_id=1, source_target_pairs={{8,0},{12,4},{16,8},{20,12},{24,16},{28,20},{32,24},{36,28},{40,32... | collective-permute-start | bytes 2359304 | tf_op jit(solution)/shard_map/ppermute | solution.py:17
  81.7 16.5 %collective-permute-start.9 = (bf16[512,384]{1,0:T(8,128)(2,1)}, bf16[512,384]{1,0:T(8,128)(2,1)}, u32[]{:S(2)}, u32[]{:S(2)}) collective-permute-start(bf16[512,384]{1,0:T(8,128)(2,1)} %convolution_convert_fusion.2), channel_id=1, source_target_pairs={{0,1},{1,2},{2,3},{3,0},{4,5},{5,6},{6,7},{7,4},{8,9},{9,10},{10,1... | collective-permute-start | bytes 1179656 | tf_op jit(solution)/shard_map/ppermute | solution.py:22
  83.0 15.4 %collective-permute-start.10 = (bf16[512,384]{1,0:T(8,128)(2,1)S(1)}, bf16[512,384]{1,0:T(8,128)(2,1)}, u32[]{:S(2)}, u32[]{:S(2)}) collective-permute-start(bf16[512,384]{1,0:T(8,128)(2,1)S(1)} %convolution_convert_fusion.1), channel_id=1, source_target_pairs={{0,3},{1,0},{2,1},{3,2},{4,7},{5,4},{6,5},{7,6},{8,11},{9,8},{10,9... | collective-permute-start | bytes 1179656 | tf_op jit(solution)/shard_map/ppermute | solution.py:22
  83.7 14.5 %collective-permute-start.12 = (bf16[256,384]{1,0:T(8,128)(2,1)}, bf16[256,384]{1,0:T(8,128)(2,1)}, u32[]{:S(2)}, u32[]{:S(2)}) collective-permute-start(bf16[256,384]{1,0:T(8,128)(2,1)} %get-tuple-element.17), channel_id=1, source_target_pairs={{0,2},{1,3},{2,0},{3,1},{4,6},{5,7},{6,4},{7,5},{8,10},{9,11},{10,... | collective-permute-start | bytes 589832 | tf_op jit(solution)/shard_map/ppermute | solution.py:22
  86.3 17.4 %copy-start.10 = (bf16[2,2,512,384]{3,2,1,0:T(8,128)(2,1)S(1)}, bf16[2,2,512,384]{3,2,1,0:T(8,128)(2,1)}, u32[]{:S(2)}) copy-start(bf16[2,2,512,384]{3,2,1,0:T(8,128)(2,1)} %copy-done.9) | copy-start | bytes 4718596

commit v2 on v1

--- a/solution.py
+++ b/solution.py
@@ -90,7 +90,7 @@
     n_cand = 5
     cand_k = refs[0:2 * n_cand:2]
     cand_v = refs[1:2 * n_cand:2]
-    g_ref, srow_ref, scol_ref, attn_ref, dq_ref, self_ref, terms_ref = refs[2 * n_cand:]
+    g_ref, srow_ref, scol_ref, attn_ref, dq_ref, self_ref, near_ref, far_ref = refs[2 * n_cand:]
     scale = HEAD_DIM ** (-0.5)
 
     def pick(cands, slot):
@@ -143,9 +143,9 @@
             routed.append((sel_ref[2 + j], dk.astype(jnp.bfloat16), dv.astype(jnp.bfloat16)))
     (off1, dk1, dv1), (off2, dk2, dv2) = routed
     zero = jnp.zeros_like(dk1)
-    for slot, value in enumerate((-2, -1, 1, 2)):
-        terms_ref[slot, 0] = jnp.where(off1 == value, dk1, jnp.where(off2 == value, dk2, zero))
-        terms_ref[slot, 1] = jnp.where(off1 == value, dv1, jnp.where(off2 == value, dv2, zero))
+    for ref, slot, value in ((far_ref, 0, -2), (near_ref, 0, -1), (near_ref, 1, 1), (far_ref, 1, 2)):
+        ref[slot, 0] = jnp.where(off1 == value, dk1, jnp.where(off2 == value, dk2, zero))
+        ref[slot, 1] = jnp.where(off1 == value, dv1, jnp.where(off2 == value, dv2, zero))
     dq_ref[...] = dq.astype(jnp.bfloat16)
 
 
@@ -157,7 +157,7 @@
     spec_ck = pl.BlockSpec((None, rows, d), lambda h, s: (0, 0, h))
     spec_cv = pl.BlockSpec((None, rows, d), lambda h, s: (1, 0, h))
     spec_self = pl.BlockSpec((2, rows, d), lambda h, s: (0, 0, h))
-    spec_terms = pl.BlockSpec((4, 2, rows, d), lambda h, s: (0, 0, 0, h))
+    spec_terms = pl.BlockSpec((2, 2, rows, d), lambda h, s: (0, 0, 0, h))
     cand_specs = []
     cand_args = []
     for c in cands:
@@ -169,13 +169,14 @@
         in_specs=[spec_q, spec_q, spec_q] + cand_specs + [spec_q,
                   pl.BlockSpec((rows, 1), lambda h, s: (0, 0)),
                   pl.BlockSpec((1, rows), lambda h, s: (0, 0))],
-        out_specs=[spec_q, spec_q, spec_self, spec_terms],
+        out_specs=[spec_q, spec_q, spec_self, spec_terms, spec_terms],
     )
     out_shape = [
         jax.ShapeDtypeStruct((rows, columns), jnp.bfloat16),
         jax.ShapeDtypeStruct((rows, columns), jnp.bfloat16),
         jax.ShapeDtypeStruct((2, rows, columns), jnp.float32),
-        jax.ShapeDtypeStruct((4, 2, rows, columns), jnp.bfloat16),
+        jax.ShapeDtypeStruct((2, 2, rows, columns), jnp.bfloat16),
+        jax.ShapeDtypeStruct((2, 2, rows, columns), jnp.bfloat16),
     ]
     kwargs = {}
     if INTERPRET is not None:
@@ -205,13 +206,12 @@
     pick = jnp.where(offs == -2, 0, jnp.where(offs == 2, 4, jnp.where(offs == partner_off, 1, relay_idx)))
     sel = jnp.concatenate([pick.astype(jnp.int32), jnp.zeros((1,), jnp.int32), offs])
     cands = (from_left2, partner_own, relay_to_odd, relay_to_even, from_right2)
-    attn, grad_q, self_term, terms = attention(sel, queries, keys, values, cands, grad_attn, shot_ids)
+    attn, grad_q, self_term, near, far = attention(sel, queries, keys, values, cands, grad_attn, shot_ids)
     attn_out = project_out(attn, out_weight)
-    near = terms[1:3]
     got_a = even_to_odd(near, "seq")
     got_b = odd_to_even(near, "seq")
-    up_plus = (terms[3].astype(jnp.float32) + got_b[1].astype(jnp.float32)).astype(jnp.bfloat16)
-    up_minus = (terms[0].astype(jnp.float32) + got_a[0].astype(jnp.float32)).astype(jnp.bfloat16)
+    up_plus = (far[1].astype(jnp.float32) + got_b[1].astype(jnp.float32)).astype(jnp.bfloat16)
+    up_minus = (far[0].astype(jnp.float32) + got_a[0].astype(jnp.float32)).astype(jnp.bfloat16)
     got_from_left = shifted(up_plus, "seq", 2)
     got_from_right = shifted(up_minus, "seq", -2)
     total = (

time: 108 us -> 106 us (0.981)
  local copies, waits for them, and re-layouts: 4.5 us -> 2.66 us
    slice x1 -> x0, local copies, waits for them, and re-layouts: 1.72 us -> none  [on_device(): near = terms[1:3]]
where the time goes in v2:
time: 106 us; the launch traced here: 105 us
  starting transfers between devices  37.1 us (35%)
  waiting for transfers between devices  33.1 us (31%)
  Pallas kernels  16.1 us (15%)
  matrix products  8.97 us (8%)
  other arithmetic  6.36 us (6%)
  local copies, waits for them, and re-layouts  2.66 us (3%)
    ppermute x8, waiting for transfers between devices, ring_shift(): lax.ppermute(block, axis, [(i, (i + distance) % size) for i in range(size)])  25.1 us
    ppermute x4, starting transfers between devices, shifted(): return lax.ppermute(block, axis, route)  17.5 us
    pallas_call x1, Pallas kernels, attention(): pl.pallas_call(attn_kernel, grid_spec=grid_spec, out_shape=out_shape, com...  16.1 us
    ppermute x8, starting transfers between devices, ring_shift(): lax.ppermute(block, axis, [(i, (i + distance) % size) for i in range(size)])  12.3 us
    ppermute x4, waiting for transfers between devices, shifted(): return lax.ppermute(block, axis, route)  7.76 us
    dot_general x4, matrix products, fold_cotangent(): lax.dot_general(piece, w_cols, nt, preferred_element_type=jnp.float32)  4.6 us
    ppermute x2, starting transfers between devices, even_to_odd(): lax.ppermute(block, axis, [(i, i + 1) for i in range(0, size - 1, 2)])  4.55 us
    ppermute x2, starting transfers between devices, odd_to_even(): return lax.ppermute(block, axis, [(i, i - 1) for i in range(1, size, 2)])  2.7 us
  transfers between devices with their start and end apart: 17, of which 7 were waited for; matrix products, arithmetic and copies ran while one was open for 12% of the time, Pallas kernels for 0%

profile of v2, /device:TPU:126, one launch (start us, length us, event | category | flops | bytes accessed | tf_op | source)
XLA Modules:
  0.0 105.3 jit_solution(11253141328322585976)
XLA Ops:
  0.7 2.2 %pad_maximum_fusion = bf16[2,512,384]{2,1,0:T(8,128)(2,1)} fusion(bf16[1,512,384]{2,1,0:T(8,128)(2,1)} %bitcast.36, bf16[1,512,384]{2,1,0:T(8,128)(2,1)} %bitcast.35), kind=kLoop, calls=%fused_computation.23 | loop fusion | flops 393216 | bytes 1572864 | tf_op jit(solution)/shard_map/stack | solution.py:197
  2.9 2.9 %collective-permute-start.2 = (bf16[2,512,384]{2,1,0:T(8,128)(2,1)}, bf16[2,512,384]{2,1,0:T(8,128)(2,1)S(1)}, u32[]{:S(2)}, u32[]{:S(2)}) collective-permute-start(bf16[2,512,384]{2,1,0:T(8,128)(2,1)} %pad_maximum_fusion), channel_id=1, source_target_pairs={{8,0},{12,4},{16,8},{20,12},{24,16},{28,20},{32,24},{36,28},{40,32... | collective-permute-start | bytes 2359304 | tf_op jit(solution)/shard_map/ppermute | solution.py:17
  5.7 6.4 %collective-permute-start = (bf16[2,512,384]{2,1,0:T(8,128)(2,1)}, bf16[2,512,384]{2,1,0:T(8,128)(2,1)S(1)}, u32[]{:S(2)}, u32[]{:S(2)}) collective-permute-start(bf16[2,512,384]{2,1,0:T(8,128)(2,1)} %pad_maximum_fusion), channel_id=1, source_target_pairs={{0,8},{4,12},{8,16},{12,20},{16,24},{20,28},{24,32},{28,36},{32,40... | collective-permute-start | bytes 2359304 | tf_op jit(solution)/shard_map/ppermute | solution.py:17
  12.5 0.8 fusion.36
  13.3 2.6 %collective-permute-start.7 = (bf16[256,384]{1,0:T(8,128)(2,1)}, bf16[256,384]{1,0:T(8,128)(2,1)}, u32[]{:S(2)}, u32[]{:S(2)}) collective-permute-start(bf16[256,384]{1,0:T(8,128)(2,1)} %get-tuple-element.20), channel_id=1, source_target_pairs={{0,2},{1,3},{2,0},{3,1},{4,6},{5,7},{6,4},{7,5},{8,10},{9,11},{10,... | collective-permute-start | bytes 589832 | tf_op jit(solution)/shard_map/ppermute | solution.py:22
  15.9 0.9 collective-permute-start.8
  17.0 1.4 %fusion.16 = f32[384,512]{0,1:T(8,128)} fusion(bf16[512,384]{1,0:T(8,128)(2,1)S(1)} %copy-done.6, bf16[384,1536]{1,0:T(8,128)(2,1)S(1)} %copy-done, s32[]{:T(128)S(6)} %select_n.72), kind=kOutput, calls=%fused_computation.31 | convolution fusion | flops 150994944 | bytes 1474564 | tf_op jit(solution)/shard_map/dot_general | solution.py:43
  18.5 4.3 %collective-permute-done.7 = bf16[256,384]{1,0:T(8,128)(2,1)} collective-permute-done((bf16[256,384]{1,0:T(8,128)(2,1)}, bf16[256,384]{1,0:T(8,128)(2,1)}, u32[]{:S(2)}, u32[]{:S(2)}) %collective-permute-start.7) | collective-permute-done | bytes 196640 | tf_op jit(solution)/shard_map/ppermute | solution.py:22
  22.9 4.8 %collective-permute-done.2.refs_8_.refs_9_ = bf16[2,512,384]{2,1,0:T(8,128)(2,1)S(1)} collective-permute-done((bf16[2,512,384]{2,1,0:T(8,128)(2,1)}, bf16[2,512,384]{2,1,0:T(8,128)(2,1)S(1)}, u32[]{:S(2)}, u32[]{:S(2)}) %collective-permute-start.2) | collective-permute-done | bytes 786464 | tf_op jit(solution)/shard_map/ppermute | solution.py:17
  27.7 1.3 %collective-permute-start.3 = (bf16[2,512,384]{2,1,0:T(8,128)(2,1)S(1)}, bf16[2,512,384]{2,1,0:T(8,128)(2,1)S(1)}, u32[]{:S(2)}, u32[]{:S(2)}) collective-permute-start(bf16[2,512,384]{2,1,0:T(8,128)(2,1)S(1)} %collective-permute-done.2.refs_8_.refs_9_), channel_id=1, source_target_pairs={{0,4},{8,12},{16,20},{24,28},{32,36},{40,44},{48,52},{56,60},{64,6... | collective-permute-start | bytes 2359304 | tf_op jit(solution)/shard_map/ppermute | solution.py:81
  29.1 1.3 %collective-permute-start.4 = (bf16[2,512,384]{2,1,0:T(8,128)(2,1)S(1)}, bf16[2,512,384]{2,1,0:T(8,128)(2,1)S(1)}, u32[]{:S(2)}, u32[]{:S(2)}) collective-permute-start(bf16[2,512,384]{2,1,0:T(8,128)(2,1)S(1)} %collective-permute-done.refs_0_.refs_1_), channel_id=1, source_target_pairs={{4,0},{12,8},{20,16},{28,24},{36,32},{44,40},{52,48},{60,56},{68,6... | collective-permute-start | bytes 2359304 | tf_op jit(solution)/shard_map/ppermute | solution.py:86
  30.4 2.8 %collective-permute-start.6 = (bf16[512,384]{1,0:T(8,128)(2,1)S(1)}, bf16[512,384]{1,0:T(8,128)(2,1)S(1)}, u32[]{:S(2)}, u32[]{:S(2)}) collective-permute-start(bf16[512,384]{1,0:T(8,128)(2,1)S(1)} %copy-done.6), channel_id=1, source_target_pairs={{0,3},{1,0},{2,1},{3,2},{4,7},{5,4},{6,5},{7,6},{8,11},{9,8},{10,9... | collective-permute-start | bytes 1179656 | tf_op jit(solution)/shard_map/ppermute | solution.py:22
  33.2 1.4 %fusion.11 = f32[512,384]{1,0:T(8,128)S(1)} fusion(bf16[256,384]{1,0:T(8,128)(2,1)} %collective-permute-done.8, bf16[256,384]{1,0:T(8,128)(2,1)} %collective-permute-done.7, bf16[384,1536]{1,0:T(8,128)(2,1)S(1)} %copy-done, s32[]{:T(128)S(6)} %select_n.78), kind=kOutput, calls=%fused_computation.26 | convolution fusion | flops 151781376 | bytes 1474564 | tf_op jit(solution)/shard_map/dot_general | solution.py:43
  34.6 1.4 %convolution_add_fusion.2 = f32[384,512]{0,1:T(8,128)S(1)} fusion(f32[384,512]{0,1:T(8,128)S(1)} %copy-done.5, bf16[512,384]{1,0:T(8,128)(2,1)} %collective-permute-done.5, bf16[384,1536]{1,0:T(8,128)(2,1)S(1)} %copy-done, s32[]{:T(128)S(6)} %select_n.74), kind=kOutput, calls=%fused_computation.10 | convolution fusion | flops 151191552 | bytes 2260996 | tf_op jit(solution)/shard_map/dot_general | solution.py:43
  36.1 8.5 %collective-permute-done.6 = bf16[512,384]{1,0:T(8,128)(2,1)S(1)} collective-permute-done((bf16[512,384]{1,0:T(8,128)(2,1)S(1)}, bf16[512,384]{1,0:T(8,128)(2,1)S(1)}, u32[]{:S(2)}, u32[]{:S(2)}) %collective-permute-start.6) | collective-permute-done | bytes 393248 | tf_op jit(solution)/shard_map/ppermute | solution.py:22
  45.1 16.1 %shard_map.102 = (bf16[512,384]{1,0:T(8,128)(2,1)S(1)}, bf16[512,384]{1,0:T(8,128)(2,1)}, f32[2,512,384]{2,1,0:T(8,128)}, bf16[2,2,512,384]{3,2,1,0:T(8,128)(2,1)}, bf16[2,2,512,384]{3,2,1,0:T(8,128)(2,1)}) custom-call(s32[5]{0:T(128)S(1)} %pad_add_fusion.sel_ref, bf16[512,384]{1,0:T(8,128)(2,1)S(1)} %copy-done.3, bf16[512,384]{1,0:T(8,128)(2,1)S(1)} %copy-done.1, ...), custom_call_target="tpu_custom_call" | custom-call | tf_op jit(solution)/shard_map/pallas_call | solution.py:184
  61.2 1.4 %collective-permute-start.14 = (bf16[2,2,512,384]{3,2,1,0:T(8,128)(2,1)}, bf16[2,2,512,384]{3,2,1,0:T(8,128)(2,1)S(1)}, u32[]{:S(2)}, u32[]{:S(2)}) collective-permute-start(bf16[2,2,512,384]{3,2,1,0:T(8,128)(2,1)} %get-tuple-element.12), channel_id=1, source_target_pairs={{4,0},{12,8},{20,16},{28,24},{36,32},{44,40},{52,48},{60,56},{68,6... | collective-permute-start | bytes 4718600 | tf_op jit(solution)/shard_map/ppermute | solution.py:86
  62.6 3.2 %collective-permute-start.13 = (bf16[2,2,512,384]{3,2,1,0:T(8,128)(2,1)}, bf16[2,2,512,384]{3,2,1,0:T(8,128)(2,1)S(1)}, u32[]{:S(2)}, u32[]{:S(2)}) collective-permute-start(bf16[2,2,512,384]{3,2,1,0:T(8,128)(2,1)} %get-tuple-element.12), channel_id=1, source_target_pairs={{0,4},{8,12},{16,20},{24,28},{32,36},{40,44},{48,52},{56,60},{64,6... | collective-permute-start | bytes 4718600 | tf_op jit(solution)/shard_map/ppermute | solution.py:81
  66.3 0.7 fusion.35
  67.0 1.3 %collective-permute-start.11 = (bf16[256,384]{1,0:T(8,128)(2,1)S(1)}, bf16[256,384]{1,0:T(8,128)(2,1)}, u32[]{:S(2)}, u32[]{:S(2)}) collective-permute-start(bf16[256,384]{1,0:T(8,128)(2,1)S(1)} %get-tuple-element.18), channel_id=1, source_target_pairs={{0,2},{1,3},{2,0},{3,1},{4,6},{5,7},{6,4},{7,5},{8,10},{9,11},{10,... | collective-permute-start | bytes 589832 | tf_op jit(solution)/shard_map/ppermute | solution.py:22
  69.0 1.8 %fusion.9 = (bf16[2,512,384]{2,1,0:T(8,128)(2,1)}, bf16[2,512,384]{2,1,0:T(8,128)(2,1)}) fusion(bf16[2,2,512,384]{3,2,1,0:T(8,128)(2,1)S(1)} %collective-permute-done.14, bf16[2,2,512,384]{3,2,1,0:T(8,128)(2,1)S(1)} %copy-done.11, bf16[2,2,512,384]{3,2,1,0:T(8,128)(2,1)S(1)} %collective-permute-done.13), kind=kLoop, calls=%fused_computation.19 | loop fusion | flops 3145728 | bytes 4718592 | tf_op jit(solution)/shard_map/convert_element_type | solution.py:213
  70.8 6.2 %collective-permute-start.15 = (bf16[2,512,384]{2,1,0:T(8,128)(2,1)}, bf16[2,512,384]{2,1,0:T(8,128)(2,1)}, u32[]{:S(2)}, u32[]{:S(2)}) collective-permute-start(bf16[2,512,384]{2,1,0:T(8,128)(2,1)} %get-tuple-element.14), channel_id=1, source_target_pairs={{0,8},{4,12},{8,16},{12,20},{16,24},{20,28},{24,32},{28,36},{32,40... | collective-permute-start | bytes 2359304 | tf_op jit(solution)/shard_map/ppermute | solution.py:17
  77.0 2.1 %collective-permute-start.16 = (bf16[2,512,384]{2,1,0:T(8,128)(2,1)}, bf16[2,512,384]{2,1,0:T(8,128)(2,1)}, u32[]{:S(2)}, u32[]{:S(2)}) collective-permute-start(bf16[2,512,384]{2,1,0:T(8,128)(2,1)} %get-tuple-element.15), channel_id=1, source_target_pairs={{8,0},{12,4},{16,8},{20,12},{24,16},{28,20},{32,24},{36,28},{40,32... | collective-permute-start | bytes 2359304 | tf_op jit(solution)/shard_map/ppermute | solution.py:17
  79.1 1.1 %convolution_convert_fusion.2 = bf16[512,384]{1,0:T(8,128)(2,1)} fusion(bf16[512,384]{1,0:T(8,128)(2,1)S(1)} %get-tuple-element.9, bf16[384,1536]{1,0:T(8,128)(2,1)S(1)} %copy-done, s32[]{:T(128)S(6)} %select_n.76), kind=kOutput, calls=%fused_computation.18 | convolution fusion | flops 151191552 | bytes 1081348 | tf_op jit(solution)/shard_map/dot_general | solution.py:56
  80.2 1.1 %collective-permute-start.9 = (bf16[512,384]{1,0:T(8,128)(2,1)}, bf16[512,384]{1,0:T(8,128)(2,1)}, u32[]{:S(2)}, u32[]{:S(2)}) collective-permute-start(bf16[512,384]{1,0:T(8,128)(2,1)} %convolution_convert_fusion.2), channel_id=1, source_target_pairs={{0,1},{1,2},{2,3},{3,0},{4,5},{5,6},{6,7},{7,4},{8,9},{9,10},{10,1... | collective-permute-start | bytes 1179656 | tf_op jit(solution)/shard_map/ppermute | solution.py:22
  81.3 0.9 collective-permute-start.10
  82.3 2.4 %collective-permute-start.12 = (bf16[256,384]{1,0:T(8,128)(2,1)}, bf16[256,384]{1,0:T(8,128)(2,1)}, u32[]{:S(2)}, u32[]{:S(2)}) collective-permute-start(bf16[256,384]{1,0:T(8,128)(2,1)} %get-tuple-element.19), channel_id=1, source_target_pairs={{0,2},{1,3},{2,0},{3,1},{4,6},{5,7},{6,4},{7,5},{8,10},{9,11},{10,... | collective-permute-start | bytes 589832 | tf_op jit(solution)/shard_map/ppermute | solution.py:22
  84.7 11.9 %collective-permute-done.12 = bf16[256,384]{1,0:T(8,128)(2,1)} collective-permute-done((bf16[256,384]{1,0:T(8,128)(2,1)}, bf16[256,384]{1,0:T(8,128)(2,1)}, u32[]{:S(2)}, u32[]{:S(2)}) %collective-permute-start.12) | collective-permute-done | bytes 196640 | tf_op jit(solution)/shard_map/ppermute | solution.py:22
  96.9 2.4 %fusion.7 = bf16[512,384]{1,0:T(8,128)(2,1)} fusion(bf16[512,384]{1,0:T(8,128)(2,1)S(1)} %get-tuple-element.9, bf16[512,384]{1,0:T(8,128)(2,1)} %collective-permute-done.10, bf16[512,384]{1,0:T(8,128)(2,1)} %collective-permute-done.9, bf16[256,384]{1,0:T(8,128)(2,1)} %collective-permute-done.12, bf16[256,384]{1,0:T(8,128)(2,1)} %collective-permute-done.11, ...), kind=kOutput, calls=%fused_computation.14 | convolution fusion | flops 152961024 | bytes 2260996 | tf_op jit(solution)/shard_map/dot_general | solution.py:66
  99.3 2.9 %collective-permute-done.16 = bf16[2,512,384]{2,1,0:T(8,128)(2,1)} collective-permute-done((bf16[2,512,384]{2,1,0:T(8,128)(2,1)}, bf16[2,512,384]{2,1,0:T(8,128)(2,1)}, u32[]{:S(2)}, u32[]{:S(2)}) %collective-permute-start.16) | collective-permute-done | bytes 786464 | tf_op jit(solution)/shard_map/ppermute | solution.py:17
  102.2 2.1 %fusion.2 = bf16[2,512,384]{2,1,0:T(8,128)(2,1)S(1)} fusion(f32[2,512,384]{2,1,0:T(8,128)S(1)} %copy-done.7, bf16[2,512,384]{2,1,0:T(8,128)(2,1)} %collective-permute-done.16, bf16[2,512,384]{2,1,0:T(8,128)(2,1)} %collective-permute-done.15, bf16[2,2,512,384]{3,2,1,0:T(8,128)(2,1)S(1)} %copy-done.9, bf16[2,2,512,384]{3,2,1,0:T(8,128)(2,1)} %copy-done.10), kind=kLoop, calls=%fused_computation.3 | loop fusion | flops 3538944 | bytes 5505024 | tf_op jit(solution)/shard_map/convert_element_type | solution.py:224
  104.3 1.0 slice_bitcast_fusion.2
  (47 shorter events, 2.6 us)
Async XLA Ops:
  0.6 16.4 %copy-start = (bf16[384,1536]{1,0:T(8,128)(2,1)S(1)}, bf16[384,1536]{1,0:T(8,128)(2,1)}, u32[]{:S(2)}) copy-start(bf16[384,1536]{1,0:T(8,128)(2,1)} %param.10) | copy-start | bytes 3538948
  0.6 11.5 %copy-start.6 = (bf16[512,384]{1,0:T(8,128)(2,1)S(1)}, bf16[512,384]{1,0:T(8,128)(2,1)}, u32[]{:S(2)}) copy-start(bf16[512,384]{1,0:T(8,128)(2,1)} %param.11) | copy-start | bytes 1179652
  0.7 16.1 %copy-start.12 = (s32[64,2]{0,1:T(2,128)S(1)}, s32[64,2]{0,1:T(2,128)}, u32[]{:S(2)}) copy-start(s32[64,2]{0,1:T(2,128)} %param.12) | copy-start | bytes 1540
  2.9 15.5 %copy-start.4 = (s32[512]{0:T(512)S(1)}, s32[512]{0:T(512)}, u32[]{:S(2)}) copy-start(s32[512]{0:T(512)} %param.13) | copy-start | bytes 6148
  2.9 24.8 %collective-permute-start.2 = (bf16[2,512,384]{2,1,0:T(8,128)(2,1)}, bf16[2,512,384]{2,1,0:T(8,128)(2,1)S(1)}, u32[]{:S(2)}, u32[]{:S(2)}) collective-permute-start(bf16[2,512,384]{2,1,0:T(8,128)(2,1)} %pad_maximum_fusion), channel_id=1, source_target_pairs={{8,0},{12,4},{16,8},{20,12},{24,16},{28,20},{32,24},{36,28},{40,32... | collective-permute-start | bytes 2359304 | tf_op jit(solution)/shard_map/ppermute | solution.py:17
  5.7 23.3 %collective-permute-start = (bf16[2,512,384]{2,1,0:T(8,128)(2,1)}, bf16[2,512,384]{2,1,0:T(8,128)(2,1)S(1)}, u32[]{:S(2)}, u32[]{:S(2)}) collective-permute-start(bf16[2,512,384]{2,1,0:T(8,128)(2,1)} %pad_maximum_fusion), channel_id=1, source_target_pairs={{0,8},{4,12},{8,16},{12,20},{16,24},{20,28},{24,32},{28,36},{32,40... | collective-permute-start | bytes 2359304 | tf_op jit(solution)/shard_map/ppermute | solution.py:17
  12.2 22.4 %collective-permute-start.5 = (bf16[512,384]{1,0:T(8,128)(2,1)S(1)}, bf16[512,384]{1,0:T(8,128)(2,1)}, u32[]{:S(2)}, u32[]{:S(2)}) collective-permute-start(bf16[512,384]{1,0:T(8,128)(2,1)S(1)} %copy-done.6), channel_id=1, source_target_pairs={{0,1},{1,2},{2,3},{3,0},{4,5},{5,6},{6,7},{7,4},{8,9},{9,10},{10,1... | collective-permute-start | bytes 1179656 | tf_op jit(solution)/shard_map/ppermute | solution.py:22
  13.3 9.6 %collective-permute-start.7 = (bf16[256,384]{1,0:T(8,128)(2,1)}, bf16[256,384]{1,0:T(8,128)(2,1)}, u32[]{:S(2)}, u32[]{:S(2)}) collective-permute-start(bf16[256,384]{1,0:T(8,128)(2,1)} %get-tuple-element.20), channel_id=1, source_target_pairs={{0,2},{1,3},{2,0},{3,1},{4,6},{5,7},{6,4},{7,5},{8,10},{9,11},{10,... | collective-permute-start | bytes 589832 | tf_op jit(solution)/shard_map/ppermute | solution.py:22
  15.9 14.6 %collective-permute-start.8 = (bf16[256,384]{1,0:T(8,128)(2,1)}, bf16[256,384]{1,0:T(8,128)(2,1)}, u32[]{:S(2)}, u32[]{:S(2)}) collective-permute-start(bf16[256,384]{1,0:T(8,128)(2,1)} %get-tuple-element.21), channel_id=1, source_target_pairs={{0,2},{1,3},{2,0},{3,1},{4,6},{5,7},{6,4},{7,5},{8,10},{9,11},{10,... | collective-permute-start | bytes 589832 | tf_op jit(solution)/shard_map/ppermute | solution.py:22
  18.5 16.1 %copy-start.5 = (f32[384,512]{0,1:T(8,128)S(1)}, f32[384,512]{0,1:T(8,128)}, u32[]{:S(2)}) copy-start(f32[384,512]{0,1:T(8,128)} %fusion.16) | copy-start | bytes 2359300
  22.9 22.2 %collective-permute-start.1 = (bf16[2,512,384]{2,1,0:T(8,128)(2,1)}, bf16[2,512,384]{2,1,0:T(8,128)(2,1)S(1)}, u32[]{:S(2)}, u32[]{:S(2)}) collective-permute-start(bf16[2,512,384]{2,1,0:T(8,128)(2,1)} %pad_maximum_fusion), channel_id=1, source_target_pairs={{0,4},{4,0},{8,12},{12,8},{16,20},{20,16},{24,28},{28,24},{32,36},... | collective-permute-start | bytes 2359304 | tf_op jit(solution)/shard_map/ppermute | solution.py:76
  27.7 17.3 %collective-permute-start.3 = (bf16[2,512,384]{2,1,0:T(8,128)(2,1)S(1)}, bf16[2,512,384]{2,1,0:T(8,128)(2,1)S(1)}, u32[]{:S(2)}, u32[]{:S(2)}) collective-permute-start(bf16[2,512,384]{2,1,0:T(8,128)(2,1)S(1)} %collective-permute-done.2.refs_8_.refs_9_), channel_id=1, source_target_pairs={{0,4},{8,12},{16,20},{24,28},{32,36},{40,44},{48,52},{56,60},{64,6... | collective-permute-start | bytes 2359304 | tf_op jit(solution)/shard_map/ppermute | solution.py:81
  29.1 16.0 %collective-permute-start.4 = (bf16[2,512,384]{2,1,0:T(8,128)(2,1)S(1)}, bf16[2,512,384]{2,1,0:T(8,128)(2,1)S(1)}, u32[]{:S(2)}, u32[]{:S(2)}) collective-permute-start(bf16[2,512,384]{2,1,0:T(8,128)(2,1)S(1)} %collective-permute-done.refs_0_.refs_1_), channel_id=1, source_target_pairs={{4,0},{12,8},{20,16},{28,24},{36,32},{44,40},{52,48},{60,56},{68,6... | collective-permute-start | bytes 2359304 | tf_op jit(solution)/shard_map/ppermute | solution.py:86
  30.4 14.2 %collective-permute-start.6 = (bf16[512,384]{1,0:T(8,128)(2,1)S(1)}, bf16[512,384]{1,0:T(8,128)(2,1)S(1)}, u32[]{:S(2)}, u32[]{:S(2)}) collective-permute-start(bf16[512,384]{1,0:T(8,128)(2,1)S(1)} %copy-done.6), channel_id=1, source_target_pairs={{0,3},{1,0},{2,1},{3,2},{4,7},{5,4},{6,5},{7,6},{8,11},{9,8},{10,9... | collective-permute-start | bytes 1179656 | tf_op jit(solution)/shard_map/ppermute | solution.py:22
  36.1 9.0 %copy-start.1 = (bf16[512,384]{1,0:T(8,128)(2,1)S(1)}, bf16[512,384]{1,0:T(8,128)(2,1)}, u32[]{:S(2)}) copy-start(bf16[512,384]{1,0:T(8,128)(2,1)} %k0_ref.1) | copy-start | bytes 1179652
  36.1 9.0 %copy-start.2 = (bf16[512,384]{1,0:T(8,128)(2,1)S(1)}, bf16[512,384]{1,0:T(8,128)(2,1)}, u32[]{:S(2)}) copy-start(bf16[512,384]{1,0:T(8,128)(2,1)} %v0_ref.1) | copy-start | bytes 1179652
  36.1 9.0 %copy-start.3 = (bf16[512,384]{1,0:T(8,128)(2,1)S(1)}, bf16[512,384]{1,0:T(8,128)(2,1)}, u32[]{:S(2)}) copy-start(bf16[512,384]{1,0:T(8,128)(2,1)} %q_ref.1) | copy-start | bytes 1179652
  61.2 7.8 %copy-start.11 = (bf16[2,2,512,384]{3,2,1,0:T(8,128)(2,1)S(1)}, bf16[2,2,512,384]{3,2,1,0:T(8,128)(2,1)}, u32[]{:S(2)}) copy-start(bf16[2,2,512,384]{3,2,1,0:T(8,128)(2,1)} %get-tuple-element.13) | copy-start | bytes 4718596
  61.2 7.5 %collective-permute-start.14 = (bf16[2,2,512,384]{3,2,1,0:T(8,128)(2,1)}, bf16[2,2,512,384]{3,2,1,0:T(8,128)(2,1)S(1)}, u32[]{:S(2)}, u32[]{:S(2)}) collective-permute-start(bf16[2,2,512,384]{3,2,1,0:T(8,128)(2,1)} %get-tuple-element.12), channel_id=1, source_target_pairs={{4,0},{12,8},{20,16},{28,24},{36,32},{44,40},{52,48},{60,56},{68,6... | collective-permute-start | bytes 4718600 | tf_op jit(solution)/shard_map/ppermute | solution.py:86
  62.6 6.4 %collective-permute-start.13 = (bf16[2,2,512,384]{3,2,1,0:T(8,128)(2,1)}, bf16[2,2,512,384]{3,2,1,0:T(8,128)(2,1)S(1)}, u32[]{:S(2)}, u32[]{:S(2)}) collective-permute-start(bf16[2,2,512,384]{3,2,1,0:T(8,128)(2,1)} %get-tuple-element.12), channel_id=1, source_target_pairs={{0,4},{8,12},{16,20},{24,28},{32,36},{40,44},{48,52},{56,60},{64,6... | collective-permute-start | bytes 4718600 | tf_op jit(solution)/shard_map/ppermute | solution.py:81
  67.0 15.3 %collective-permute-start.11 = (bf16[256,384]{1,0:T(8,128)(2,1)S(1)}, bf16[256,384]{1,0:T(8,128)(2,1)}, u32[]{:S(2)}, u32[]{:S(2)}) collective-permute-start(bf16[256,384]{1,0:T(8,128)(2,1)S(1)} %get-tuple-element.18), channel_id=1, source_target_pairs={{0,2},{1,3},{2,0},{3,1},{4,6},{5,7},{6,4},{7,5},{8,10},{9,11},{10,... | collective-permute-start | bytes 589832 | tf_op jit(solution)/shard_map/ppermute | solution.py:22
  68.7 2.1 %copy-start.8 = (bf16[2,2,512,384]{3,2,1,0:T(8,128)(2,1)}, bf16[2,2,512,384]{3,2,1,0:T(8,128)(2,1)S(1)}, u32[]{:S(2)}) copy-start(bf16[2,2,512,384]{3,2,1,0:T(8,128)(2,1)S(1)} %collective-permute-done.14) | copy-start | bytes 4718596
  69.0 1.8 %copy-start.10 = (bf16[2,2,512,384]{3,2,1,0:T(8,128)(2,1)}, bf16[2,2,512,384]{3,2,1,0:T(8,128)(2,1)S(1)}, u32[]{:S(2)}) copy-start(bf16[2,2,512,384]{3,2,1,0:T(8,128)(2,1)S(1)} %collective-permute-done.13) | copy-start | bytes 4718596
  70.8 28.5 %collective-permute-start.15 = (bf16[2,512,384]{2,1,0:T(8,128)(2,1)}, bf16[2,512,384]{2,1,0:T(8,128)(2,1)}, u32[]{:S(2)}, u32[]{:S(2)}) collective-permute-start(bf16[2,512,384]{2,1,0:T(8,128)(2,1)} %get-tuple-element.14), channel_id=1, source_target_pairs={{0,8},{4,12},{8,16},{12,20},{16,24},{20,28},{24,32},{28,36},{32,40... | collective-permute-start | bytes 2359304 | tf_op jit(solution)/shard_map/ppermute | solution.py:17
  77.0 25.2 %copy-start.7 = (f32[2,512,384]{2,1,0:T(8,128)S(1)}, f32[2,512,384]{2,1,0:T(8,128)}, u32[]{:S(2)}) copy-start(f32[2,512,384]{2,1,0:T(8,128)} %get-tuple-element.11) | copy-start | bytes 4718596
  77.0 25.2 %collective-permute-start.16 = (bf16[2,512,384]{2,1,0:T(8,128)(2,1)}, bf16[2,512,384]{2,1,0:T(8,128)(2,1)}, u32[]{:S(2)}, u32[]{:S(2)}) collective-permute-start(bf16[2,512,384]{2,1,0:T(8,128)(2,1)} %get-tuple-element.15), channel_id=1, source_target_pairs={{8,0},{12,4},{16,8},{20,12},{24,16},{28,20},{32,24},{36,28},{40,32... | collective-permute-start | bytes 2359304 | tf_op jit(solution)/shard_map/ppermute | solution.py:17
  80.2 16.3 %collective-permute-start.9 = (bf16[512,384]{1,0:T(8,128)(2,1)}, bf16[512,384]{1,0:T(8,128)(2,1)}, u32[]{:S(2)}, u32[]{:S(2)}) collective-permute-start(bf16[512,384]{1,0:T(8,128)(2,1)} %convolution_convert_fusion.2), channel_id=1, source_target_pairs={{0,1},{1,2},{2,3},{3,0},{4,5},{5,6},{6,7},{7,4},{8,9},{9,10},{10,1... | collective-permute-start | bytes 1179656 | tf_op jit(solution)/shard_map/ppermute | solution.py:22
  81.3 15.6 %collective-permute-start.10 = (bf16[512,384]{1,0:T(8,128)(2,1)S(1)}, bf16[512,384]{1,0:T(8,128)(2,1)}, u32[]{:S(2)}, u32[]{:S(2)}) collective-permute-start(bf16[512,384]{1,0:T(8,128)(2,1)S(1)} %convolution_convert_fusion.1), channel_id=1, source_target_pairs={{0,3},{1,0},{2,1},{3,2},{4,7},{5,4},{6,5},{7,6},{8,11},{9,8},{10,9... | collective-permute-start | bytes 1179656 | tf_op jit(solution)/shard_map/ppermute | solution.py:22
  82.3 14.3 %collective-permute-start.12 = (bf16[256,384]{1,0:T(8,128)(2,1)}, bf16[256,384]{1,0:T(8,128)(2,1)}, u32[]{:S(2)}, u32[]{:S(2)}) collective-permute-start(bf16[256,384]{1,0:T(8,128)(2,1)} %get-tuple-element.19), channel_id=1, source_target_pairs={{0,2},{1,3},{2,0},{3,1},{4,6},{5,7},{6,4},{7,5},{8,10},{9,11},{10,... | collective-permute-start | bytes 589832 | tf_op jit(solution)/shard_map/ppermute | solution.py:22
  84.7 17.6 %copy-start.9 = (bf16[2,2,512,384]{3,2,1,0:T(8,128)(2,1)S(1)}, bf16[2,2,512,384]{3,2,1,0:T(8,128)(2,1)}, u32[]{:S(2)}) copy-start(bf16[2,2,512,384]{3,2,1,0:T(8,128)(2,1)} %copy-done.8) | copy-start | bytes 4718596

commit v3 on v2

--- a/solution.py
+++ b/solution.py
@@ -190,10 +190,7 @@
     )(sel, queries, keys, values, *cand_args, grad_attn, shot_ids.reshape(rows, 1), shot_ids.reshape(1, rows))
 
 
-def on_device(queries, keys, values, out_weight, cotangent, routes, shot_ids):
-    seq_index = lax.axis_index("seq")
-    parity = seq_index % 2
-    grad_attn = fold_cotangent(cotangent, out_weight)
+def routed_chunk(queries, keys, values, grad_attn, shot_ids, offs, parity):
     own_kv = jnp.stack([keys, values])
     from_left2 = shifted(own_kv, "seq", 2)
     from_right2 = shifted(own_kv, "seq", -2)
@@ -201,13 +198,11 @@
     relay_to_odd = even_to_odd(from_right2, "seq")
     relay_to_even = odd_to_even(from_left2, "seq")
     partner_off = 1 - 2 * parity
-    offs = (routes[seq_index] - seq_index).astype(jnp.int32)
     relay_idx = jnp.where(parity == 1, 2, 3)
     pick = jnp.where(offs == -2, 0, jnp.where(offs == 2, 4, jnp.where(offs == partner_off, 1, relay_idx)))
     sel = jnp.concatenate([pick.astype(jnp.int32), jnp.zeros((1,), jnp.int32), offs])
     cands = (from_left2, partner_own, relay_to_odd, relay_to_even, from_right2)
     attn, grad_q, self_term, near, far = attention(sel, queries, keys, values, cands, grad_attn, shot_ids)
-    attn_out = project_out(attn, out_weight)
     got_a = even_to_odd(near, "seq")
     got_b = odd_to_even(near, "seq")
     up_plus = (far[1].astype(jnp.float32) + got_b[1].astype(jnp.float32)).astype(jnp.bfloat16)
@@ -222,7 +217,25 @@
         + got_from_right.astype(jnp.float32)
     )
     rounded = total.astype(jnp.bfloat16)
-    return (attn_out, grad_q, rounded[0], rounded[1])
+    return attn, grad_q, rounded[0], rounded[1]
+
+
+def on_device(queries, keys, values, out_weight, cotangent, routes, shot_ids):
+    seq_index = lax.axis_index("seq")
+    parity = seq_index % 2
+    columns = queries.shape[1]
+    grad_attn = fold_cotangent(cotangent, out_weight)
+    offs = (routes[seq_index] - seq_index).astype(jnp.int32)
+    bounds = [0, HEAD_DIM, columns] if columns > HEAD_DIM else [0, columns]
+    pieces = []
+    for lo, hi in zip(bounds[:-1], bounds[1:]):
+        pieces.append(routed_chunk(
+            queries[:, lo:hi], keys[:, lo:hi], values[:, lo:hi], grad_attn[:, lo:hi],
+            shot_ids, offs, parity,
+        ))
+    attn, grad_q, grad_keys, grad_values = [jnp.concatenate(p, axis=1) for p in zip(*pieces)]
+    attn_out = project_out(attn, out_weight)
+    return (attn_out, grad_q, grad_keys, grad_values)
 
 
 def solution(mesh):

time: 106 us -> 131 us (1.24)
  the two profiles are of different devices: /device:TPU:126 before, /device:TPU:102 now
where the time goes in v3:
time: 131 us; the launch traced here: 130 us
  starting transfers between devices  65.3 us (50%)
  Pallas kernels  18.3 us (14%)
  local copies, waits for them, and re-layouts  15.6 us (12%)
  waiting for transfers between devices  15.3 us (12%)
  matrix products  7.84 us (6%)
  other arithmetic  6.49 us (5%)
    ppermute x8, starting transfers between devices, shifted(): return lax.ppermute(block, axis, route)  33.4 us
    pallas_call x2, Pallas kernels, attention(): pl.pallas_call(attn_kernel, grid_spec=grid_spec, out_shape=out_shape, com...  18.3 us
    ppermute x4, starting transfers between devices, even_to_odd(): lax.ppermute(block, axis, [(i, i + 1) for i in range(0, size - 1, 2)])  12.7 us
    ppermute x8, starting transfers between devices, ring_shift(): lax.ppermute(block, axis, [(i, (i + distance) % size) for i in range(size)])  12.6 us
    ppermute x8, waiting for transfers between devices, ring_shift(): lax.ppermute(block, axis, [(i, (i + distance) % size) for i in range(size)])  9.03 us
    unnamed x43, local copies, waits for them, and re-layouts  6.75 us
    ppermute x8, waiting for transfers between devices, shifted(): return lax.ppermute(block, axis, route)  6.27 us
    dot_general x4, matrix products, fold_cotangent(): lax.dot_general(piece, w_cols, nt, preferred_element_type=jnp.float32)  5.42 us
  transfers between devices with their start and end apart: 26, of which 3 were waited for; matrix products, arithmetic and copies ran while one was open for 17% of the time, Pallas kernels for 14%

profile of v3, /device:TPU:102, one launch (start us, length us, event | category | flops | bytes accessed | tf_op | source)
XLA Modules:
  0.0 130.1 jit_solution(939466956640982661)
XLA Ops:
  0.7 1.7 %collective-permute-start.5 = (bf16[512,384]{1,0:T(8,128)(2,1)}, bf16[512,384]{1,0:T(8,128)(2,1)}, u32[]{:S(2)}, u32[]{:S(2)}) collective-permute-start(bf16[512,384]{1,0:T(8,128)(2,1)} %param.11), channel_id=1, source_target_pairs={{0,1},{1,2},{2,3},{3,0},{4,5},{5,6},{6,7},{7,4},{8,9},{9,10},{10,1... | collective-permute-start | bytes 1179656 | tf_op jit(solution)/shard_map/ppermute | solution.py:22
  2.3 1.7 %collective-permute-start.6 = (bf16[512,384]{1,0:T(8,128)(2,1)}, bf16[512,384]{1,0:T(8,128)(2,1)}, u32[]{:S(2)}, u32[]{:S(2)}) collective-permute-start(bf16[512,384]{1,0:T(8,128)(2,1)} %param.11), channel_id=1, source_target_pairs={{0,3},{1,0},{2,1},{3,2},{4,7},{5,4},{6,5},{7,6},{8,11},{9,8},{10,9... | collective-permute-start | bytes 1179656 | tf_op jit(solution)/shard_map/ppermute | solution.py:22
  4.0 1.8 %fusion.41 = (bf16[256,384]{1,0:T(8,128)(2,1)}, bf16[256,384]{1,0:T(8,128)(2,1)}) fusion(bf16[512,384]{1,0:T(8,128)(2,1)} %param.11), kind=kLoop, calls=%fused_computation.79 | loop fusion | bytes 786432 | tf_op jit(solution)/shard_map/slice | solution.py:36
  5.8 2.0 %collective-permute-start.7 = (bf16[256,384]{1,0:T(8,128)(2,1)}, bf16[256,384]{1,0:T(8,128)(2,1)}, u32[]{:S(2)}, u32[]{:S(2)}) collective-permute-start(bf16[256,384]{1,0:T(8,128)(2,1)} %get-tuple-element.36), channel_id=1, source_target_pairs={{0,2},{1,3},{2,0},{3,1},{4,6},{5,7},{6,4},{7,5},{8,10},{9,11},{10,... | collective-permute-start | bytes 589832 | tf_op jit(solution)/shard_map/ppermute | solution.py:22
  7.8 1.5 %collective-permute-start.8 = (bf16[256,384]{1,0:T(8,128)(2,1)}, bf16[256,384]{1,0:T(8,128)(2,1)}, u32[]{:S(2)}, u32[]{:S(2)}) collective-permute-start(bf16[256,384]{1,0:T(8,128)(2,1)} %get-tuple-element.37), channel_id=1, source_target_pairs={{0,2},{1,3},{2,0},{3,1},{4,6},{5,7},{6,4},{7,5},{8,10},{9,11},{10,... | collective-permute-start | bytes 589832 | tf_op jit(solution)/shard_map/ppermute | solution.py:22
  9.3 1.7 %slice_bitcast_fusion.8 = (bf16[1,512,128]{2,1,0:T(8,128)(2,1)S(1)}, bf16[512,128]{1,0:T(8,128)(2,1)}, bf16[512,128]{1,0:T(8,128)(2,1)}, bf16[1,512,128]{2,1,0:T(8,128)(2,1)S(1)}) fusion(bf16[512,384]{1,0:T(8,128)(2,1)} %param.9, bf16[512,384]{1,0:T(8,128)(2,1)} %param.8), kind=kLoop, calls=%fused_computation.74 | loop fusion | bytes 786432 | tf_op jit(solution)/shard_map/stack | solution.py:194
  11.1 2.7 %collective-permute-start.2 = (bf16[2,512,128]{2,1,0:T(8,128)(2,1)S(1)}, bf16[2,512,128]{2,1,0:T(8,128)(2,1)}, u32[]{:S(2)}, u32[]{:S(2)}) collective-permute-start(bf16[2,512,128]{2,1,0:T(8,128)(2,1)S(1)} %pad_maximum_fusion.4), channel_id=1, source_target_pairs={{8,0},{12,4},{16,8},{20,12},{24,16},{28,20},{32,24},{36,28},{40,32... | collective-permute-start | bytes 786440 | tf_op jit(solution)/shard_map/ppermute | solution.py:17
  16.0 1.6 %slice.84.q_ref = bf16[512,128]{1,0:T(8,128)(2,1)} slice(bf16[512,384]{1,0:T(8,128)(2,1)} %param.7), slice={[0:512], [0:128]} | slice | bytes 262144 | tf_op jit(solution)/shard_map/slice | solution.py:233
  18.0 1.7 %collective-permute-done.7 = bf16[256,384]{1,0:T(8,128)(2,1)} collective-permute-done((bf16[256,384]{1,0:T(8,128)(2,1)}, bf16[256,384]{1,0:T(8,128)(2,1)}, u32[]{:S(2)}, u32[]{:S(2)}) %collective-permute-start.7) | collective-permute-done | bytes 196640 | tf_op jit(solution)/shard_map/ppermute | solution.py:22
  19.7 4.9 %collective-permute-start = (bf16[2,512,128]{2,1,0:T(8,128)(2,1)S(1)}, bf16[2,512,128]{2,1,0:T(8,128)(2,1)S(1)}, u32[]{:S(2)}, u32[]{:S(2)}) collective-permute-start(bf16[2,512,128]{2,1,0:T(8,128)(2,1)S(1)} %pad_maximum_fusion.4), channel_id=1, source_target_pairs={{0,8},{4,12},{8,16},{12,20},{16,24},{20,28},{24,32},{28,36},{32,40... | collective-permute-start | bytes 786440 | tf_op jit(solution)/shard_map/ppermute | solution.py:17
  24.7 1.9 %collective-permute-start.11 = (bf16[2,512,256]{2,1,0:T(8,128)(2,1)}, bf16[2,512,256]{2,1,0:T(8,128)(2,1)S(1)}, u32[]{:S(2)}, u32[]{:S(2)}) collective-permute-start(bf16[2,512,256]{2,1,0:T(8,128)(2,1)} %pad_maximum_fusion), channel_id=1, source_target_pairs={{8,0},{12,4},{16,8},{20,12},{24,16},{28,20},{32,24},{36,28},{40,32... | collective-permute-start | bytes 1572872 | tf_op jit(solution)/shard_map/ppermute | solution.py:17
  26.6 1.4 %fusion.14 = f32[512,384]{1,0:T(8,128)S(1)} fusion(bf16[256,384]{1,0:T(8,128)(2,1)} %collective-permute-done.8, bf16[256,384]{1,0:T(8,128)(2,1)} %collective-permute-done.7, bf16[384,1536]{1,0:T(8,128)(2,1)S(1)} %copy-done, s32[]{:T(128)S(6)} %select_n.82), kind=kOutput, calls=%fused_computation.31 | convolution fusion | flops 151781376 | bytes 1474564 | tf_op jit(solution)/shard_map/dot_general | solution.py:43
  28.1 7.2 %collective-permute-start.9 = (bf16[2,512,256]{2,1,0:T(8,128)(2,1)}, bf16[2,512,256]{2,1,0:T(8,128)(2,1)S(1)}, u32[]{:S(2)}, u32[]{:S(2)}) collective-permute-start(bf16[2,512,256]{2,1,0:T(8,128)(2,1)} %pad_maximum_fusion), channel_id=1, source_target_pairs={{0,8},{4,12},{8,16},{12,20},{16,24},{20,28},{24,32},{28,36},{32,40... | collective-permute-start | bytes 1572872 | tf_op jit(solution)/shard_map/ppermute | solution.py:17
  35.3 1.4 %convolution_add_fusion.2 = f32[384,512]{0,1:T(8,128)S(1)} fusion(f32[384,512]{0,1:T(8,128)S(1)} %fusion.19, bf16[512,384]{1,0:T(8,128)(2,1)} %collective-permute-done.5, bf16[384,1536]{1,0:T(8,128)(2,1)S(1)} %copy-done, s32[]{:T(128)S(6)} %select_n.78), kind=kOutput, calls=%fused_computation.3 | convolution fusion | flops 151191552 | bytes 2260996 | tf_op jit(solution)/shard_map/dot_general | solution.py:43
  36.9 2.4 %collective-permute-start.3 = (bf16[2,512,128]{2,1,0:T(8,128)(2,1)}, bf16[2,512,128]{2,1,0:T(8,128)(2,1)S(1)}, u32[]{:S(2)}, u32[]{:S(2)}) collective-permute-start(bf16[2,512,128]{2,1,0:T(8,128)(2,1)} %collective-permute-done.2.refs_8_.refs_9_), channel_id=1, source_target_pairs={{0,4},{8,12},{16,20},{24,28},{32,36},{40,44},{48,52},{56,60},{64,6... | collective-permute-start | bytes 786440 | tf_op jit(solution)/shard_map/ppermute | solution.py:81
  39.3 1.3 collective-permute-start.4
  40.6 2.2 %fusion.5 = bf16[512,384]{1,0:T(8,128)(2,1)} fusion(f32[512,384]{1,0:T(8,128)S(1)} %fusion.14, f32[384,512]{0,1:T(8,128)S(1)} %convolution_add_fusion.2, bf16[512,384]{1,0:T(8,128)(2,1)} %collective-permute-done.6, bf16[384,1536]{1,0:T(8,128)(2,1)S(1)} %copy-done, s32[]{:T(128)S(6)} %select_n.80), kind=kOutput, calls=%fused_computation.8 | convolution fusion | flops 151584768 | bytes 2654212 | tf_op jit(solution)/shard_map/dot_general | solution.py:43
  44.9 2.0 %collective-permute-start.12 = (bf16[2,512,256]{2,1,0:T(8,128)(2,1)S(1)}, bf16[2,512,256]{2,1,0:T(8,128)(2,1)S(1)}, u32[]{:S(2)}, u32[]{:S(2)}) collective-permute-start(bf16[2,512,256]{2,1,0:T(8,128)(2,1)S(1)} %collective-permute-done.11.refs_8_.refs_9_), channel_id=1, source_target_pairs={{0,4},{8,12},{16,20},{24,28},{32,36},{40,44},{48,52},{56,60},{64,6... | collective-permute-start | bytes 1572872 | tf_op jit(solution)/shard_map/ppermute | solution.py:81
  46.9 1.3 collective-permute-start.13
  48.2 6.6 %shard_map.102 = (bf16[512,128]{1,0:T(8,128)(2,1)S(1)}, bf16[512,128]{1,0:T(8,128)(2,1)S(1)}, f32[2,512,128]{2,1,0:T(8,128)S(1)}, bf16[2,2,512,128]{3,2,1,0:T(8,128)(2,1)}, bf16[2,2,512,128]{3,2,1,0:T(8,128)(2,1)S(1)}) custom-call(s32[5]{0:T(128)S(1)} %pad_add_fusion.sel_ref, bf16[512,128]{1,0:T(8,128)(2,1)S(1)} %copy-done.8, ...), custom_call_target="tpu_custom_call" | custom-call | tf_op jit(solution)/shard_map/pallas_call | solution.py:184
  57.8 4.6 %collective-permute-start.18 = (bf16[2,2,512,128]{3,2,1,0:T(8,128)(2,1)}, bf16[2,2,512,128]{3,2,1,0:T(8,128)(2,1)}, u32[]{:S(2)}, u32[]{:S(2)}) collective-permute-start(bf16[2,2,512,128]{3,2,1,0:T(8,128)(2,1)} %get-tuple-element.19), channel_id=1, source_target_pairs={{0,4},{8,12},{16,20},{24,28},{32,36},{40,44},{48,52},{56,60},{64,6... | collective-permute-start | bytes 1572872 | tf_op jit(solution)/shard_map/ppermute | solution.py:81
  62.4 1.5 %collective-permute-start.19 = (bf16[2,2,512,128]{3,2,1,0:T(8,128)(2,1)}, bf16[2,2,512,128]{3,2,1,0:T(8,128)(2,1)}, u32[]{:S(2)}, u32[]{:S(2)}) collective-permute-start(bf16[2,2,512,128]{3,2,1,0:T(8,128)(2,1)} %get-tuple-element.19), channel_id=1, source_target_pairs={{4,0},{12,8},{20,16},{28,24},{36,32},{44,40},{52,48},{60,56},{68,6... | collective-permute-start | bytes 1572872 | tf_op jit(solution)/shard_map/ppermute | solution.py:86
  69.4 11.7 %shard_map.103 = (bf16[512,256]{1,0:T(8,128)(2,1)S(1)}, bf16[512,256]{1,0:T(8,128)(2,1)S(1)}, f32[2,512,256]{2,1,0:T(8,128)S(1)}, bf16[2,2,512,256]{3,2,1,0:T(8,128)(2,1)}, bf16[2,2,512,256]{3,2,1,0:T(8,128)(2,1)}) custom-call(s32[5]{0:T(128)S(1)} %pad_add_fusion.sel_ref, bf16[512,256]{1,0:T(8,128)(2,1)S(1)} %copy-done.1, bf16[512,256]{1,0:T(8,128)(2,1)S(1)} %copy-done.3, ...), custom_call_target="tpu_custom_call" | custom-call | tf_op jit(solution)/shard_map/pallas_call | solution.py:184
  81.0 3.7 %collective-permute-start.22 = (bf16[2,2,512,256]{3,2,1,0:T(8,128)(2,1)}, bf16[2,2,512,256]{3,2,1,0:T(8,128)(2,1)S(1)}, u32[]{:S(2)}, u32[]{:S(2)}) collective-permute-start(bf16[2,2,512,256]{3,2,1,0:T(8,128)(2,1)} %get-tuple-element.22), channel_id=1, source_target_pairs={{0,4},{8,12},{16,20},{24,28},{32,36},{40,44},{48,52},{56,60},{64,6... | collective-permute-start | bytes 3145736 | tf_op jit(solution)/shard_map/ppermute | solution.py:81
  87.3 5.5 %collective-permute-start.20 = (bf16[2,512,128]{2,1,0:T(8,128)(2,1)S(1)}, bf16[2,512,128]{2,1,0:T(8,128)(2,1)S(1)}, u32[]{:S(2)}, u32[]{:S(2)}) collective-permute-start(bf16[2,512,128]{2,1,0:T(8,128)(2,1)S(1)} %get-tuple-element.28), channel_id=1, source_target_pairs={{0,8},{4,12},{8,16},{12,20},{16,24},{20,28},{24,32},{28,36},{32,40... | collective-permute-start | bytes 786440 | tf_op jit(solution)/shard_map/ppermute | solution.py:17
  92.7 1.9 %collective-permute-start.21 = (bf16[2,512,128]{2,1,0:T(8,128)(2,1)S(1)}, bf16[2,512,128]{2,1,0:T(8,128)(2,1)S(1)}, u32[]{:S(2)}, u32[]{:S(2)}) collective-permute-start(bf16[2,512,128]{2,1,0:T(8,128)(2,1)S(1)} %get-tuple-element.29), channel_id=1, source_target_pairs={{8,0},{12,4},{16,8},{20,12},{24,16},{28,20},{32,24},{36,28},{40,32... | collective-permute-start | bytes 786440 | tf_op jit(solution)/shard_map/ppermute | solution.py:17
  95.2 1.9 %collective-permute-start.16 = (bf16[256,384]{1,0:T(8,128)(2,1)S(1)}, bf16[256,384]{1,0:T(8,128)(2,1)S(1)}, u32[]{:S(2)}, u32[]{:S(2)}) collective-permute-start(bf16[256,384]{1,0:T(8,128)(2,1)S(1)} %get-tuple-element.30), channel_id=1, source_target_pairs={{0,2},{1,3},{2,0},{3,1},{4,6},{5,7},{6,4},{7,5},{8,10},{9,11},{10,... | collective-permute-start | bytes 589832 | tf_op jit(solution)/shard_map/ppermute | solution.py:22
  99.4 2.6 %collective-permute-start.15 = (bf16[512,384]{1,0:T(8,128)(2,1)S(1)}, bf16[512,384]{1,0:T(8,128)(2,1)S(1)}, u32[]{:S(2)}, u32[]{:S(2)}) collective-permute-start(bf16[512,384]{1,0:T(8,128)(2,1)S(1)} %convolution_convert_fusion.1), channel_id=1, source_target_pairs={{0,3},{1,0},{2,1},{3,2},{4,7},{5,4},{6,5},{7,6},{8,11},{9,8},{10,9... | collective-permute-start | bytes 1179656 | tf_op jit(solution)/shard_map/ppermute | solution.py:22
  102.3 7.2 %collective-permute-start.24 = (bf16[2,512,256]{2,1,0:T(8,128)(2,1)S(1)}, bf16[2,512,256]{2,1,0:T(8,128)(2,1)S(1)}, u32[]{:S(2)}, u32[]{:S(2)}) collective-permute-start(bf16[2,512,256]{2,1,0:T(8,128)(2,1)S(1)} %get-tuple-element.24), channel_id=1, source_target_pairs={{0,8},{4,12},{8,16},{12,20},{16,24},{20,28},{24,32},{28,36},{32,40... | collective-permute-start | bytes 1572872 | tf_op jit(solution)/shard_map/ppermute | solution.py:17
  109.6 1.9 %collective-permute-start.25 = (bf16[2,512,256]{2,1,0:T(8,128)(2,1)S(1)}, bf16[2,512,256]{2,1,0:T(8,128)(2,1)S(1)}, u32[]{:S(2)}, u32[]{:S(2)}) collective-permute-start(bf16[2,512,256]{2,1,0:T(8,128)(2,1)S(1)} %get-tuple-element.25), channel_id=1, source_target_pairs={{8,0},{12,4},{16,8},{20,12},{24,16},{28,20},{32,24},{36,28},{40,32... | collective-permute-start | bytes 1572872 | tf_op jit(solution)/shard_map/ppermute | solution.py:17
  113.3 7.3 %collective-permute-done.17 = bf16[256,384]{1,0:T(8,128)(2,1)S(1)} collective-permute-done((bf16[256,384]{1,0:T(8,128)(2,1)S(1)}, bf16[256,384]{1,0:T(8,128)(2,1)S(1)}, u32[]{:S(2)}, u32[]{:S(2)}) %collective-permute-start.17) | collective-permute-done | bytes 196640 | tf_op jit(solution)/shard_map/ppermute | solution.py:22
  121.9 6.2 %collective-permute-done.25 = bf16[2,512,256]{2,1,0:T(8,128)(2,1)S(1)} collective-permute-done((bf16[2,512,256]{2,1,0:T(8,128)(2,1)S(1)}, bf16[2,512,256]{2,1,0:T(8,128)(2,1)S(1)}, u32[]{:S(2)}, u32[]{:S(2)}) %collective-permute-start.25) | collective-permute-done | bytes 524320 | tf_op jit(solution)/shard_map/ppermute | solution.py:17
  (97 shorter events, 23.8 us)
Async XLA Ops:
  0.6 17.0 %copy-start = (bf16[384,1536]{1,0:T(8,128)(2,1)S(1)}, bf16[384,1536]{1,0:T(8,128)(2,1)}, u32[]{:S(2)}) copy-start(bf16[384,1536]{1,0:T(8,128)(2,1)} %param.10) | copy-start | bytes 3538948
  0.6 13.2 %copy-start.19 = (bf16[512,384]{1,0:T(8,128)(2,1)S(1)}, bf16[512,384]{1,0:T(8,128)(2,1)}, u32[]{:S(2)}) copy-start(bf16[512,384]{1,0:T(8,128)(2,1)} %param.8) | copy-start | bytes 1179652
  0.7 13.2 %copy-start.18 = (bf16[512,384]{1,0:T(8,128)(2,1)S(1)}, bf16[512,384]{1,0:T(8,128)(2,1)}, u32[]{:S(2)}) copy-start(bf16[512,384]{1,0:T(8,128)(2,1)} %param.9) | copy-start | bytes 1179652
  0.7 27.4 %collective-permute-start.5 = (bf16[512,384]{1,0:T(8,128)(2,1)}, bf16[512,384]{1,0:T(8,128)(2,1)}, u32[]{:S(2)}, u32[]{:S(2)}) collective-permute-start(bf16[512,384]{1,0:T(8,128)(2,1)} %param.11), channel_id=1, source_target_pairs={{0,1},{1,2},{2,3},{3,0},{4,5},{5,6},{6,7},{7,4},{8,9},{9,10},{10,1... | collective-permute-start | bytes 1179656 | tf_op jit(solution)/shard_map/ppermute | solution.py:22
  2.3 37.0 %collective-permute-start.6 = (bf16[512,384]{1,0:T(8,128)(2,1)}, bf16[512,384]{1,0:T(8,128)(2,1)}, u32[]{:S(2)}, u32[]{:S(2)}) collective-permute-start(bf16[512,384]{1,0:T(8,128)(2,1)} %param.11), channel_id=1, source_target_pairs={{0,3},{1,0},{2,1},{3,2},{4,7},{5,4},{6,5},{7,6},{8,11},{9,8},{10,9... | collective-permute-start | bytes 1179656 | tf_op jit(solution)/shard_map/ppermute | solution.py:22
  5.8 13.9 %collective-permute-start.7 = (bf16[256,384]{1,0:T(8,128)(2,1)}, bf16[256,384]{1,0:T(8,128)(2,1)}, u32[]{:S(2)}, u32[]{:S(2)}) collective-permute-start(bf16[256,384]{1,0:T(8,128)(2,1)} %get-tuple-element.36), channel_id=1, source_target_pairs={{0,2},{1,3},{2,0},{3,1},{4,6},{5,7},{6,4},{7,5},{8,10},{9,11},{10,... | collective-permute-start | bytes 589832 | tf_op jit(solution)/shard_map/ppermute | solution.py:22
  7.8 16.9 %collective-permute-start.8 = (bf16[256,384]{1,0:T(8,128)(2,1)}, bf16[256,384]{1,0:T(8,128)(2,1)}, u32[]{:S(2)}, u32[]{:S(2)}) collective-permute-start(bf16[256,384]{1,0:T(8,128)(2,1)} %get-tuple-element.37), channel_id=1, source_target_pairs={{0,2},{1,3},{2,0},{3,1},{4,6},{5,7},{6,4},{7,5},{8,10},{9,11},{10,... | collective-permute-start | bytes 589832 | tf_op jit(solution)/shard_map/ppermute | solution.py:22
  11.1 25.7 %collective-permute-start.2 = (bf16[2,512,128]{2,1,0:T(8,128)(2,1)S(1)}, bf16[2,512,128]{2,1,0:T(8,128)(2,1)}, u32[]{:S(2)}, u32[]{:S(2)}) collective-permute-start(bf16[2,512,128]{2,1,0:T(8,128)(2,1)S(1)} %pad_maximum_fusion.4), channel_id=1, source_target_pairs={{8,0},{12,4},{16,8},{20,12},{24,16},{28,20},{32,24},{36,28},{40,32... | collective-permute-start | bytes 786440 | tf_op jit(solution)/shard_map/ppermute | solution.py:17
  19.7 17.1 %collective-permute-start = (bf16[2,512,128]{2,1,0:T(8,128)(2,1)S(1)}, bf16[2,512,128]{2,1,0:T(8,128)(2,1)S(1)}, u32[]{:S(2)}, u32[]{:S(2)}) collective-permute-start(bf16[2,512,128]{2,1,0:T(8,128)(2,1)S(1)} %pad_maximum_fusion.4), channel_id=1, source_target_pairs={{0,8},{4,12},{8,16},{12,20},{16,24},{20,28},{24,32},{28,36},{32,40... | collective-permute-start | bytes 786440 | tf_op jit(solution)/shard_map/ppermute | solution.py:17
  24.7 20.2 %collective-permute-start.11 = (bf16[2,512,256]{2,1,0:T(8,128)(2,1)}, bf16[2,512,256]{2,1,0:T(8,128)(2,1)S(1)}, u32[]{:S(2)}, u32[]{:S(2)}) collective-permute-start(bf16[2,512,256]{2,1,0:T(8,128)(2,1)} %pad_maximum_fusion), channel_id=1, source_target_pairs={{8,0},{12,4},{16,8},{20,12},{24,16},{28,20},{32,24},{36,28},{40,32... | collective-permute-start | bytes 1572872 | tf_op jit(solution)/shard_map/ppermute | solution.py:17
  28.1 18.8 %collective-permute-start.9 = (bf16[2,512,256]{2,1,0:T(8,128)(2,1)}, bf16[2,512,256]{2,1,0:T(8,128)(2,1)S(1)}, u32[]{:S(2)}, u32[]{:S(2)}) collective-permute-start(bf16[2,512,256]{2,1,0:T(8,128)(2,1)} %pad_maximum_fusion), channel_id=1, source_target_pairs={{0,8},{4,12},{8,16},{12,20},{16,24},{20,28},{24,32},{28,36},{32,40... | collective-permute-start | bytes 1572872 | tf_op jit(solution)/shard_map/ppermute | solution.py:17
  36.7 11.5 %copy-start.8 = (bf16[512,128]{1,0:T(8,128)(2,1)S(1)}, bf16[512,128]{1,0:T(8,128)(2,1)}, u32[]{:S(2)}) copy-start(bf16[512,128]{1,0:T(8,128)(2,1)} %slice.84.q_ref) | copy-start | bytes 393220
  36.8 6.9 %collective-permute-start.1 = (bf16[2,512,128]{2,1,0:T(8,128)(2,1)S(1)}, bf16[2,512,128]{2,1,0:T(8,128)(2,1)S(1)}, u32[]{:S(2)}, u32[]{:S(2)}) collective-permute-start(bf16[2,512,128]{2,1,0:T(8,128)(2,1)S(1)} %pad_maximum_fusion.4), channel_id=1, source_target_pairs={{0,4},{4,0},{8,12},{12,8},{16,20},{20,16},{24,28},{28,24},{32,36},... | collective-permute-start | bytes 786440 | tf_op jit(solution)/shard_map/ppermute | solution.py:76
  36.9 11.3 %collective-permute-start.3 = (bf16[2,512,128]{2,1,0:T(8,128)(2,1)}, bf16[2,512,128]{2,1,0:T(8,128)(2,1)S(1)}, u32[]{:S(2)}, u32[]{:S(2)}) collective-permute-start(bf16[2,512,128]{2,1,0:T(8,128)(2,1)} %collective-permute-done.2.refs_8_.refs_9_), channel_id=1, source_target_pairs={{0,4},{8,12},{16,20},{24,28},{32,36},{40,44},{48,52},{56,60},{64,6... | collective-permute-start | bytes 786440 | tf_op jit(solution)/shard_map/ppermute | solution.py:81
  39.3 8.9 %collective-permute-start.4 = (bf16[2,512,128]{2,1,0:T(8,128)(2,1)S(1)}, bf16[2,512,128]{2,1,0:T(8,128)(2,1)S(1)}, u32[]{:S(2)}, u32[]{:S(2)}) collective-permute-start(bf16[2,512,128]{2,1,0:T(8,128)(2,1)S(1)} %collective-permute-done.refs_0_.refs_1_), channel_id=1, source_target_pairs={{4,0},{12,8},{20,16},{28,24},{36,32},{44,40},{52,48},{60,56},{68,6... | collective-permute-start | bytes 786440 | tf_op jit(solution)/shard_map/ppermute | solution.py:86
  43.7 22.8 %collective-permute-start.10 = (bf16[2,512,256]{2,1,0:T(8,128)(2,1)}, bf16[2,512,256]{2,1,0:T(8,128)(2,1)S(1)}, u32[]{:S(2)}, u32[]{:S(2)}) collective-permute-start(bf16[2,512,256]{2,1,0:T(8,128)(2,1)} %pad_maximum_fusion), channel_id=1, source_target_pairs={{0,4},{4,0},{8,12},{12,8},{16,20},{20,16},{24,28},{28,24},{32,36},... | collective-permute-start | bytes 1572872 | tf_op jit(solution)/shard_map/ppermute | solution.py:76
  44.9 21.6 %collective-permute-start.12 = (bf16[2,512,256]{2,1,0:T(8,128)(2,1)S(1)}, bf16[2,512,256]{2,1,0:T(8,128)(2,1)S(1)}, u32[]{:S(2)}, u32[]{:S(2)}) collective-permute-start(bf16[2,512,256]{2,1,0:T(8,128)(2,1)S(1)} %collective-permute-done.11.refs_8_.refs_9_), channel_id=1, source_target_pairs={{0,4},{8,12},{16,20},{24,28},{32,36},{40,44},{48,52},{56,60},{64,6... | collective-permute-start | bytes 1572872 | tf_op jit(solution)/shard_map/ppermute | solution.py:81
  46.9 19.6 %collective-permute-start.13 = (bf16[2,512,256]{2,1,0:T(8,128)(2,1)S(1)}, bf16[2,512,256]{2,1,0:T(8,128)(2,1)}, u32[]{:S(2)}, u32[]{:S(2)}) collective-permute-start(bf16[2,512,256]{2,1,0:T(8,128)(2,1)S(1)} %collective-permute-done.9.refs_0_.refs_1_), channel_id=1, source_target_pairs={{4,0},{12,8},{20,16},{28,24},{36,32},{44,40},{52,48},{60,56},{68,6... | collective-permute-start | bytes 1572872 | tf_op jit(solution)/shard_map/ppermute | solution.py:86
  48.2 15.6 %copy-start.17 = (bf16[512,384]{1,0:T(8,128)(2,1)S(1)}, bf16[512,384]{1,0:T(8,128)(2,1)}, u32[]{:S(2)}) copy-start(bf16[512,384]{1,0:T(8,128)(2,1)} %param.7) | copy-start | bytes 1179652
  57.8 28.3 %collective-permute-start.18 = (bf16[2,2,512,128]{3,2,1,0:T(8,128)(2,1)}, bf16[2,2,512,128]{3,2,1,0:T(8,128)(2,1)}, u32[]{:S(2)}, u32[]{:S(2)}) collective-permute-start(bf16[2,2,512,128]{3,2,1,0:T(8,128)(2,1)} %get-tuple-element.19), channel_id=1, source_target_pairs={{0,4},{8,12},{16,20},{24,28},{32,36},{40,44},{48,52},{56,60},{64,6... | collective-permute-start | bytes 1572872 | tf_op jit(solution)/shard_map/ppermute | solution.py:81
  62.4 23.7 %collective-permute-start.19 = (bf16[2,2,512,128]{3,2,1,0:T(8,128)(2,1)}, bf16[2,2,512,128]{3,2,1,0:T(8,128)(2,1)}, u32[]{:S(2)}, u32[]{:S(2)}) collective-permute-start(bf16[2,2,512,128]{3,2,1,0:T(8,128)(2,1)} %get-tuple-element.19), channel_id=1, source_target_pairs={{4,0},{12,8},{20,16},{28,24},{36,32},{44,40},{52,48},{60,56},{68,6... | collective-permute-start | bytes 1572872 | tf_op jit(solution)/shard_map/ppermute | solution.py:86
  69.4 16.7 %copy-start.7 = (bf16[2,2,512,128]{3,2,1,0:T(8,128)(2,1)S(1)}, bf16[2,2,512,128]{3,2,1,0:T(8,128)(2,1)}, u32[]{:S(2)}) copy-start(bf16[2,2,512,128]{3,2,1,0:T(8,128)(2,1)} %copy-done.6) | copy-start | bytes 1572868
  81.0 17.6 %collective-permute-start.22 = (bf16[2,2,512,256]{3,2,1,0:T(8,128)(2,1)}, bf16[2,2,512,256]{3,2,1,0:T(8,128)(2,1)S(1)}, u32[]{:S(2)}, u32[]{:S(2)}) collective-permute-start(bf16[2,2,512,256]{3,2,1,0:T(8,128)(2,1)} %get-tuple-element.22), channel_id=1, source_target_pairs={{0,4},{8,12},{16,20},{24,28},{32,36},{40,44},{48,52},{56,60},{64,6... | collective-permute-start | bytes 3145736 | tf_op jit(solution)/shard_map/ppermute | solution.py:81
  84.7 14.7 %collective-permute-start.23 = (bf16[2,2,512,256]{3,2,1,0:T(8,128)(2,1)}, bf16[2,2,512,256]{3,2,1,0:T(8,128)(2,1)S(1)}, u32[]{:S(2)}, u32[]{:S(2)}) collective-permute-start(bf16[2,2,512,256]{3,2,1,0:T(8,128)(2,1)} %get-tuple-element.22), channel_id=1, source_target_pairs={{4,0},{12,8},{20,16},{28,24},{36,32},{44,40},{52,48},{60,56},{68,6... | collective-permute-start | bytes 3145736 | tf_op jit(solution)/shard_map/ppermute | solution.py:86
  87.3 15.0 %collective-permute-start.20 = (bf16[2,512,128]{2,1,0:T(8,128)(2,1)S(1)}, bf16[2,512,128]{2,1,0:T(8,128)(2,1)S(1)}, u32[]{:S(2)}, u32[]{:S(2)}) collective-permute-start(bf16[2,512,128]{2,1,0:T(8,128)(2,1)S(1)} %get-tuple-element.28), channel_id=1, source_target_pairs={{0,8},{4,12},{8,16},{12,20},{16,24},{20,28},{24,32},{28,36},{32,40... | collective-permute-start | bytes 786440 | tf_op jit(solution)/shard_map/ppermute | solution.py:17
  92.7 16.8 %collective-permute-start.21 = (bf16[2,512,128]{2,1,0:T(8,128)(2,1)S(1)}, bf16[2,512,128]{2,1,0:T(8,128)(2,1)S(1)}, u32[]{:S(2)}, u32[]{:S(2)}) collective-permute-start(bf16[2,512,128]{2,1,0:T(8,128)(2,1)S(1)} %get-tuple-element.29), channel_id=1, source_target_pairs={{8,0},{12,4},{16,8},{20,12},{24,16},{28,20},{32,24},{36,28},{40,32... | collective-permute-start | bytes 786440 | tf_op jit(solution)/shard_map/ppermute | solution.py:17
  95.2 17.5 %collective-permute-start.16 = (bf16[256,384]{1,0:T(8,128)(2,1)S(1)}, bf16[256,384]{1,0:T(8,128)(2,1)S(1)}, u32[]{:S(2)}, u32[]{:S(2)}) collective-permute-start(bf16[256,384]{1,0:T(8,128)(2,1)S(1)} %get-tuple-element.30), channel_id=1, source_target_pairs={{0,2},{1,3},{2,0},{3,1},{4,6},{5,7},{6,4},{7,5},{8,10},{9,11},{10,... | collective-permute-start | bytes 589832 | tf_op jit(solution)/shard_map/ppermute | solution.py:22
  98.7 21.9 %collective-permute-start.14 = (bf16[512,384]{1,0:T(8,128)(2,1)S(1)}, bf16[512,384]{1,0:T(8,128)(2,1)S(1)}, u32[]{:S(2)}, u32[]{:S(2)}) collective-permute-start(bf16[512,384]{1,0:T(8,128)(2,1)S(1)} %convolution_convert_fusion.2), channel_id=1, source_target_pairs={{0,1},{1,2},{2,3},{3,0},{4,5},{5,6},{6,7},{7,4},{8,9},{9,10},{10,1... | collective-permute-start | bytes 1179656 | tf_op jit(solution)/shard_map/ppermute | solution.py:22
  99.4 21.2 %collective-permute-start.15 = (bf16[512,384]{1,0:T(8,128)(2,1)S(1)}, bf16[512,384]{1,0:T(8,128)(2,1)S(1)}, u32[]{:S(2)}, u32[]{:S(2)}) collective-permute-start(bf16[512,384]{1,0:T(8,128)(2,1)S(1)} %convolution_convert_fusion.1), channel_id=1, source_target_pairs={{0,3},{1,0},{2,1},{3,2},{4,7},{5,4},{6,5},{7,6},{8,11},{9,8},{10,9... | collective-permute-start | bytes 1179656 | tf_op jit(solution)/shard_map/ppermute | solution.py:22
  102.3 19.6 %collective-permute-start.24 = (bf16[2,512,256]{2,1,0:T(8,128)(2,1)S(1)}, bf16[2,512,256]{2,1,0:T(8,128)(2,1)S(1)}, u32[]{:S(2)}, u32[]{:S(2)}) collective-permute-start(bf16[2,512,256]{2,1,0:T(8,128)(2,1)S(1)} %get-tuple-element.24), channel_id=1, source_target_pairs={{0,8},{4,12},{8,16},{12,20},{16,24},{20,28},{24,32},{28,36},{32,40... | collective-permute-start | bytes 1572872 | tf_op jit(solution)/shard_map/ppermute | solution.py:17
  109.6 18.6 %collective-permute-start.25 = (bf16[2,512,256]{2,1,0:T(8,128)(2,1)S(1)}, bf16[2,512,256]{2,1,0:T(8,128)(2,1)S(1)}, u32[]{:S(2)}, u32[]{:S(2)}) collective-permute-start(bf16[2,512,256]{2,1,0:T(8,128)(2,1)S(1)} %get-tuple-element.25), channel_id=1, source_target_pairs={{8,0},{12,4},{16,8},{20,12},{24,16},{28,20},{32,24},{36,28},{40,32... | collective-permute-start | bytes 1572872 | tf_op jit(solution)/shard_map/ppermute | solution.py:17
  112.7 7.9 %collective-permute-start.17 = (bf16[256,384]{1,0:T(8,128)(2,1)S(1)}, bf16[256,384]{1,0:T(8,128)(2,1)S(1)}, u32[]{:S(2)}, u32[]{:S(2)}) collective-permute-start(bf16[256,384]{1,0:T(8,128)(2,1)S(1)} %get-tuple-element.31), channel_id=1, source_target_pairs={{0,2},{1,3},{2,0},{3,1},{4,6},{5,7},{6,4},{7,5},{8,10},{9,11},{10,... | collective-permute-start | bytes 589832 | tf_op jit(solution)/shard_map/ppermute | solution.py:22
  (15 other events, 53.3 us)

commit v4 on v2

--- a/solution.py
+++ b/solution.py
@@ -29,13 +29,10 @@
 def fold_cotangent(cotangent, out_weight):
     groups = lax.axis_size("head")
     me = lax.axis_index("head")
-    rows, width = cotangent.shape
-    half = rows // 2
+    _, width = cotangent.shape
     from_prev = ring_shift(cotangent, "head", 1)
     from_next = ring_shift(cotangent, "head", -1)
-    far_a = ring_shift(cotangent[:half], "head", 2)
-    far_b = ring_shift(cotangent[half:], "head", -2)
-    far = jnp.concatenate([far_a, far_b], axis=0)
+    far = ring_shift(cotangent, "head", 2)
     nt = (((1,), (1,)), ((), ()))
     acc = None
     for piece, group in ((cotangent, me), (from_prev, me - 1), (from_next, me + 1), (far, me + 2)):
@@ -48,8 +45,7 @@
 def project_out(attn, out_weight):
     groups = lax.axis_size("head")
     me = lax.axis_index("head")
-    rows, width = attn.shape
-    half = rows // 2
+    _, width = attn.shape
 
     def part(group):
         w_cols = head_slice(out_weight, group % groups, width)
@@ -58,15 +54,14 @@
     far = part(me + 2)
     near_up = part(me + 1)
     near_down = part(me - 1)
-    got_a = ring_shift(far[:half], "head", 2)
-    got_b = ring_shift(far[half:], "head", -2)
+    got_far = ring_shift(far, "head", 2)
     from_prev = ring_shift(near_up, "head", 1)
     from_next = ring_shift(near_down, "head", -1)
     total = (
         jnp.dot(attn, head_slice(out_weight, me, width), preferred_element_type=jnp.float32)
         + from_prev.astype(jnp.float32)
         + from_next.astype(jnp.float32)
-        + jnp.concatenate([got_a, got_b], axis=0).astype(jnp.float32)
+        + got_far.astype(jnp.float32)
     )
     return total.astype(jnp.bfloat16)
 

time: 106 us -> 101 us (0.953)
  starting transfers between devices: 37.1 us -> 33.6 us
  waiting for transfers between devices: 33.1 us -> 30.3 us
  matrix products: 8.97 us -> 11.4 us
  local copies, waits for them, and re-layouts: 2.66 us -> 1.16 us
    ppermute x4, waiting for transfers between devices: 7.76 us -> 1.38 us  [shifted(): return lax.ppermute(block, axis, route)]
    ppermute x8 -> x6, starting transfers between devices: 12.3 us -> 8.14 us  [ring_shift(): lax.ppermute(block, axis, [(i, (i + distance) % size) for i in range(size)])]
    ppermute x8 -> x6, waiting for transfers between devices: 25.1 us -> 28 us  [ring_shift(): lax.ppermute(block, axis, [(i, (i + distance) % size) for i in range(size)])]
    dot_general x3, matrix products: 1.94 us -> 3.44 us  [part(): jnp.dot(attn, w_cols, preferred_element_type=jnp.float32)]
    slice x2 -> x0, local copies, waits for them, and re-layouts: 1.5 us -> none  [the longest x1 0.78 us: fold_cotangent(): far_a = ring_shift(cotangent[:half], 'head', 2)]
  transfers between devices with their start and end apart: 17 -> 15, of which waited for: 7 -> 6; matrix products, arithmetic and copies ran while one was open for 12% -> 12% of each run, Pallas kernels for 0% -> 0%
where the time goes in v4:
time: 101 us; the launch traced here: 99.7 us
  starting transfers between devices  33.6 us (33%)
  waiting for transfers between devices  30.3 us (30%)
  Pallas kernels  16.1 us (16%)
  matrix products  11.4 us (11%)
  other arithmetic  6.16 us (6%)
  local copies, waits for them, and re-layouts  1.16 us (1%)
    ppermute x6, waiting for transfers between devices, ring_shift(): lax.ppermute(block, axis, [(i, (i + distance) % size) for i in range(size)])  28 us
    ppermute x4, starting transfers between devices, shifted(): return lax.ppermute(block, axis, route)  18.2 us
    pallas_call x1, Pallas kernels, attention(): pl.pallas_call(attn_kernel, grid_spec=grid_spec, out_shape=out_shape, com...  16.1 us
    ppermute x6, starting transfers between devices, ring_shift(): lax.ppermute(block, axis, [(i, (i + distance) % size) for i in range(size)])  8.14 us
    dot_general x4, matrix products, fold_cotangent(): lax.dot_general(piece, w_cols, nt, preferred_element_type=jnp.float32)  5.63 us
    ppermute x2, starting transfers between devices, even_to_odd(): lax.ppermute(block, axis, [(i, i + 1) for i in range(0, size - 1, 2)])  4.55 us
    dot_general x3, matrix products, part(): jnp.dot(attn, w_cols, preferred_element_type=jnp.float32)  3.44 us
    ppermute x2, starting transfers between devices, odd_to_even(): return lax.ppermute(block, axis, [(i, i - 1) for i in range(1, size, 2)])  2.7 us
  transfers between devices with their start and end apart: 15, of which 6 were waited for; matrix products, arithmetic and copies ran while one was open for 12% of the time, Pallas kernels for 0%

profile of v4, /device:TPU:126, one launch (start us, length us, event | category | flops | bytes accessed | tf_op | source)
XLA Modules:
  0.0 99.7 jit_solution(17162469812839436009)
XLA Ops:
  0.7 2.2 %pad_maximum_fusion = bf16[2,512,384]{2,1,0:T(8,128)(2,1)} fusion(bf16[1,512,384]{2,1,0:T(8,128)(2,1)} %bitcast.33, bf16[1,512,384]{2,1,0:T(8,128)(2,1)} %bitcast.32), kind=kLoop, calls=%fused_computation.23 | loop fusion | flops 393216 | bytes 1572864 | tf_op jit(solution)/shard_map/stack | solution.py:192
  2.8 2.7 %collective-permute-start.2 = (bf16[2,512,384]{2,1,0:T(8,128)(2,1)}, bf16[2,512,384]{2,1,0:T(8,128)(2,1)S(1)}, u32[]{:S(2)}, u32[]{:S(2)}) collective-permute-start(bf16[2,512,384]{2,1,0:T(8,128)(2,1)} %pad_maximum_fusion), channel_id=1, source_target_pairs={{8,0},{12,4},{16,8},{20,12},{24,16},{28,20},{32,24},{36,28},{40,32... | collective-permute-start | bytes 2359304 | tf_op jit(solution)/shard_map/ppermute | solution.py:17
  5.6 6.4 %collective-permute-start = (bf16[2,512,384]{2,1,0:T(8,128)(2,1)}, bf16[2,512,384]{2,1,0:T(8,128)(2,1)S(1)}, u32[]{:S(2)}, u32[]{:S(2)}) collective-permute-start(bf16[2,512,384]{2,1,0:T(8,128)(2,1)} %pad_maximum_fusion), channel_id=1, source_target_pairs={{0,8},{4,12},{8,16},{12,20},{16,24},{20,28},{24,32},{28,36},{32,40... | collective-permute-start | bytes 2359304 | tf_op jit(solution)/shard_map/ppermute | solution.py:17
  12.0 0.3 collective-permute-start.5
  12.3 2.6 %collective-permute-start.7 = (bf16[512,384]{1,0:T(8,128)(2,1)}, bf16[512,384]{1,0:T(8,128)(2,1)}, u32[]{:S(2)}, u32[]{:S(2)}) collective-permute-start(bf16[512,384]{1,0:T(8,128)(2,1)} %param.11), channel_id=1, source_target_pairs={{0,2},{1,3},{2,0},{3,1},{4,6},{5,7},{6,4},{7,5},{8,10},{9,11},{10,... | collective-permute-start | bytes 1179656 | tf_op jit(solution)/shard_map/ppermute | solution.py:22
  14.9 2.4 %fusion.12 = f32[384,512]{0,1:T(8,128)} fusion(bf16[512,384]{1,0:T(8,128)(2,1)} %param.11, bf16[384,1536]{1,0:T(8,128)(2,1)S(1)} %copy-done, s32[]{:T(128)S(6)} %select_n.72), kind=kOutput, calls=%fused_computation.27 | convolution fusion | flops 150994944 | bytes 1474564 | tf_op jit(solution)/shard_map/dot_general | solution.py:40
  17.3 0.2 fusion.30
  17.8 8.4 %collective-permute-done.7 = bf16[512,384]{1,0:T(8,128)(2,1)} collective-permute-done((bf16[512,384]{1,0:T(8,128)(2,1)}, bf16[512,384]{1,0:T(8,128)(2,1)}, u32[]{:S(2)}, u32[]{:S(2)}) %collective-permute-start.7) | collective-permute-done | bytes 393248 | tf_op jit(solution)/shard_map/ppermute | solution.py:22
  26.2 1.4 %collective-permute-done.2.refs_8_.refs_9_ = bf16[2,512,384]{2,1,0:T(8,128)(2,1)S(1)} collective-permute-done((bf16[2,512,384]{2,1,0:T(8,128)(2,1)}, bf16[2,512,384]{2,1,0:T(8,128)(2,1)S(1)}, u32[]{:S(2)}, u32[]{:S(2)}) %collective-permute-start.2) | collective-permute-done | bytes 786464 | tf_op jit(solution)/shard_map/ppermute | solution.py:17
  27.5 1.3 %collective-permute-start.3 = (bf16[2,512,384]{2,1,0:T(8,128)(2,1)S(1)}, bf16[2,512,384]{2,1,0:T(8,128)(2,1)S(1)}, u32[]{:S(2)}, u32[]{:S(2)}) collective-permute-start(bf16[2,512,384]{2,1,0:T(8,128)(2,1)S(1)} %collective-permute-done.2.refs_8_.refs_9_), channel_id=1, source_target_pairs={{0,4},{8,12},{16,20},{24,28},{32,36},{40,44},{48,52},{56,60},{64,6... | collective-permute-start | bytes 2359304 | tf_op jit(solution)/shard_map/ppermute | solution.py:76
  28.9 1.3 %collective-permute-start.4 = (bf16[2,512,384]{2,1,0:T(8,128)(2,1)S(1)}, bf16[2,512,384]{2,1,0:T(8,128)(2,1)S(1)}, u32[]{:S(2)}, u32[]{:S(2)}) collective-permute-start(bf16[2,512,384]{2,1,0:T(8,128)(2,1)S(1)} %collective-permute-done.refs_0_.refs_1_), channel_id=1, source_target_pairs={{4,0},{12,8},{20,16},{28,24},{36,32},{44,40},{52,48},{60,56},{68,6... | collective-permute-start | bytes 2359304 | tf_op jit(solution)/shard_map/ppermute | solution.py:81
  30.2 1.4 %fusion.15 = f32[384,512]{0,1:T(8,128)S(1)} fusion(bf16[512,384]{1,0:T(8,128)(2,1)} %collective-permute-done.7, bf16[384,1536]{1,0:T(8,128)(2,1)S(1)} %copy-done, s32[]{:T(128)S(6)} %select_n.78), kind=kOutput, calls=%fused_computation.30 | convolution fusion | flops 150994944 | bytes 1474564 | tf_op jit(solution)/shard_map/dot_general | solution.py:40
  31.6 0.4 convolution_add_fusion.2
  32.1 0.7 collective-permute-done.6
  32.7 1.4 %fusion.8.refs_10_ = bf16[512,384]{1,0:T(8,128)(2,1)S(1)} fusion(f32[384,512]{0,1:T(8,128)S(1)} %fusion.15, f32[384,512]{0,1:T(8,128)S(1)} %convolution_add_fusion.2, bf16[512,384]{1,0:T(8,128)(2,1)} %collective-permute-done.6, bf16[384,1536]{1,0:T(8,128)(2,1)S(1)} %copy-done, s32[]{:T(128)S(6)} %select_n.76), kind=kOutput, calls=%fused_computation.18 | convolution fusion | flops 151584768 | bytes 2654212 | tf_op jit(solution)/shard_map/dot_general | solution.py:40
  34.2 16.1 %shard_map.102 = (bf16[512,384]{1,0:T(8,128)(2,1)S(1)}, bf16[512,384]{1,0:T(8,128)(2,1)}, f32[2,512,384]{2,1,0:T(8,128)}, bf16[2,2,512,384]{3,2,1,0:T(8,128)(2,1)}, bf16[2,2,512,384]{3,2,1,0:T(8,128)(2,1)}) custom-call(s32[5]{0:T(128)S(1)} %pad_add_fusion.sel_ref, bf16[512,384]{1,0:T(8,128)(2,1)S(1)} %copy-done.3, bf16[512,384]{1,0:T(8,128)(2,1)S(1)} %copy-done.1, ...), custom_call_target="tpu_custom_call" | custom-call | tf_op jit(solution)/shard_map/pallas_call | solution.py:179
  50.4 1.4 %collective-permute-start.12 = (bf16[2,2,512,384]{3,2,1,0:T(8,128)(2,1)}, bf16[2,2,512,384]{3,2,1,0:T(8,128)(2,1)S(1)}, u32[]{:S(2)}, u32[]{:S(2)}) collective-permute-start(bf16[2,2,512,384]{3,2,1,0:T(8,128)(2,1)} %get-tuple-element.12), channel_id=1, source_target_pairs={{4,0},{12,8},{20,16},{28,24},{36,32},{44,40},{52,48},{60,56},{68,6... | collective-permute-start | bytes 4718600 | tf_op jit(solution)/shard_map/ppermute | solution.py:81
  51.8 3.2 %collective-permute-start.11 = (bf16[2,2,512,384]{3,2,1,0:T(8,128)(2,1)}, bf16[2,2,512,384]{3,2,1,0:T(8,128)(2,1)S(1)}, u32[]{:S(2)}, u32[]{:S(2)}) collective-permute-start(bf16[2,2,512,384]{3,2,1,0:T(8,128)(2,1)} %get-tuple-element.12), channel_id=1, source_target_pairs={{0,4},{8,12},{16,20},{24,28},{32,36},{40,44},{48,52},{56,60},{64,6... | collective-permute-start | bytes 4718600 | tf_op jit(solution)/shard_map/ppermute | solution.py:76
  55.0 1.1 %convolution_convert_fusion = bf16[512,384]{1,0:T(8,128)(2,1)} fusion(bf16[512,384]{1,0:T(8,128)(2,1)S(1)} %get-tuple-element.9, bf16[384,1536]{1,0:T(8,128)(2,1)S(1)} %copy-done, s32[]{:T(128)S(6)} %select_n.78), kind=kOutput, calls=%fused_computation.15 | convolution fusion | flops 151191552 | bytes 1081348 | tf_op jit(solution)/shard_map/dot_general | solution.py:52
  56.2 1.1 %convolution_convert_fusion.1 = bf16[512,384]{1,0:T(8,128)(2,1)} fusion(bf16[512,384]{1,0:T(8,128)(2,1)S(1)} %get-tuple-element.9, bf16[384,1536]{1,0:T(8,128)(2,1)S(1)} %copy-done, s32[]{:T(128)S(6)} %select_n.74), kind=kOutput, calls=%fused_computation.16 | convolution fusion | flops 151191552 | bytes 1081348 | tf_op jit(solution)/shard_map/dot_general | solution.py:52
  57.3 0.8 collective-permute-done.11
  58.1 1.6 %fusion.9 = (bf16[2,512,384]{2,1,0:T(8,128)(2,1)}, bf16[2,512,384]{2,1,0:T(8,128)(2,1)}) fusion(bf16[2,2,512,384]{3,2,1,0:T(8,128)(2,1)S(1)} %collective-permute-done.12, bf16[2,2,512,384]{3,2,1,0:T(8,128)(2,1)S(1)} %copy-done.10, bf16[2,2,512,384]{3,2,1,0:T(8,128)(2,1)S(1)} %collective-permute-done.11), kind=kLoop, calls=%fused_computation.19 | loop fusion | flops 3145728 | bytes 4718592 | tf_op jit(solution)/shard_map/convert_element_type | solution.py:208
  59.8 7.0 %collective-permute-start.13 = (bf16[2,512,384]{2,1,0:T(8,128)(2,1)}, bf16[2,512,384]{2,1,0:T(8,128)(2,1)}, u32[]{:S(2)}, u32[]{:S(2)}) collective-permute-start(bf16[2,512,384]{2,1,0:T(8,128)(2,1)} %get-tuple-element.14), channel_id=1, source_target_pairs={{0,8},{4,12},{8,16},{12,20},{16,24},{20,28},{24,32},{28,36},{32,40... | collective-permute-start | bytes 2359304 | tf_op jit(solution)/shard_map/ppermute | solution.py:17
  66.8 2.1 %collective-permute-start.14 = (bf16[2,512,384]{2,1,0:T(8,128)(2,1)}, bf16[2,512,384]{2,1,0:T(8,128)(2,1)}, u32[]{:S(2)}, u32[]{:S(2)}) collective-permute-start(bf16[2,512,384]{2,1,0:T(8,128)(2,1)} %get-tuple-element.15), channel_id=1, source_target_pairs={{8,0},{12,4},{16,8},{20,12},{24,16},{28,20},{32,24},{36,28},{40,32... | collective-permute-start | bytes 2359304 | tf_op jit(solution)/shard_map/ppermute | solution.py:17
  68.9 1.1 %convolution_convert_fusion.2 = bf16[512,384]{1,0:T(8,128)(2,1)} fusion(bf16[512,384]{1,0:T(8,128)(2,1)S(1)} %get-tuple-element.9, bf16[384,1536]{1,0:T(8,128)(2,1)S(1)} %copy-done, s32[]{:T(128)S(6)} %select_n.76), kind=kOutput, calls=%fused_computation.17 | convolution fusion | flops 151191552 | bytes 1081348 | tf_op jit(solution)/shard_map/dot_general | solution.py:52
  70.0 3.8 %collective-permute-start.8 = (bf16[512,384]{1,0:T(8,128)(2,1)}, bf16[512,384]{1,0:T(8,128)(2,1)S(1)}, u32[]{:S(2)}, u32[]{:S(2)}) collective-permute-start(bf16[512,384]{1,0:T(8,128)(2,1)} %convolution_convert_fusion.2), channel_id=1, source_target_pairs={{0,1},{1,2},{2,3},{3,0},{4,5},{5,6},{6,7},{7,4},{8,9},{9,10},{10,1... | collective-permute-start | bytes 1179656 | tf_op jit(solution)/shard_map/ppermute | solution.py:22
  73.8 1.5 %collective-permute-start.10 = (bf16[512,384]{1,0:T(8,128)(2,1)}, bf16[512,384]{1,0:T(8,128)(2,1)}, u32[]{:S(2)}, u32[]{:S(2)}) collective-permute-start(bf16[512,384]{1,0:T(8,128)(2,1)} %convolution_convert_fusion), channel_id=1, source_target_pairs={{0,2},{1,3},{2,0},{3,1},{4,6},{5,7},{6,4},{7,5},{8,10},{9,11},{10,... | collective-permute-start | bytes 1179656 | tf_op jit(solution)/shard_map/ppermute | solution.py:22
  75.3 15.6 %collective-permute-done.8 = bf16[512,384]{1,0:T(8,128)(2,1)S(1)} collective-permute-done((bf16[512,384]{1,0:T(8,128)(2,1)}, bf16[512,384]{1,0:T(8,128)(2,1)S(1)}, u32[]{:S(2)}, u32[]{:S(2)}) %collective-permute-start.8) | collective-permute-done | bytes 393248 | tf_op jit(solution)/shard_map/ppermute | solution.py:22
  90.9 3.4 %collective-permute-done.9 = bf16[512,384]{1,0:T(8,128)(2,1)} collective-permute-done((bf16[512,384]{1,0:T(8,128)(2,1)}, bf16[512,384]{1,0:T(8,128)(2,1)}, u32[]{:S(2)}, u32[]{:S(2)}) %collective-permute-start.9) | collective-permute-done | bytes 393248 | tf_op jit(solution)/shard_map/ppermute | solution.py:22
  94.3 2.3 %fusion.6 = bf16[512,384]{1,0:T(8,128)(2,1)} fusion(bf16[512,384]{1,0:T(8,128)(2,1)S(1)} %get-tuple-element.9, bf16[512,384]{1,0:T(8,128)(2,1)} %collective-permute-done.10, bf16[512,384]{1,0:T(8,128)(2,1)} %collective-permute-done.9, bf16[512,384]{1,0:T(8,128)(2,1)S(1)} %collective-permute-done.8, bf16[384,1536]{1,0:T(8,128)(2,1)S(1)} %copy-done, ...), kind=kOutput, calls=%fused_computation.13 | convolution fusion | flops 152371200 | bytes 2260996 | tf_op jit(solution)/shard_map/dot_general | solution.py:61
  96.7 2.1 %fusion.2 = bf16[2,512,384]{2,1,0:T(8,128)(2,1)S(1)} fusion(f32[2,512,384]{2,1,0:T(8,128)S(1)} %copy-done.6, bf16[2,512,384]{2,1,0:T(8,128)(2,1)} %collective-permute-done.14, bf16[2,512,384]{2,1,0:T(8,128)(2,1)} %collective-permute-done.13, bf16[2,2,512,384]{3,2,1,0:T(8,128)(2,1)S(1)} %copy-done.8, bf16[2,2,512,384]{3,2,1,0:T(8,128)(2,1)} %copy-done.9), kind=kLoop, calls=%fused_computation.3 | loop fusion | flops 3538944 | bytes 5505024 | tf_op jit(solution)/shard_map/convert_element_type | solution.py:219
  98.8 1.0 slice_bitcast_fusion.2
  (39 shorter events, 0.3 us)
Async XLA Ops:
  0.6 14.3 %copy-start = (bf16[384,1536]{1,0:T(8,128)(2,1)S(1)}, bf16[384,1536]{1,0:T(8,128)(2,1)}, u32[]{:S(2)}) copy-start(bf16[384,1536]{1,0:T(8,128)(2,1)} %param.10) | copy-start | bytes 3538948
  0.6 16.7 %copy-start.11 = (s32[64,2]{0,1:T(2,128)S(1)}, s32[64,2]{0,1:T(2,128)}, u32[]{:S(2)}) copy-start(s32[64,2]{0,1:T(2,128)} %param.12) | copy-start | bytes 1540
  0.7 16.9 %copy-start.4 = (s32[512]{0:T(512)S(1)}, s32[512]{0:T(512)}, u32[]{:S(2)}) copy-start(s32[512]{0:T(512)} %param.13) | copy-start | bytes 6148
  2.8 24.7 %collective-permute-start.2 = (bf16[2,512,384]{2,1,0:T(8,128)(2,1)}, bf16[2,512,384]{2,1,0:T(8,128)(2,1)S(1)}, u32[]{:S(2)}, u32[]{:S(2)}) collective-permute-start(bf16[2,512,384]{2,1,0:T(8,128)(2,1)} %pad_maximum_fusion), channel_id=1, source_target_pairs={{8,0},{12,4},{16,8},{20,12},{24,16},{28,20},{32,24},{36,28},{40,32... | collective-permute-start | bytes 2359304 | tf_op jit(solution)/shard_map/ppermute | solution.py:17
  5.6 23.3 %collective-permute-start = (bf16[2,512,384]{2,1,0:T(8,128)(2,1)}, bf16[2,512,384]{2,1,0:T(8,128)(2,1)S(1)}, u32[]{:S(2)}, u32[]{:S(2)}) collective-permute-start(bf16[2,512,384]{2,1,0:T(8,128)(2,1)} %pad_maximum_fusion), channel_id=1, source_target_pairs={{0,8},{4,12},{8,16},{12,20},{16,24},{20,28},{24,32},{28,36},{32,40... | collective-permute-start | bytes 2359304 | tf_op jit(solution)/shard_map/ppermute | solution.py:17
  12.0 19.6 %collective-permute-start.5 = (bf16[512,384]{1,0:T(8,128)(2,1)}, bf16[512,384]{1,0:T(8,128)(2,1)S(1)}, u32[]{:S(2)}, u32[]{:S(2)}) collective-permute-start(bf16[512,384]{1,0:T(8,128)(2,1)} %param.11), channel_id=1, source_target_pairs={{0,1},{1,2},{2,3},{3,0},{4,5},{5,6},{6,7},{7,4},{8,9},{9,10},{10,1... | collective-permute-start | bytes 1179656 | tf_op jit(solution)/shard_map/ppermute | solution.py:22
  12.3 13.9 %collective-permute-start.7 = (bf16[512,384]{1,0:T(8,128)(2,1)}, bf16[512,384]{1,0:T(8,128)(2,1)}, u32[]{:S(2)}, u32[]{:S(2)}) collective-permute-start(bf16[512,384]{1,0:T(8,128)(2,1)} %param.11), channel_id=1, source_target_pairs={{0,2},{1,3},{2,0},{3,1},{4,6},{5,7},{6,4},{7,5},{8,10},{9,11},{10,... | collective-permute-start | bytes 1179656 | tf_op jit(solution)/shard_map/ppermute | solution.py:22
  14.9 17.8 %collective-permute-start.6 = (bf16[512,384]{1,0:T(8,128)(2,1)}, bf16[512,384]{1,0:T(8,128)(2,1)}, u32[]{:S(2)}, u32[]{:S(2)}) collective-permute-start(bf16[512,384]{1,0:T(8,128)(2,1)} %param.11), channel_id=1, source_target_pairs={{0,3},{1,0},{2,1},{3,2},{4,7},{5,4},{6,5},{7,6},{8,11},{9,8},{10,9... | collective-permute-start | bytes 1179656 | tf_op jit(solution)/shard_map/ppermute | solution.py:22
  17.7 13.9 %copy-start.5 = (f32[384,512]{0,1:T(8,128)S(1)}, f32[384,512]{0,1:T(8,128)}, u32[]{:S(2)}) copy-start(f32[384,512]{0,1:T(8,128)} %fusion.12) | copy-start | bytes 2359300
  26.2 8.0 %collective-permute-start.1 = (bf16[2,512,384]{2,1,0:T(8,128)(2,1)}, bf16[2,512,384]{2,1,0:T(8,128)(2,1)S(1)}, u32[]{:S(2)}, u32[]{:S(2)}) collective-permute-start(bf16[2,512,384]{2,1,0:T(8,128)(2,1)} %pad_maximum_fusion), channel_id=1, source_target_pairs={{0,4},{4,0},{8,12},{12,8},{16,20},{20,16},{24,28},{28,24},{32,36},... | collective-permute-start | bytes 2359304 | tf_op jit(solution)/shard_map/ppermute | solution.py:71
  27.5 6.6 %collective-permute-start.3 = (bf16[2,512,384]{2,1,0:T(8,128)(2,1)S(1)}, bf16[2,512,384]{2,1,0:T(8,128)(2,1)S(1)}, u32[]{:S(2)}, u32[]{:S(2)}) collective-permute-start(bf16[2,512,384]{2,1,0:T(8,128)(2,1)S(1)} %collective-permute-done.2.refs_8_.refs_9_), channel_id=1, source_target_pairs={{0,4},{8,12},{16,20},{24,28},{32,36},{40,44},{48,52},{56,60},{64,6... | collective-permute-start | bytes 2359304 | tf_op jit(solution)/shard_map/ppermute | solution.py:76
  28.9 5.3 %collective-permute-start.4 = (bf16[2,512,384]{2,1,0:T(8,128)(2,1)S(1)}, bf16[2,512,384]{2,1,0:T(8,128)(2,1)S(1)}, u32[]{:S(2)}, u32[]{:S(2)}) collective-permute-start(bf16[2,512,384]{2,1,0:T(8,128)(2,1)S(1)} %collective-permute-done.refs_0_.refs_1_), channel_id=1, source_target_pairs={{4,0},{12,8},{20,16},{28,24},{36,32},{44,40},{52,48},{60,56},{68,6... | collective-permute-start | bytes 2359304 | tf_op jit(solution)/shard_map/ppermute | solution.py:81
  32.0 2.1 %copy-start.1 = (bf16[512,384]{1,0:T(8,128)(2,1)S(1)}, bf16[512,384]{1,0:T(8,128)(2,1)}, u32[]{:S(2)}) copy-start(bf16[512,384]{1,0:T(8,128)(2,1)} %k0_ref.1) | copy-start | bytes 1179652
  32.1 2.1 %copy-start.2 = (bf16[512,384]{1,0:T(8,128)(2,1)S(1)}, bf16[512,384]{1,0:T(8,128)(2,1)}, u32[]{:S(2)}) copy-start(bf16[512,384]{1,0:T(8,128)(2,1)} %v0_ref.1) | copy-start | bytes 1179652
  32.1 2.1 %copy-start.3 = (bf16[512,384]{1,0:T(8,128)(2,1)S(1)}, bf16[512,384]{1,0:T(8,128)(2,1)}, u32[]{:S(2)}) copy-start(bf16[512,384]{1,0:T(8,128)(2,1)} %q_ref.1) | copy-start | bytes 1179652
  50.4 7.8 %copy-start.10 = (bf16[2,2,512,384]{3,2,1,0:T(8,128)(2,1)S(1)}, bf16[2,2,512,384]{3,2,1,0:T(8,128)(2,1)}, u32[]{:S(2)}) copy-start(bf16[2,2,512,384]{3,2,1,0:T(8,128)(2,1)} %get-tuple-element.13) | copy-start | bytes 4718596
  50.4 6.9 %collective-permute-start.12 = (bf16[2,2,512,384]{3,2,1,0:T(8,128)(2,1)}, bf16[2,2,512,384]{3,2,1,0:T(8,128)(2,1)S(1)}, u32[]{:S(2)}, u32[]{:S(2)}) collective-permute-start(bf16[2,2,512,384]{3,2,1,0:T(8,128)(2,1)} %get-tuple-element.12), channel_id=1, source_target_pairs={{4,0},{12,8},{20,16},{28,24},{36,32},{44,40},{52,48},{60,56},{68,6... | collective-permute-start | bytes 4718600 | tf_op jit(solution)/shard_map/ppermute | solution.py:81
  51.8 6.4 %collective-permute-start.11 = (bf16[2,2,512,384]{3,2,1,0:T(8,128)(2,1)}, bf16[2,2,512,384]{3,2,1,0:T(8,128)(2,1)S(1)}, u32[]{:S(2)}, u32[]{:S(2)}) collective-permute-start(bf16[2,2,512,384]{3,2,1,0:T(8,128)(2,1)} %get-tuple-element.12), channel_id=1, source_target_pairs={{0,4},{8,12},{16,20},{24,28},{32,36},{40,44},{48,52},{56,60},{64,6... | collective-permute-start | bytes 4718600 | tf_op jit(solution)/shard_map/ppermute | solution.py:76
  57.3 2.5 %copy-start.7 = (bf16[2,2,512,384]{3,2,1,0:T(8,128)(2,1)}, bf16[2,2,512,384]{3,2,1,0:T(8,128)(2,1)S(1)}, u32[]{:S(2)}) copy-start(bf16[2,2,512,384]{3,2,1,0:T(8,128)(2,1)S(1)} %collective-permute-done.12) | copy-start | bytes 4718596
  58.1 1.6 %copy-start.9 = (bf16[2,2,512,384]{3,2,1,0:T(8,128)(2,1)}, bf16[2,2,512,384]{3,2,1,0:T(8,128)(2,1)S(1)}, u32[]{:S(2)}) copy-start(bf16[2,2,512,384]{3,2,1,0:T(8,128)(2,1)S(1)} %collective-permute-done.11) | copy-start | bytes 4718596
  59.8 36.9 %collective-permute-start.13 = (bf16[2,512,384]{2,1,0:T(8,128)(2,1)}, bf16[2,512,384]{2,1,0:T(8,128)(2,1)}, u32[]{:S(2)}, u32[]{:S(2)}) collective-permute-start(bf16[2,512,384]{2,1,0:T(8,128)(2,1)} %get-tuple-element.14), channel_id=1, source_target_pairs={{0,8},{4,12},{8,16},{12,20},{16,24},{20,28},{24,32},{28,36},{32,40... | collective-permute-start | bytes 2359304 | tf_op jit(solution)/shard_map/ppermute | solution.py:17
  66.8 29.9 %copy-start.6 = (f32[2,512,384]{2,1,0:T(8,128)S(1)}, f32[2,512,384]{2,1,0:T(8,128)}, u32[]{:S(2)}) copy-start(f32[2,512,384]{2,1,0:T(8,128)} %get-tuple-element.11) | copy-start | bytes 4718596
  66.8 29.9 %collective-permute-start.14 = (bf16[2,512,384]{2,1,0:T(8,128)(2,1)}, bf16[2,512,384]{2,1,0:T(8,128)(2,1)}, u32[]{:S(2)}, u32[]{:S(2)}) collective-permute-start(bf16[2,512,384]{2,1,0:T(8,128)(2,1)} %get-tuple-element.15), channel_id=1, source_target_pairs={{8,0},{12,4},{16,8},{20,12},{24,16},{28,20},{32,24},{36,28},{40,32... | collective-permute-start | bytes 2359304 | tf_op jit(solution)/shard_map/ppermute | solution.py:17
  70.0 20.9 %collective-permute-start.8 = (bf16[512,384]{1,0:T(8,128)(2,1)}, bf16[512,384]{1,0:T(8,128)(2,1)S(1)}, u32[]{:S(2)}, u32[]{:S(2)}) collective-permute-start(bf16[512,384]{1,0:T(8,128)(2,1)} %convolution_convert_fusion.2), channel_id=1, source_target_pairs={{0,1},{1,2},{2,3},{3,0},{4,5},{5,6},{6,7},{7,4},{8,9},{9,10},{10,1... | collective-permute-start | bytes 1179656 | tf_op jit(solution)/shard_map/ppermute | solution.py:22
  73.8 20.5 %collective-permute-start.9 = (bf16[512,384]{1,0:T(8,128)(2,1)}, bf16[512,384]{1,0:T(8,128)(2,1)}, u32[]{:S(2)}, u32[]{:S(2)}) collective-permute-start(bf16[512,384]{1,0:T(8,128)(2,1)} %convolution_convert_fusion.1), channel_id=1, source_target_pairs={{0,3},{1,0},{2,1},{3,2},{4,7},{5,4},{6,5},{7,6},{8,11},{9,8},{10,9... | collective-permute-start | bytes 1179656 | tf_op jit(solution)/shard_map/ppermute | solution.py:22
  73.8 20.5 %collective-permute-start.10 = (bf16[512,384]{1,0:T(8,128)(2,1)}, bf16[512,384]{1,0:T(8,128)(2,1)}, u32[]{:S(2)}, u32[]{:S(2)}) collective-permute-start(bf16[512,384]{1,0:T(8,128)(2,1)} %convolution_convert_fusion), channel_id=1, source_target_pairs={{0,2},{1,3},{2,0},{3,1},{4,6},{5,7},{6,4},{7,5},{8,10},{9,11},{10,... | collective-permute-start | bytes 1179656 | tf_op jit(solution)/shard_map/ppermute | solution.py:22
  75.3 21.4 %copy-start.8 = (bf16[2,2,512,384]{3,2,1,0:T(8,128)(2,1)S(1)}, bf16[2,2,512,384]{3,2,1,0:T(8,128)(2,1)}, u32[]{:S(2)}) copy-start(bf16[2,2,512,384]{3,2,1,0:T(8,128)(2,1)} %copy-done.7) | copy-start | bytes 4718596

commit v5 on v4

--- a/solution.py
+++ b/solution.py
@@ -71,18 +71,14 @@
     return lax.ppermute(block, axis, [(i, i ^ 1) for i in range(size)])
 
 
-def even_to_odd(block, axis):
+def cross_chip(block, axis):
     size = lax.axis_size(axis)
-    return lax.ppermute(block, axis, [(i, i + 1) for i in range(0, size - 1, 2)])
-
-
-def odd_to_even(block, axis):
-    size = lax.axis_size(axis)
-    return lax.ppermute(block, axis, [(i, i - 1) for i in range(1, size, 2)])
+    pairs = [(i, i - 1) for i in range(2, size, 2)] + [(i, i + 1) for i in range(1, size - 1, 2)]
+    return lax.ppermute(block, axis, pairs)
 
 
 def attn_kernel(sel_ref, q_ref, k0_ref, v0_ref, *refs):
-    n_cand = 5
+    n_cand = 4
     cand_k = refs[0:2 * n_cand:2]
     cand_v = refs[1:2 * n_cand:2]
     g_ref, srow_ref, scol_ref, attn_ref, dq_ref, self_ref, near_ref, far_ref = refs[2 * n_cand:]
@@ -138,7 +134,9 @@
             routed.append((sel_ref[2 + j], dk.astype(jnp.bfloat16), dv.astype(jnp.bfloat16)))
     (off1, dk1, dv1), (off2, dk2, dv2) = routed
     zero = jnp.zeros_like(dk1)
-    for ref, slot, value in ((far_ref, 0, -2), (near_ref, 0, -1), (near_ref, 1, 1), (far_ref, 1, 2)):
+    partner_off = 1 - 2 * sel_ref[5]
+    for ref, slot, value in ((far_ref, 0, -2), (near_ref, 0, partner_off), (near_ref, 1, -partner_off),
+                             (far_ref, 1, 2)):
         ref[slot, 0] = jnp.where(off1 == value, dk1, jnp.where(off2 == value, dk2, zero))
         ref[slot, 1] = jnp.where(off1 == value, dv1, jnp.where(off2 == value, dv2, zero))
     dq_ref[...] = dq.astype(jnp.bfloat16)
@@ -193,26 +191,23 @@
     from_left2 = shifted(own_kv, "seq", 2)
     from_right2 = shifted(own_kv, "seq", -2)
     partner_own = partner_swap(own_kv, "seq")
-    relay_to_odd = even_to_odd(from_right2, "seq")
-    relay_to_even = odd_to_even(from_left2, "seq")
+    from_cross = cross_chip(own_kv, "seq")
     partner_off = 1 - 2 * parity
     offs = (routes[seq_index] - seq_index).astype(jnp.int32)
-    relay_idx = jnp.where(parity == 1, 2, 3)
-    pick = jnp.where(offs == -2, 0, jnp.where(offs == 2, 4, jnp.where(offs == partner_off, 1, relay_idx)))
-    sel = jnp.concatenate([pick.astype(jnp.int32), jnp.zeros((1,), jnp.int32), offs])
-    cands = (from_left2, partner_own, relay_to_odd, relay_to_even, from_right2)
+    pick = jnp.where(offs == -2, 0, jnp.where(offs == 2, 3, jnp.where(offs == partner_off, 1, 2)))
+    sel = jnp.concatenate([pick.astype(jnp.int32), jnp.zeros((1,), jnp.int32), offs, parity[None]])
+    sel = sel.astype(jnp.int32)
+    cands = (from_left2, partner_own, from_cross, from_right2)
     attn, grad_q, self_term, near, far = attention(sel, queries, keys, values, cands, grad_attn, shot_ids)
     attn_out = project_out(attn, out_weight)
-    got_a = even_to_odd(near, "seq")
-    got_b = odd_to_even(near, "seq")
-    up_plus = (far[1].astype(jnp.float32) + got_b[1].astype(jnp.float32)).astype(jnp.bfloat16)
-    up_minus = (far[0].astype(jnp.float32) + got_a[0].astype(jnp.float32)).astype(jnp.bfloat16)
-    got_from_left = shifted(up_plus, "seq", 2)
-    got_from_right = shifted(up_minus, "seq", -2)
+    back_partner = partner_swap(near[0], "seq")
+    back_cross = cross_chip(near[1], "seq")
+    got_from_left = shifted(far[1], "seq", 2)
+    got_from_right = shifted(far[0], "seq", -2)
     total = (
         self_term
-        + got_a[1].astype(jnp.float32)
-        + got_b[0].astype(jnp.float32)
+        + back_partner.astype(jnp.float32)
+        + back_cross.astype(jnp.float32)
         + got_from_left.astype(jnp.float32)
         + got_from_right.astype(jnp.float32)
     )

time: 101 us -> 105 us (1.040)
  the two profiles are of different devices: /device:TPU:126 before, /device:TPU:129 now
where the time goes in v5:
time: 105 us
  waiting for transfers between devices  38 us (36%)
  starting transfers between devices  32.8 us (31%)
  Pallas kernels  15.8 us (15%)
  matrix products  9 us (9%)
  other arithmetic  4.65 us (4%)
  local copies, waits for them, and re-layouts  3.78 us (4%)
    pallas_call x1, Pallas kernels, attention(): pl.pallas_call(attn_kernel, grid_spec=grid_spec, out_shape=out_shape, com...  15.8 us
    ppermute x6, waiting for transfers between devices, ring_shift(): lax.ppermute(block, axis, [(i, (i + distance) % size) for i in range(size)])  15.7 us
    ppermute x4, starting transfers between devices, shifted(): return lax.ppermute(block, axis, route)  15.6 us
    ppermute x4, waiting for transfers between devices, shifted(): return lax.ppermute(block, axis, route)  12.9 us
    ppermute x2, waiting for transfers between devices, cross_chip(): return lax.ppermute(block, axis, pairs)  9.43 us
    ppermute x6, starting transfers between devices, ring_shift(): lax.ppermute(block, axis, [(i, (i + distance) % size) for i in range(size)])  8.5 us
    ppermute x2, starting transfers between devices, cross_chip(): return lax.ppermute(block, axis, pairs)  4.94 us
    dot_general x4, matrix products, fold_cotangent(): lax.dot_general(piece, w_cols, nt, preferred_element_type=jnp.float32)  4.73 us
  transfers between devices with their start and end apart: 14, of which 5 were waited for; matrix products, arithmetic and copies ran while one was open for 13% of the time, Pallas kernels for 0%

profile of v5, /device:TPU:129, one launch (start us, length us, event | category | flops | bytes accessed | tf_op | source)
XLA Modules:
  0.0 104.9 jit_solution(534652428622955134)
XLA Ops:
  0.7 1.4 %collective-permute-start.4 = (bf16[512,384]{1,0:T(8,128)(2,1)}, bf16[512,384]{1,0:T(8,128)(2,1)S(1)}, u32[]{:S(2)}, u32[]{:S(2)}) collective-permute-start(bf16[512,384]{1,0:T(8,128)(2,1)} %param.11), channel_id=1, source_target_pairs={{0,1},{1,2},{2,3},{3,0},{4,5},{5,6},{6,7},{7,4},{8,9},{9,10},{10,1... | collective-permute-start | bytes 1179656 | tf_op jit(solution)/shard_map/ppermute | solution.py:22
  2.0 2.6 %collective-permute-start.6 = (bf16[512,384]{1,0:T(8,128)(2,1)}, bf16[512,384]{1,0:T(8,128)(2,1)}, u32[]{:S(2)}, u32[]{:S(2)}) collective-permute-start(bf16[512,384]{1,0:T(8,128)(2,1)} %param.11), channel_id=1, source_target_pairs={{0,2},{1,3},{2,0},{3,1},{4,6},{5,7},{6,4},{7,5},{8,10},{9,11},{10,... | collective-permute-start | bytes 1179656 | tf_op jit(solution)/shard_map/ppermute | solution.py:22
  4.7 1.1 %collective-permute-start.5 = (bf16[512,384]{1,0:T(8,128)(2,1)}, bf16[512,384]{1,0:T(8,128)(2,1)}, u32[]{:S(2)}, u32[]{:S(2)}) collective-permute-start(bf16[512,384]{1,0:T(8,128)(2,1)} %param.11), channel_id=1, source_target_pairs={{0,3},{1,0},{2,1},{3,2},{4,7},{5,4},{6,5},{7,6},{8,11},{9,8},{10,9... | collective-permute-start | bytes 1179656 | tf_op jit(solution)/shard_map/ppermute | solution.py:22
  5.7 2.1 %pad_maximum_fusion = bf16[2,512,384]{2,1,0:T(8,128)(2,1)} fusion(bf16[1,512,384]{2,1,0:T(8,128)(2,1)} %bitcast.28, bf16[1,512,384]{2,1,0:T(8,128)(2,1)} %bitcast.27), kind=kLoop, calls=%fused_computation.13 | loop fusion | flops 393216 | bytes 1572864 | tf_op jit(solution)/shard_map/stack | solution.py:190
  7.8 3.9 %collective-permute-start.3 = (bf16[2,512,384]{2,1,0:T(8,128)(2,1)}, bf16[2,512,384]{2,1,0:T(8,128)(2,1)S(1)}, u32[]{:S(2)}, u32[]{:S(2)}) collective-permute-start(bf16[2,512,384]{2,1,0:T(8,128)(2,1)} %pad_maximum_fusion), channel_id=1, source_target_pairs={{8,0},{12,4},{16,8},{20,12},{24,16},{28,20},{32,24},{36,28},{40,32... | collective-permute-start | bytes 2359304 | tf_op jit(solution)/shard_map/ppermute | solution.py:17
  11.7 3.0 %collective-permute-start.2 = (bf16[2,512,384]{2,1,0:T(8,128)(2,1)}, bf16[2,512,384]{2,1,0:T(8,128)(2,1)S(1)}, u32[]{:S(2)}, u32[]{:S(2)}) collective-permute-start(bf16[2,512,384]{2,1,0:T(8,128)(2,1)} %pad_maximum_fusion), channel_id=1, source_target_pairs={{8,4},{16,12},{24,20},{32,28},{40,36},{48,44},{56,52},{64,60},{72,... | collective-permute-start | bytes 2359304 | tf_op jit(solution)/shard_map/ppermute | solution.py:77
  15.3 1.4 %fusion.7 = f32[384,512]{0,1:T(8,128)S(1)} fusion(bf16[512,384]{1,0:T(8,128)(2,1)} %param.11, bf16[384,1536]{1,0:T(8,128)(2,1)S(1)} %copy-done, s32[]{:T(128)S(6)} %select_n.67), kind=kOutput, calls=%fused_computation.21 | convolution fusion | flops 150994944 | bytes 1474564 | tf_op jit(solution)/shard_map/dot_general | solution.py:40
  16.7 0.8 collective-permute-start.1
  17.5 4.4 %collective-permute-done.6 = bf16[512,384]{1,0:T(8,128)(2,1)} collective-permute-done((bf16[512,384]{1,0:T(8,128)(2,1)}, bf16[512,384]{1,0:T(8,128)(2,1)}, u32[]{:S(2)}, u32[]{:S(2)}) %collective-permute-start.6) | collective-permute-done | bytes 393248 | tf_op jit(solution)/shard_map/ppermute | solution.py:22
  21.9 3.1 %collective-permute-start = (bf16[2,512,384]{2,1,0:T(8,128)(2,1)}, bf16[2,512,384]{2,1,0:T(8,128)(2,1)S(1)}, u32[]{:S(2)}, u32[]{:S(2)}) collective-permute-start(bf16[2,512,384]{2,1,0:T(8,128)(2,1)} %pad_maximum_fusion), channel_id=1, source_target_pairs={{0,8},{4,12},{8,16},{12,20},{16,24},{20,28},{24,32},{28,36},{32,40... | collective-permute-start | bytes 2359304 | tf_op jit(solution)/shard_map/ppermute | solution.py:17
  25.1 1.4 %fusion.10 = f32[384,512]{0,1:T(8,128)S(1)} fusion(bf16[512,384]{1,0:T(8,128)(2,1)} %collective-permute-done.6, bf16[384,1536]{1,0:T(8,128)(2,1)S(1)} %copy-done, s32[]{:T(128)S(6)} %select_n.73), kind=kOutput, calls=%fused_computation.24 | convolution fusion | flops 150994944 | bytes 1474564 | tf_op jit(solution)/shard_map/dot_general | solution.py:40
  26.5 0.4 convolution_add_fusion.2
  26.9 1.5 %fusion.5.refs_8_ = bf16[512,384]{1,0:T(8,128)(2,1)S(1)} fusion(f32[384,512]{0,1:T(8,128)S(1)} %fusion.10, f32[384,512]{0,1:T(8,128)S(1)} %convolution_add_fusion.2, bf16[512,384]{1,0:T(8,128)(2,1)} %collective-permute-done.5, bf16[384,1536]{1,0:T(8,128)(2,1)S(1)} %copy-done, s32[]{:T(128)S(6)} %select_n.71), kind=kOutput, calls=%fused_computation.12 | convolution fusion | flops 151584768 | bytes 2654212 | tf_op jit(solution)/shard_map/dot_general | solution.py:40
  28.5 9.4 %collective-permute-done.2.refs_4_.refs_5_ = bf16[2,512,384]{2,1,0:T(8,128)(2,1)S(1)} collective-permute-done((bf16[2,512,384]{2,1,0:T(8,128)(2,1)}, bf16[2,512,384]{2,1,0:T(8,128)(2,1)S(1)}, u32[]{:S(2)}, u32[]{:S(2)}) %collective-permute-start.2) | collective-permute-done | bytes 786464 | tf_op jit(solution)/shard_map/ppermute | solution.py:77
  37.9 7.0 %collective-permute-done.refs_0_.refs_1_ = bf16[2,512,384]{2,1,0:T(8,128)(2,1)S(1)} collective-permute-done((bf16[2,512,384]{2,1,0:T(8,128)(2,1)}, bf16[2,512,384]{2,1,0:T(8,128)(2,1)S(1)}, u32[]{:S(2)}, u32[]{:S(2)}) %collective-permute-start) | collective-permute-done | bytes 786464 | tf_op jit(solution)/shard_map/ppermute | solution.py:17
  44.9 15.8 %shard_map.102 = (bf16[512,384]{1,0:T(8,128)(2,1)S(1)}, bf16[512,384]{1,0:T(8,128)(2,1)}, f32[2,512,384]{2,1,0:T(8,128)}, bf16[2,2,512,384]{3,2,1,0:T(8,128)(2,1)}, bf16[2,2,512,384]{3,2,1,0:T(8,128)(2,1)}) custom-call(s32[6]{0:T(128)S(1)} %pad_add_fusion.sel_ref, bf16[512,384]{1,0:T(8,128)(2,1)S(1)} %copy-done.3, bf16[512,384]{1,0:T(8,128)(2,1)S(1)} %copy-done.1, ...), custom_call_target="tpu_custom_call" | custom-call | tf_op jit(solution)/shard_map/pallas_call | solution.py:177
  61.1 0.4 convolution_convert_fusion.2
  61.5 2.1 %collective-permute-start.7 = (bf16[512,384]{1,0:T(8,128)(2,1)S(1)}, bf16[512,384]{1,0:T(8,128)(2,1)S(1)}, u32[]{:S(2)}, u32[]{:S(2)}) collective-permute-start(bf16[512,384]{1,0:T(8,128)(2,1)S(1)} %convolution_convert_fusion.2), channel_id=1, source_target_pairs={{0,1},{1,2},{2,3},{3,0},{4,5},{5,6},{6,7},{7,4},{8,9},{9,10},{10,1... | collective-permute-start | bytes 1179656 | tf_op jit(solution)/shard_map/ppermute | solution.py:22
  63.6 0.7 collective-permute-start.8
  64.3 1.3 %slice_bitcast_fusion.3 = (bf16[2,512,384]{2,1,0:T(8,128)(2,1)}, bf16[2,512,384]{2,1,0:T(8,128)(2,1)}) fusion(bf16[2,2,512,384]{3,2,1,0:T(8,128)(2,1)S(1)} %copy-done.6), kind=kLoop, calls=%fused_computation.17 | loop fusion | bytes 3145728 | tf_op jit(solution)/shard_map/squeeze | solution.py:203
  65.6 2.9 %collective-permute-start.10 = (bf16[2,512,384]{2,1,0:T(8,128)(2,1)}, bf16[2,512,384]{2,1,0:T(8,128)(2,1)}, u32[]{:S(2)}, u32[]{:S(2)}) collective-permute-start(bf16[2,512,384]{2,1,0:T(8,128)(2,1)} %get-tuple-element.14), channel_id=1, source_target_pairs={{0,4},{4,0},{8,12},{12,8},{16,20},{20,16},{24,28},{28,24},{32,36},... | collective-permute-start | bytes 2359304 | tf_op jit(solution)/shard_map/ppermute | solution.py:71
  68.6 1.9 %collective-permute-start.11 = (bf16[2,512,384]{2,1,0:T(8,128)(2,1)}, bf16[2,512,384]{2,1,0:T(8,128)(2,1)}, u32[]{:S(2)}, u32[]{:S(2)}) collective-permute-start(bf16[2,512,384]{2,1,0:T(8,128)(2,1)} %get-tuple-element.15), channel_id=1, source_target_pairs={{8,4},{16,12},{24,20},{32,28},{40,36},{48,44},{56,52},{64,60},{72,... | collective-permute-start | bytes 2359304 | tf_op jit(solution)/shard_map/ppermute | solution.py:77
  70.5 1.3 %slice_bitcast_fusion.1 = (bf16[2,512,384]{2,1,0:T(8,128)(2,1)}, bf16[2,512,384]{2,1,0:T(8,128)(2,1)}) fusion(bf16[2,2,512,384]{3,2,1,0:T(8,128)(2,1)S(1)} %copy-done.5), kind=kLoop, calls=%fused_computation.15 | loop fusion | bytes 3145728 | tf_op jit(solution)/shard_map/squeeze | solution.py:205
  71.8 1.9 %collective-permute-start.12 = (bf16[2,512,384]{2,1,0:T(8,128)(2,1)}, bf16[2,512,384]{2,1,0:T(8,128)(2,1)}, u32[]{:S(2)}, u32[]{:S(2)}) collective-permute-start(bf16[2,512,384]{2,1,0:T(8,128)(2,1)} %get-tuple-element.16), channel_id=1, source_target_pairs={{0,8},{4,12},{8,16},{12,20},{16,24},{20,28},{24,32},{28,36},{32,40... | collective-permute-start | bytes 2359304 | tf_op jit(solution)/shard_map/ppermute | solution.py:17
  73.7 6.7 %collective-permute-start.13 = (bf16[2,512,384]{2,1,0:T(8,128)(2,1)}, bf16[2,512,384]{2,1,0:T(8,128)(2,1)}, u32[]{:S(2)}, u32[]{:S(2)}) collective-permute-start(bf16[2,512,384]{2,1,0:T(8,128)(2,1)} %get-tuple-element.17), channel_id=1, source_target_pairs={{8,0},{12,4},{16,8},{20,12},{24,16},{28,20},{32,24},{36,28},{40,32... | collective-permute-start | bytes 2359304 | tf_op jit(solution)/shard_map/ppermute | solution.py:17
  80.4 1.1 %convolution_convert_fusion = bf16[512,384]{1,0:T(8,128)(2,1)} fusion(bf16[512,384]{1,0:T(8,128)(2,1)S(1)} %get-tuple-element.9, bf16[384,1536]{1,0:T(8,128)(2,1)S(1)} %copy-done, s32[]{:T(128)S(6)} %select_n.73), kind=kOutput, calls=%fused_computation.9 | convolution fusion | flops 151191552 | bytes 1081348 | tf_op jit(solution)/shard_map/dot_general | solution.py:52
  81.6 0.7 collective-permute-start.9
  82.3 11.2 %collective-permute-done.9 = bf16[512,384]{1,0:T(8,128)(2,1)} collective-permute-done((bf16[512,384]{1,0:T(8,128)(2,1)}, bf16[512,384]{1,0:T(8,128)(2,1)}, u32[]{:S(2)}, u32[]{:S(2)}) %collective-permute-start.9) | collective-permute-done | bytes 393248 | tf_op jit(solution)/shard_map/ppermute | solution.py:22
  93.5 2.3 %fusion.3 = bf16[512,384]{1,0:T(8,128)(2,1)} fusion(bf16[512,384]{1,0:T(8,128)(2,1)S(1)} %get-tuple-element.9, bf16[512,384]{1,0:T(8,128)(2,1)} %collective-permute-done.9, bf16[512,384]{1,0:T(8,128)(2,1)} %collective-permute-done.8, bf16[512,384]{1,0:T(8,128)(2,1)S(1)} %collective-permute-done.7, bf16[384,1536]{1,0:T(8,128)(2,1)S(1)} %copy-done, ...), kind=kOutput, calls=%fused_computation.7 | convolution fusion | flops 152371200 | bytes 2260996 | tf_op jit(solution)/shard_map/dot_general | solution.py:61
  95.8 5.8 %collective-permute-done.12 = bf16[2,512,384]{2,1,0:T(8,128)(2,1)} collective-permute-done((bf16[2,512,384]{2,1,0:T(8,128)(2,1)}, bf16[2,512,384]{2,1,0:T(8,128)(2,1)}, u32[]{:S(2)}, u32[]{:S(2)}) %collective-permute-start.12) | collective-permute-done | bytes 786464 | tf_op jit(solution)/shard_map/ppermute | solution.py:17
  101.7 2.3 %add_convert_fusion = bf16[2,512,384]{2,1,0:T(8,128)(2,1)S(1)} fusion(bf16[2,512,384]{2,1,0:T(8,128)(2,1)} %collective-permute-done.13, bf16[2,512,384]{2,1,0:T(8,128)(2,1)} %collective-permute-done.12, bf16[2,512,384]{2,1,0:T(8,128)(2,1)} %collective-permute-done.11, f32[2,512,384]{2,1,0:T(8,128)S(1)} %copy-done.7, bf16[2,512,384]{2,1,0:T(8,128)(2,1)} %collective-permute-done.10), kind=kLoop, calls=%fused_computation | loop fusion | flops 3538944 | bytes 5505024 | tf_op jit(solution)/shard_map/convert_element_type | solution.py:214
  104.0 1.0 slice_bitcast_fusion.4
  (32 shorter events, 0.9 us)
Async XLA Ops:
  0.6 14.7 %copy-start = (bf16[384,1536]{1,0:T(8,128)(2,1)S(1)}, bf16[384,1536]{1,0:T(8,128)(2,1)}, u32[]{:S(2)}) copy-start(bf16[384,1536]{1,0:T(8,128)(2,1)} %param.10) | copy-start | bytes 3538948
  0.6 14.1 %copy-start.8 = (s32[64,2]{0,1:T(2,128)S(1)}, s32[64,2]{0,1:T(2,128)}, u32[]{:S(2)}) copy-start(s32[64,2]{0,1:T(2,128)} %param.12) | copy-start | bytes 1540
  0.7 14.4 %copy-start.4 = (s32[512]{0:T(512)S(1)}, s32[512]{0:T(512)}, u32[]{:S(2)}) copy-start(s32[512]{0:T(512)} %param.13) | copy-start | bytes 6148
  0.7 16.1 %collective-permute-start.4 = (bf16[512,384]{1,0:T(8,128)(2,1)}, bf16[512,384]{1,0:T(8,128)(2,1)S(1)}, u32[]{:S(2)}, u32[]{:S(2)}) collective-permute-start(bf16[512,384]{1,0:T(8,128)(2,1)} %param.11), channel_id=1, source_target_pairs={{0,1},{1,2},{2,3},{3,0},{4,5},{5,6},{6,7},{7,4},{8,9},{9,10},{10,1... | collective-permute-start | bytes 1179656 | tf_op jit(solution)/shard_map/ppermute | solution.py:22
  2.0 19.9 %collective-permute-start.6 = (bf16[512,384]{1,0:T(8,128)(2,1)}, bf16[512,384]{1,0:T(8,128)(2,1)}, u32[]{:S(2)}, u32[]{:S(2)}) collective-permute-start(bf16[512,384]{1,0:T(8,128)(2,1)} %param.11), channel_id=1, source_target_pairs={{0,2},{1,3},{2,0},{3,1},{4,6},{5,7},{6,4},{7,5},{8,10},{9,11},{10,... | collective-permute-start | bytes 1179656 | tf_op jit(solution)/shard_map/ppermute | solution.py:22
  4.7 22.3 %collective-permute-start.5 = (bf16[512,384]{1,0:T(8,128)(2,1)}, bf16[512,384]{1,0:T(8,128)(2,1)}, u32[]{:S(2)}, u32[]{:S(2)}) collective-permute-start(bf16[512,384]{1,0:T(8,128)(2,1)} %param.11), channel_id=1, source_target_pairs={{0,3},{1,0},{2,1},{3,2},{4,7},{5,4},{6,5},{7,6},{8,11},{9,8},{10,9... | collective-permute-start | bytes 1179656 | tf_op jit(solution)/shard_map/ppermute | solution.py:22
  7.8 20.6 %collective-permute-start.3 = (bf16[2,512,384]{2,1,0:T(8,128)(2,1)}, bf16[2,512,384]{2,1,0:T(8,128)(2,1)S(1)}, u32[]{:S(2)}, u32[]{:S(2)}) collective-permute-start(bf16[2,512,384]{2,1,0:T(8,128)(2,1)} %pad_maximum_fusion), channel_id=1, source_target_pairs={{8,0},{12,4},{16,8},{20,12},{24,16},{28,20},{32,24},{36,28},{40,32... | collective-permute-start | bytes 2359304 | tf_op jit(solution)/shard_map/ppermute | solution.py:17
  11.7 26.2 %collective-permute-start.2 = (bf16[2,512,384]{2,1,0:T(8,128)(2,1)}, bf16[2,512,384]{2,1,0:T(8,128)(2,1)S(1)}, u32[]{:S(2)}, u32[]{:S(2)}) collective-permute-start(bf16[2,512,384]{2,1,0:T(8,128)(2,1)} %pad_maximum_fusion), channel_id=1, source_target_pairs={{8,4},{16,12},{24,20},{32,28},{40,36},{48,44},{56,52},{64,60},{72,... | collective-permute-start | bytes 2359304 | tf_op jit(solution)/shard_map/ppermute | solution.py:77
  16.7 21.2 %collective-permute-start.1 = (bf16[2,512,384]{2,1,0:T(8,128)(2,1)}, bf16[2,512,384]{2,1,0:T(8,128)(2,1)S(1)}, u32[]{:S(2)}, u32[]{:S(2)}) collective-permute-start(bf16[2,512,384]{2,1,0:T(8,128)(2,1)} %pad_maximum_fusion), channel_id=1, source_target_pairs={{0,4},{4,0},{8,12},{12,8},{16,20},{20,16},{24,28},{28,24},{32,36},... | collective-permute-start | bytes 2359304 | tf_op jit(solution)/shard_map/ppermute | solution.py:71
  21.9 23.0 %collective-permute-start = (bf16[2,512,384]{2,1,0:T(8,128)(2,1)}, bf16[2,512,384]{2,1,0:T(8,128)(2,1)S(1)}, u32[]{:S(2)}, u32[]{:S(2)}) collective-permute-start(bf16[2,512,384]{2,1,0:T(8,128)(2,1)} %pad_maximum_fusion), channel_id=1, source_target_pairs={{0,8},{4,12},{8,16},{12,20},{16,24},{20,28},{24,32},{28,36},{32,40... | collective-permute-start | bytes 2359304 | tf_op jit(solution)/shard_map/ppermute | solution.py:17
  26.9 18.0 %copy-start.1 = (bf16[512,384]{1,0:T(8,128)(2,1)S(1)}, bf16[512,384]{1,0:T(8,128)(2,1)}, u32[]{:S(2)}) copy-start(bf16[512,384]{1,0:T(8,128)(2,1)} %k0_ref.1) | copy-start | bytes 1179652
  26.9 18.0 %copy-start.2 = (bf16[512,384]{1,0:T(8,128)(2,1)S(1)}, bf16[512,384]{1,0:T(8,128)(2,1)}, u32[]{:S(2)}) copy-start(bf16[512,384]{1,0:T(8,128)(2,1)} %v0_ref.1) | copy-start | bytes 1179652
  26.9 18.0 %copy-start.3 = (bf16[512,384]{1,0:T(8,128)(2,1)S(1)}, bf16[512,384]{1,0:T(8,128)(2,1)}, u32[]{:S(2)}) copy-start(bf16[512,384]{1,0:T(8,128)(2,1)} %q_ref.1) | copy-start | bytes 1179652
  60.7 3.6 %copy-start.6 = (bf16[2,2,512,384]{3,2,1,0:T(8,128)(2,1)S(1)}, bf16[2,2,512,384]{3,2,1,0:T(8,128)(2,1)}, u32[]{:S(2)}) copy-start(bf16[2,2,512,384]{3,2,1,0:T(8,128)(2,1)} %get-tuple-element.12) | copy-start | bytes 4718596
  61.5 12.2 %collective-permute-start.7 = (bf16[512,384]{1,0:T(8,128)(2,1)S(1)}, bf16[512,384]{1,0:T(8,128)(2,1)S(1)}, u32[]{:S(2)}, u32[]{:S(2)}) collective-permute-start(bf16[512,384]{1,0:T(8,128)(2,1)S(1)} %convolution_convert_fusion.2), channel_id=1, source_target_pairs={{0,1},{1,2},{2,3},{3,0},{4,5},{5,6},{6,7},{7,4},{8,9},{9,10},{10,1... | collective-permute-start | bytes 1179656 | tf_op jit(solution)/shard_map/ppermute | solution.py:22
  63.6 17.9 %collective-permute-start.8 = (bf16[512,384]{1,0:T(8,128)(2,1)S(1)}, bf16[512,384]{1,0:T(8,128)(2,1)}, u32[]{:S(2)}, u32[]{:S(2)}) collective-permute-start(bf16[512,384]{1,0:T(8,128)(2,1)S(1)} %convolution_convert_fusion.1), channel_id=1, source_target_pairs={{0,3},{1,0},{2,1},{3,2},{4,7},{5,4},{6,5},{7,6},{8,11},{9,8},{10,9... | collective-permute-start | bytes 1179656 | tf_op jit(solution)/shard_map/ppermute | solution.py:22
  64.3 6.2 %copy-start.5 = (bf16[2,2,512,384]{3,2,1,0:T(8,128)(2,1)S(1)}, bf16[2,2,512,384]{3,2,1,0:T(8,128)(2,1)}, u32[]{:S(2)}) copy-start(bf16[2,2,512,384]{3,2,1,0:T(8,128)(2,1)} %get-tuple-element.13) | copy-start | bytes 4718596
  65.6 30.2 %collective-permute-start.10 = (bf16[2,512,384]{2,1,0:T(8,128)(2,1)}, bf16[2,512,384]{2,1,0:T(8,128)(2,1)}, u32[]{:S(2)}, u32[]{:S(2)}) collective-permute-start(bf16[2,512,384]{2,1,0:T(8,128)(2,1)} %get-tuple-element.14), channel_id=1, source_target_pairs={{0,4},{4,0},{8,12},{12,8},{16,20},{20,16},{24,28},{28,24},{32,36},... | collective-permute-start | bytes 2359304 | tf_op jit(solution)/shard_map/ppermute | solution.py:71
  68.6 27.3 %collective-permute-start.11 = (bf16[2,512,384]{2,1,0:T(8,128)(2,1)}, bf16[2,512,384]{2,1,0:T(8,128)(2,1)}, u32[]{:S(2)}, u32[]{:S(2)}) collective-permute-start(bf16[2,512,384]{2,1,0:T(8,128)(2,1)} %get-tuple-element.15), channel_id=1, source_target_pairs={{8,4},{16,12},{24,20},{32,28},{40,36},{48,44},{56,52},{64,60},{72,... | collective-permute-start | bytes 2359304 | tf_op jit(solution)/shard_map/ppermute | solution.py:77
  71.8 29.9 %collective-permute-start.12 = (bf16[2,512,384]{2,1,0:T(8,128)(2,1)}, bf16[2,512,384]{2,1,0:T(8,128)(2,1)}, u32[]{:S(2)}, u32[]{:S(2)}) collective-permute-start(bf16[2,512,384]{2,1,0:T(8,128)(2,1)} %get-tuple-element.16), channel_id=1, source_target_pairs={{0,8},{4,12},{8,16},{12,20},{16,24},{20,28},{24,32},{28,36},{32,40... | collective-permute-start | bytes 2359304 | tf_op jit(solution)/shard_map/ppermute | solution.py:17
  73.7 28.0 %collective-permute-start.13 = (bf16[2,512,384]{2,1,0:T(8,128)(2,1)}, bf16[2,512,384]{2,1,0:T(8,128)(2,1)}, u32[]{:S(2)}, u32[]{:S(2)}) collective-permute-start(bf16[2,512,384]{2,1,0:T(8,128)(2,1)} %get-tuple-element.17), channel_id=1, source_target_pairs={{8,0},{12,4},{16,8},{20,12},{24,16},{28,20},{32,24},{36,28},{40,32... | collective-permute-start | bytes 2359304 | tf_op jit(solution)/shard_map/ppermute | solution.py:17
  81.6 20.1 %copy-start.7 = (f32[2,512,384]{2,1,0:T(8,128)S(1)}, f32[2,512,384]{2,1,0:T(8,128)}, u32[]{:S(2)}) copy-start(f32[2,512,384]{2,1,0:T(8,128)} %get-tuple-element.11) | copy-start | bytes 4718596
  81.6 11.9 %collective-permute-start.9 = (bf16[512,384]{1,0:T(8,128)(2,1)}, bf16[512,384]{1,0:T(8,128)(2,1)}, u32[]{:S(2)}, u32[]{:S(2)}) collective-permute-start(bf16[512,384]{1,0:T(8,128)(2,1)} %convolution_convert_fusion), channel_id=1, source_target_pairs={{0,2},{1,3},{2,0},{3,1},{4,6},{5,7},{6,4},{7,5},{8,10},{9,11},{10,... | collective-permute-start | bytes 1179656 | tf_op jit(solution)/shard_map/ppermute | solution.py:22

commit v6 on v4

--- a/solution.py
+++ b/solution.py
@@ -209,15 +209,18 @@
     up_minus = (far[0].astype(jnp.float32) + got_a[0].astype(jnp.float32)).astype(jnp.bfloat16)
     got_from_left = shifted(up_plus, "seq", 2)
     got_from_right = shifted(up_minus, "seq", -2)
-    total = (
-        self_term
-        + got_a[1].astype(jnp.float32)
-        + got_b[0].astype(jnp.float32)
-        + got_from_left.astype(jnp.float32)
-        + got_from_right.astype(jnp.float32)
-    )
-    rounded = total.astype(jnp.bfloat16)
-    return (attn_out, grad_q, rounded[0], rounded[1])
+
+    def summed(part):
+        total = (
+            self_term[part]
+            + got_a[1, part].astype(jnp.float32)
+            + got_b[0, part].astype(jnp.float32)
+            + got_from_left[part].astype(jnp.float32)
+            + got_from_right[part].astype(jnp.float32)
+        )
+        return total.astype(jnp.bfloat16)
+
+    return (attn_out, grad_q, summed(0), summed(1))
 
 
 def solution(mesh):

time: 101 us -> 101 us (level)
  no operation moved by 1% of the time
where the time goes in v6:
time: 101 us; the launch traced here: 99.6 us
  starting transfers between devices  33.6 us (33%)
  waiting for transfers between devices  30.3 us (30%)
  Pallas kernels  16.1 us (16%)
  matrix products  11.4 us (11%)
  other arithmetic  7 us (7%)
    ppermute x6, waiting for transfers between devices, ring_shift(): lax.ppermute(block, axis, [(i, (i + distance) % size) for i in range(size)])  28 us
    ppermute x4, starting transfers between devices, shifted(): return lax.ppermute(block, axis, route)  18.2 us
    pallas_call x1, Pallas kernels, attention(): pl.pallas_call(attn_kernel, grid_spec=grid_spec, out_shape=out_shape, com...  16.1 us
    ppermute x6, starting transfers between devices, ring_shift(): lax.ppermute(block, axis, [(i, (i + distance) % size) for i in range(size)])  8.14 us
    dot_general x4, matrix products, fold_cotangent(): lax.dot_general(piece, w_cols, nt, preferred_element_type=jnp.float32)  5.63 us
    ppermute x2, starting transfers between devices, even_to_odd(): lax.ppermute(block, axis, [(i, i + 1) for i in range(0, size - 1, 2)])  4.55 us
    dot_general x3, matrix products, part(): jnp.dot(attn, w_cols, preferred_element_type=jnp.float32)  3.44 us
    convert_element_type x1, other arithmetic, summed(): return total.astype(jnp.bfloat16)  2.93 us
  transfers between devices with their start and end apart: 15, of which 6 were waited for; matrix products, arithmetic and copies ran while one was open for 12% of the time, Pallas kernels for 0%

profile of v6, /device:TPU:126, one launch (start us, length us, event | category | flops | bytes accessed | tf_op | source)
XLA Modules:
  0.0 99.6 jit_solution(10072415231744158564)
XLA Ops:
  0.7 2.2 %pad_maximum_fusion = bf16[2,512,384]{2,1,0:T(8,128)(2,1)} fusion(bf16[1,512,384]{2,1,0:T(8,128)(2,1)} %bitcast.63, bf16[1,512,384]{2,1,0:T(8,128)(2,1)} %bitcast.62), kind=kLoop, calls=%fused_computation.16 | loop fusion | flops 393216 | bytes 1572864 | tf_op jit(solution)/shard_map/stack | solution.py:192
  2.8 2.7 %collective-permute-start.2 = (bf16[2,512,384]{2,1,0:T(8,128)(2,1)}, bf16[2,512,384]{2,1,0:T(8,128)(2,1)S(1)}, u32[]{:S(2)}, u32[]{:S(2)}) collective-permute-start(bf16[2,512,384]{2,1,0:T(8,128)(2,1)} %pad_maximum_fusion), channel_id=1, source_target_pairs={{8,0},{12,4},{16,8},{20,12},{24,16},{28,20},{32,24},{36,28},{40,32... | collective-permute-start | bytes 2359304 | tf_op jit(solution)/shard_map/ppermute | solution.py:17
  5.6 6.4 %collective-permute-start = (bf16[2,512,384]{2,1,0:T(8,128)(2,1)}, bf16[2,512,384]{2,1,0:T(8,128)(2,1)S(1)}, u32[]{:S(2)}, u32[]{:S(2)}) collective-permute-start(bf16[2,512,384]{2,1,0:T(8,128)(2,1)} %pad_maximum_fusion), channel_id=1, source_target_pairs={{0,8},{4,12},{8,16},{12,20},{16,24},{20,28},{24,32},{28,36},{32,40... | collective-permute-start | bytes 2359304 | tf_op jit(solution)/shard_map/ppermute | solution.py:17
  12.0 0.3 collective-permute-start.5
  12.3 2.6 %collective-permute-start.7 = (bf16[512,384]{1,0:T(8,128)(2,1)}, bf16[512,384]{1,0:T(8,128)(2,1)}, u32[]{:S(2)}, u32[]{:S(2)}) collective-permute-start(bf16[512,384]{1,0:T(8,128)(2,1)} %param.11), channel_id=1, source_target_pairs={{0,2},{1,3},{2,0},{3,1},{4,6},{5,7},{6,4},{7,5},{8,10},{9,11},{10,... | collective-permute-start | bytes 1179656 | tf_op jit(solution)/shard_map/ppermute | solution.py:22
  14.9 2.4 %fusion.11 = f32[384,512]{0,1:T(8,128)} fusion(bf16[512,384]{1,0:T(8,128)(2,1)} %param.11, bf16[384,1536]{1,0:T(8,128)(2,1)S(1)} %copy-done, s32[]{:T(128)S(6)} %select_n.72), kind=kOutput, calls=%fused_computation.36 | convolution fusion | flops 150994944 | bytes 1474564 | tf_op jit(solution)/shard_map/dot_general | solution.py:40
  17.3 0.2 fusion.29
  17.6 0.1 copy.19.refs_11_
  17.8 8.4 %collective-permute-done.7 = bf16[512,384]{1,0:T(8,128)(2,1)} collective-permute-done((bf16[512,384]{1,0:T(8,128)(2,1)}, bf16[512,384]{1,0:T(8,128)(2,1)}, u32[]{:S(2)}, u32[]{:S(2)}) %collective-permute-start.7) | collective-permute-done | bytes 393248 | tf_op jit(solution)/shard_map/ppermute | solution.py:22
  26.2 1.4 %collective-permute-done.2.refs_8_.refs_9_ = bf16[2,512,384]{2,1,0:T(8,128)(2,1)S(1)} collective-permute-done((bf16[2,512,384]{2,1,0:T(8,128)(2,1)}, bf16[2,512,384]{2,1,0:T(8,128)(2,1)S(1)}, u32[]{:S(2)}, u32[]{:S(2)}) %collective-permute-start.2) | collective-permute-done | bytes 786464 | tf_op jit(solution)/shard_map/ppermute | solution.py:17
  27.5 1.3 %collective-permute-start.3 = (bf16[2,512,384]{2,1,0:T(8,128)(2,1)S(1)}, bf16[2,512,384]{2,1,0:T(8,128)(2,1)S(1)}, u32[]{:S(2)}, u32[]{:S(2)}) collective-permute-start(bf16[2,512,384]{2,1,0:T(8,128)(2,1)S(1)} %collective-permute-done.2.refs_8_.refs_9_), channel_id=1, source_target_pairs={{0,4},{8,12},{16,20},{24,28},{32,36},{40,44},{48,52},{56,60},{64,6... | collective-permute-start | bytes 2359304 | tf_op jit(solution)/shard_map/ppermute | solution.py:76
  28.9 1.3 %collective-permute-start.4 = (bf16[2,512,384]{2,1,0:T(8,128)(2,1)S(1)}, bf16[2,512,384]{2,1,0:T(8,128)(2,1)S(1)}, u32[]{:S(2)}, u32[]{:S(2)}) collective-permute-start(bf16[2,512,384]{2,1,0:T(8,128)(2,1)S(1)} %collective-permute-done.refs_0_.refs_1_), channel_id=1, source_target_pairs={{4,0},{12,8},{20,16},{28,24},{36,32},{44,40},{52,48},{60,56},{68,6... | collective-permute-start | bytes 2359304 | tf_op jit(solution)/shard_map/ppermute | solution.py:81
  30.2 1.4 %fusion.14 = f32[384,512]{0,1:T(8,128)S(1)} fusion(bf16[512,384]{1,0:T(8,128)(2,1)} %collective-permute-done.7, bf16[384,1536]{1,0:T(8,128)(2,1)S(1)} %copy-done, s32[]{:T(128)S(6)} %select_n.78), kind=kOutput, calls=%fused_computation.39 | convolution fusion | flops 150994944 | bytes 1474564 | tf_op jit(solution)/shard_map/dot_general | solution.py:40
  31.6 0.4 convolution_add_fusion.2
  32.1 0.7 collective-permute-done.6
  32.7 1.4 %fusion.5.refs_10_ = bf16[512,384]{1,0:T(8,128)(2,1)S(1)} fusion(f32[384,512]{0,1:T(8,128)S(1)} %fusion.14, f32[384,512]{0,1:T(8,128)S(1)} %convolution_add_fusion.2, bf16[512,384]{1,0:T(8,128)(2,1)} %collective-permute-done.6, bf16[384,1536]{1,0:T(8,128)(2,1)S(1)} %copy-done, s32[]{:T(128)S(6)} %select_n.76), kind=kOutput, calls=%fused_computation.13 | convolution fusion | flops 151584768 | bytes 2654212 | tf_op jit(solution)/shard_map/dot_general | solution.py:40
  34.2 16.1 %shard_map.102 = (bf16[512,384]{1,0:T(8,128)(2,1)S(1)}, bf16[512,384]{1,0:T(8,128)(2,1)}, f32[2,512,384]{2,1,0:T(8,128)}, bf16[2,2,512,384]{3,2,1,0:T(8,128)(2,1)}, bf16[2,2,512,384]{3,2,1,0:T(8,128)(2,1)}) custom-call(s32[5]{0:T(128)S(1)} %pad_add_fusion.sel_ref, bf16[512,384]{1,0:T(8,128)(2,1)S(1)} %copy-done.3, bf16[512,384]{1,0:T(8,128)(2,1)S(1)} %copy-done.1, ...), custom_call_target="tpu_custom_call" | custom-call | tf_op jit(solution)/shard_map/pallas_call | solution.py:179
  50.4 1.4 %collective-permute-start.12 = (bf16[2,2,512,384]{3,2,1,0:T(8,128)(2,1)}, bf16[2,2,512,384]{3,2,1,0:T(8,128)(2,1)S(1)}, u32[]{:S(2)}, u32[]{:S(2)}) collective-permute-start(bf16[2,2,512,384]{3,2,1,0:T(8,128)(2,1)} %get-tuple-element.12), channel_id=1, source_target_pairs={{4,0},{12,8},{20,16},{28,24},{36,32},{44,40},{52,48},{60,56},{68,6... | collective-permute-start | bytes 4718600 | tf_op jit(solution)/shard_map/ppermute | solution.py:81
  51.8 3.2 %collective-permute-start.11 = (bf16[2,2,512,384]{3,2,1,0:T(8,128)(2,1)}, bf16[2,2,512,384]{3,2,1,0:T(8,128)(2,1)S(1)}, u32[]{:S(2)}, u32[]{:S(2)}) collective-permute-start(bf16[2,2,512,384]{3,2,1,0:T(8,128)(2,1)} %get-tuple-element.12), channel_id=1, source_target_pairs={{0,4},{8,12},{16,20},{24,28},{32,36},{40,44},{48,52},{56,60},{64,6... | collective-permute-start | bytes 4718600 | tf_op jit(solution)/shard_map/ppermute | solution.py:76
  55.0 1.1 %convolution_convert_fusion = bf16[512,384]{1,0:T(8,128)(2,1)} fusion(bf16[512,384]{1,0:T(8,128)(2,1)S(1)} %get-tuple-element.9, bf16[384,1536]{1,0:T(8,128)(2,1)S(1)} %copy-done, s32[]{:T(128)S(6)} %select_n.78), kind=kOutput, calls=%fused_computation.10 | convolution fusion | flops 151191552 | bytes 1081348 | tf_op jit(solution)/shard_map/dot_general | solution.py:52
  56.2 1.1 %convolution_convert_fusion.1 = bf16[512,384]{1,0:T(8,128)(2,1)} fusion(bf16[512,384]{1,0:T(8,128)(2,1)S(1)} %get-tuple-element.9, bf16[384,1536]{1,0:T(8,128)(2,1)S(1)} %copy-done, s32[]{:T(128)S(6)} %select_n.74), kind=kOutput, calls=%fused_computation.11 | convolution fusion | flops 151191552 | bytes 1081348 | tf_op jit(solution)/shard_map/dot_general | solution.py:52
  57.3 0.8 collective-permute-done.11
  58.1 1.6 %fusion.6 = (bf16[2,512,384]{2,1,0:T(8,128)(2,1)}, bf16[2,512,384]{2,1,0:T(8,128)(2,1)}) fusion(bf16[2,2,512,384]{3,2,1,0:T(8,128)(2,1)S(1)} %collective-permute-done.12, bf16[2,2,512,384]{3,2,1,0:T(8,128)(2,1)S(1)} %copy-done.10, bf16[2,2,512,384]{3,2,1,0:T(8,128)(2,1)S(1)} %collective-permute-done.11), kind=kLoop, calls=%fused_computation.14 | loop fusion | flops 3145728 | bytes 4718592 | tf_op jit(solution)/shard_map/convert_element_type | solution.py:208
  59.8 7.0 %collective-permute-start.13 = (bf16[2,512,384]{2,1,0:T(8,128)(2,1)}, bf16[2,512,384]{2,1,0:T(8,128)(2,1)}, u32[]{:S(2)}, u32[]{:S(2)}) collective-permute-start(bf16[2,512,384]{2,1,0:T(8,128)(2,1)} %get-tuple-element.16), channel_id=1, source_target_pairs={{0,8},{4,12},{8,16},{12,20},{16,24},{20,28},{24,32},{28,36},{32,40... | collective-permute-start | bytes 2359304 | tf_op jit(solution)/shard_map/ppermute | solution.py:17
  66.8 2.1 %collective-permute-start.14 = (bf16[2,512,384]{2,1,0:T(8,128)(2,1)}, bf16[2,512,384]{2,1,0:T(8,128)(2,1)}, u32[]{:S(2)}, u32[]{:S(2)}) collective-permute-start(bf16[2,512,384]{2,1,0:T(8,128)(2,1)} %get-tuple-element.17), channel_id=1, source_target_pairs={{8,0},{12,4},{16,8},{20,12},{24,16},{28,20},{32,24},{36,28},{40,32... | collective-permute-start | bytes 2359304 | tf_op jit(solution)/shard_map/ppermute | solution.py:17
  68.9 1.1 %convolution_convert_fusion.2 = bf16[512,384]{1,0:T(8,128)(2,1)} fusion(bf16[512,384]{1,0:T(8,128)(2,1)S(1)} %get-tuple-element.9, bf16[384,1536]{1,0:T(8,128)(2,1)S(1)} %copy-done, s32[]{:T(128)S(6)} %select_n.76), kind=kOutput, calls=%fused_computation.12 | convolution fusion | flops 151191552 | bytes 1081348 | tf_op jit(solution)/shard_map/dot_general | solution.py:52
  70.0 3.8 %collective-permute-start.8 = (bf16[512,384]{1,0:T(8,128)(2,1)}, bf16[512,384]{1,0:T(8,128)(2,1)S(1)}, u32[]{:S(2)}, u32[]{:S(2)}) collective-permute-start(bf16[512,384]{1,0:T(8,128)(2,1)} %convolution_convert_fusion.2), channel_id=1, source_target_pairs={{0,1},{1,2},{2,3},{3,0},{4,5},{5,6},{6,7},{7,4},{8,9},{9,10},{10,1... | collective-permute-start | bytes 1179656 | tf_op jit(solution)/shard_map/ppermute | solution.py:22
  73.8 1.5 %collective-permute-start.10 = (bf16[512,384]{1,0:T(8,128)(2,1)}, bf16[512,384]{1,0:T(8,128)(2,1)}, u32[]{:S(2)}, u32[]{:S(2)}) collective-permute-start(bf16[512,384]{1,0:T(8,128)(2,1)} %convolution_convert_fusion), channel_id=1, source_target_pairs={{0,2},{1,3},{2,0},{3,1},{4,6},{5,7},{6,4},{7,5},{8,10},{9,11},{10,... | collective-permute-start | bytes 1179656 | tf_op jit(solution)/shard_map/ppermute | solution.py:22
  75.3 15.6 %collective-permute-done.8 = bf16[512,384]{1,0:T(8,128)(2,1)S(1)} collective-permute-done((bf16[512,384]{1,0:T(8,128)(2,1)}, bf16[512,384]{1,0:T(8,128)(2,1)S(1)}, u32[]{:S(2)}, u32[]{:S(2)}) %collective-permute-start.8) | collective-permute-done | bytes 393248 | tf_op jit(solution)/shard_map/ppermute | solution.py:22
  90.9 3.4 %collective-permute-done.9 = bf16[512,384]{1,0:T(8,128)(2,1)} collective-permute-done((bf16[512,384]{1,0:T(8,128)(2,1)}, bf16[512,384]{1,0:T(8,128)(2,1)}, u32[]{:S(2)}, u32[]{:S(2)}) %collective-permute-start.9) | collective-permute-done | bytes 393248 | tf_op jit(solution)/shard_map/ppermute | solution.py:22
  94.3 2.3 %fusion.3 = bf16[512,384]{1,0:T(8,128)(2,1)} fusion(bf16[512,384]{1,0:T(8,128)(2,1)S(1)} %get-tuple-element.9, bf16[512,384]{1,0:T(8,128)(2,1)} %collective-permute-done.10, bf16[512,384]{1,0:T(8,128)(2,1)} %collective-permute-done.9, bf16[512,384]{1,0:T(8,128)(2,1)S(1)} %collective-permute-done.8, bf16[384,1536]{1,0:T(8,128)(2,1)S(1)} %copy-done, ...), kind=kOutput, calls=%fused_computation.8 | convolution fusion | flops 152371200 | bytes 2260996 | tf_op jit(solution)/shard_map/dot_general | solution.py:61
  96.7 2.9 %fusion.8 = (bf16[512,384]{1,0:T(8,128)(2,1)}, bf16[512,384]{1,0:T(8,128)(2,1)}) fusion(f32[2,512,384]{2,1,0:T(8,128)S(1)} %copy-done.6, bf16[2,512,384]{2,1,0:T(8,128)(2,1)} %collective-permute-done.14, bf16[2,512,384]{2,1,0:T(8,128)(2,1)} %collective-permute-done.13, bf16[2,2,512,384]{3,2,1,0:T(8,128)(2,1)S(1)} %copy-done.8, ...), kind=kLoop, calls=%fused_computation.18 | loop fusion | flops 3538944 | bytes 5505024 | tf_op jit(solution)/shard_map/convert_element_type | solution.py:221
  (38 shorter events, 0.2 us)
Async XLA Ops:
  0.6 14.3 %copy-start = (bf16[384,1536]{1,0:T(8,128)(2,1)S(1)}, bf16[384,1536]{1,0:T(8,128)(2,1)}, u32[]{:S(2)}) copy-start(bf16[384,1536]{1,0:T(8,128)(2,1)} %param.10) | copy-start | bytes 3538948
  0.6 16.7 %copy-start.11 = (s32[64,2]{0,1:T(2,128)S(1)}, s32[64,2]{0,1:T(2,128)}, u32[]{:S(2)}) copy-start(s32[64,2]{0,1:T(2,128)} %param.12) | copy-start | bytes 1540
  0.7 16.9 %copy-start.4 = (s32[512]{0:T(512)S(1)}, s32[512]{0:T(512)}, u32[]{:S(2)}) copy-start(s32[512]{0:T(512)} %param.13) | copy-start | bytes 6148
  2.8 24.7 %collective-permute-start.2 = (bf16[2,512,384]{2,1,0:T(8,128)(2,1)}, bf16[2,512,384]{2,1,0:T(8,128)(2,1)S(1)}, u32[]{:S(2)}, u32[]{:S(2)}) collective-permute-start(bf16[2,512,384]{2,1,0:T(8,128)(2,1)} %pad_maximum_fusion), channel_id=1, source_target_pairs={{8,0},{12,4},{16,8},{20,12},{24,16},{28,20},{32,24},{36,28},{40,32... | collective-permute-start | bytes 2359304 | tf_op jit(solution)/shard_map/ppermute | solution.py:17
  5.6 23.3 %collective-permute-start = (bf16[2,512,384]{2,1,0:T(8,128)(2,1)}, bf16[2,512,384]{2,1,0:T(8,128)(2,1)S(1)}, u32[]{:S(2)}, u32[]{:S(2)}) collective-permute-start(bf16[2,512,384]{2,1,0:T(8,128)(2,1)} %pad_maximum_fusion), channel_id=1, source_target_pairs={{0,8},{4,12},{8,16},{12,20},{16,24},{20,28},{24,32},{28,36},{32,40... | collective-permute-start | bytes 2359304 | tf_op jit(solution)/shard_map/ppermute | solution.py:17
  12.0 19.6 %collective-permute-start.5 = (bf16[512,384]{1,0:T(8,128)(2,1)}, bf16[512,384]{1,0:T(8,128)(2,1)S(1)}, u32[]{:S(2)}, u32[]{:S(2)}) collective-permute-start(bf16[512,384]{1,0:T(8,128)(2,1)} %param.11), channel_id=1, source_target_pairs={{0,1},{1,2},{2,3},{3,0},{4,5},{5,6},{6,7},{7,4},{8,9},{9,10},{10,1... | collective-permute-start | bytes 1179656 | tf_op jit(solution)/shard_map/ppermute | solution.py:22
  12.3 13.9 %collective-permute-start.7 = (bf16[512,384]{1,0:T(8,128)(2,1)}, bf16[512,384]{1,0:T(8,128)(2,1)}, u32[]{:S(2)}, u32[]{:S(2)}) collective-permute-start(bf16[512,384]{1,0:T(8,128)(2,1)} %param.11), channel_id=1, source_target_pairs={{0,2},{1,3},{2,0},{3,1},{4,6},{5,7},{6,4},{7,5},{8,10},{9,11},{10,... | collective-permute-start | bytes 1179656 | tf_op jit(solution)/shard_map/ppermute | solution.py:22
  14.9 17.8 %collective-permute-start.6 = (bf16[512,384]{1,0:T(8,128)(2,1)}, bf16[512,384]{1,0:T(8,128)(2,1)}, u32[]{:S(2)}, u32[]{:S(2)}) collective-permute-start(bf16[512,384]{1,0:T(8,128)(2,1)} %param.11), channel_id=1, source_target_pairs={{0,3},{1,0},{2,1},{3,2},{4,7},{5,4},{6,5},{7,6},{8,11},{9,8},{10,9... | collective-permute-start | bytes 1179656 | tf_op jit(solution)/shard_map/ppermute | solution.py:22
  17.7 13.9 %copy-start.5 = (f32[384,512]{0,1:T(8,128)S(1)}, f32[384,512]{0,1:T(8,128)}, u32[]{:S(2)}) copy-start(f32[384,512]{0,1:T(8,128)} %fusion.11) | copy-start | bytes 2359300
  26.2 8.0 %collective-permute-start.1 = (bf16[2,512,384]{2,1,0:T(8,128)(2,1)}, bf16[2,512,384]{2,1,0:T(8,128)(2,1)S(1)}, u32[]{:S(2)}, u32[]{:S(2)}) collective-permute-start(bf16[2,512,384]{2,1,0:T(8,128)(2,1)} %pad_maximum_fusion), channel_id=1, source_target_pairs={{0,4},{4,0},{8,12},{12,8},{16,20},{20,16},{24,28},{28,24},{32,36},... | collective-permute-start | bytes 2359304 | tf_op jit(solution)/shard_map/ppermute | solution.py:71
  27.5 6.6 %collective-permute-start.3 = (bf16[2,512,384]{2,1,0:T(8,128)(2,1)S(1)}, bf16[2,512,384]{2,1,0:T(8,128)(2,1)S(1)}, u32[]{:S(2)}, u32[]{:S(2)}) collective-permute-start(bf16[2,512,384]{2,1,0:T(8,128)(2,1)S(1)} %collective-permute-done.2.refs_8_.refs_9_), channel_id=1, source_target_pairs={{0,4},{8,12},{16,20},{24,28},{32,36},{40,44},{48,52},{56,60},{64,6... | collective-permute-start | bytes 2359304 | tf_op jit(solution)/shard_map/ppermute | solution.py:76
  28.9 5.3 %collective-permute-start.4 = (bf16[2,512,384]{2,1,0:T(8,128)(2,1)S(1)}, bf16[2,512,384]{2,1,0:T(8,128)(2,1)S(1)}, u32[]{:S(2)}, u32[]{:S(2)}) collective-permute-start(bf16[2,512,384]{2,1,0:T(8,128)(2,1)S(1)} %collective-permute-done.refs_0_.refs_1_), channel_id=1, source_target_pairs={{4,0},{12,8},{20,16},{28,24},{36,32},{44,40},{52,48},{60,56},{68,6... | collective-permute-start | bytes 2359304 | tf_op jit(solution)/shard_map/ppermute | solution.py:81
  32.0 2.1 %copy-start.1 = (bf16[512,384]{1,0:T(8,128)(2,1)S(1)}, bf16[512,384]{1,0:T(8,128)(2,1)}, u32[]{:S(2)}) copy-start(bf16[512,384]{1,0:T(8,128)(2,1)} %k0_ref.1) | copy-start | bytes 1179652
  32.1 2.1 %copy-start.2 = (bf16[512,384]{1,0:T(8,128)(2,1)S(1)}, bf16[512,384]{1,0:T(8,128)(2,1)}, u32[]{:S(2)}) copy-start(bf16[512,384]{1,0:T(8,128)(2,1)} %v0_ref.1) | copy-start | bytes 1179652
  32.1 2.1 %copy-start.3 = (bf16[512,384]{1,0:T(8,128)(2,1)S(1)}, bf16[512,384]{1,0:T(8,128)(2,1)}, u32[]{:S(2)}) copy-start(bf16[512,384]{1,0:T(8,128)(2,1)} %q_ref.1) | copy-start | bytes 1179652
  50.4 7.8 %copy-start.10 = (bf16[2,2,512,384]{3,2,1,0:T(8,128)(2,1)S(1)}, bf16[2,2,512,384]{3,2,1,0:T(8,128)(2,1)}, u32[]{:S(2)}) copy-start(bf16[2,2,512,384]{3,2,1,0:T(8,128)(2,1)} %get-tuple-element.13) | copy-start | bytes 4718596
  50.4 6.9 %collective-permute-start.12 = (bf16[2,2,512,384]{3,2,1,0:T(8,128)(2,1)}, bf16[2,2,512,384]{3,2,1,0:T(8,128)(2,1)S(1)}, u32[]{:S(2)}, u32[]{:S(2)}) collective-permute-start(bf16[2,2,512,384]{3,2,1,0:T(8,128)(2,1)} %get-tuple-element.12), channel_id=1, source_target_pairs={{4,0},{12,8},{20,16},{28,24},{36,32},{44,40},{52,48},{60,56},{68,6... | collective-permute-start | bytes 4718600 | tf_op jit(solution)/shard_map/ppermute | solution.py:81
  51.8 6.4 %collective-permute-start.11 = (bf16[2,2,512,384]{3,2,1,0:T(8,128)(2,1)}, bf16[2,2,512,384]{3,2,1,0:T(8,128)(2,1)S(1)}, u32[]{:S(2)}, u32[]{:S(2)}) collective-permute-start(bf16[2,2,512,384]{3,2,1,0:T(8,128)(2,1)} %get-tuple-element.12), channel_id=1, source_target_pairs={{0,4},{8,12},{16,20},{24,28},{32,36},{40,44},{48,52},{56,60},{64,6... | collective-permute-start | bytes 4718600 | tf_op jit(solution)/shard_map/ppermute | solution.py:76
  57.3 2.5 %copy-start.7 = (bf16[2,2,512,384]{3,2,1,0:T(8,128)(2,1)}, bf16[2,2,512,384]{3,2,1,0:T(8,128)(2,1)S(1)}, u32[]{:S(2)}) copy-start(bf16[2,2,512,384]{3,2,1,0:T(8,128)(2,1)S(1)} %collective-permute-done.12) | copy-start | bytes 4718596
  58.1 1.6 %copy-start.9 = (bf16[2,2,512,384]{3,2,1,0:T(8,128)(2,1)}, bf16[2,2,512,384]{3,2,1,0:T(8,128)(2,1)S(1)}, u32[]{:S(2)}) copy-start(bf16[2,2,512,384]{3,2,1,0:T(8,128)(2,1)S(1)} %collective-permute-done.11) | copy-start | bytes 4718596
  59.8 36.9 %collective-permute-start.13 = (bf16[2,512,384]{2,1,0:T(8,128)(2,1)}, bf16[2,512,384]{2,1,0:T(8,128)(2,1)}, u32[]{:S(2)}, u32[]{:S(2)}) collective-permute-start(bf16[2,512,384]{2,1,0:T(8,128)(2,1)} %get-tuple-element.16), channel_id=1, source_target_pairs={{0,8},{4,12},{8,16},{12,20},{16,24},{20,28},{24,32},{28,36},{32,40... | collective-permute-start | bytes 2359304 | tf_op jit(solution)/shard_map/ppermute | solution.py:17
  66.8 29.9 %copy-start.6 = (f32[2,512,384]{2,1,0:T(8,128)S(1)}, f32[2,512,384]{2,1,0:T(8,128)}, u32[]{:S(2)}) copy-start(f32[2,512,384]{2,1,0:T(8,128)} %get-tuple-element.11) | copy-start | bytes 4718596
  66.8 29.9 %collective-permute-start.14 = (bf16[2,512,384]{2,1,0:T(8,128)(2,1)}, bf16[2,512,384]{2,1,0:T(8,128)(2,1)}, u32[]{:S(2)}, u32[]{:S(2)}) collective-permute-start(bf16[2,512,384]{2,1,0:T(8,128)(2,1)} %get-tuple-element.17), channel_id=1, source_target_pairs={{8,0},{12,4},{16,8},{20,12},{24,16},{28,20},{32,24},{36,28},{40,32... | collective-permute-start | bytes 2359304 | tf_op jit(solution)/shard_map/ppermute | solution.py:17
  70.0 20.9 %collective-permute-start.8 = (bf16[512,384]{1,0:T(8,128)(2,1)}, bf16[512,384]{1,0:T(8,128)(2,1)S(1)}, u32[]{:S(2)}, u32[]{:S(2)}) collective-permute-start(bf16[512,384]{1,0:T(8,128)(2,1)} %convolution_convert_fusion.2), channel_id=1, source_target_pairs={{0,1},{1,2},{2,3},{3,0},{4,5},{5,6},{6,7},{7,4},{8,9},{9,10},{10,1... | collective-permute-start | bytes 1179656 | tf_op jit(solution)/shard_map/ppermute | solution.py:22
  73.8 20.5 %collective-permute-start.9 = (bf16[512,384]{1,0:T(8,128)(2,1)}, bf16[512,384]{1,0:T(8,128)(2,1)}, u32[]{:S(2)}, u32[]{:S(2)}) collective-permute-start(bf16[512,384]{1,0:T(8,128)(2,1)} %convolution_convert_fusion.1), channel_id=1, source_target_pairs={{0,3},{1,0},{2,1},{3,2},{4,7},{5,4},{6,5},{7,6},{8,11},{9,8},{10,9... | collective-permute-start | bytes 1179656 | tf_op jit(solution)/shard_map/ppermute | solution.py:22
  73.8 20.5 %collective-permute-start.10 = (bf16[512,384]{1,0:T(8,128)(2,1)}, bf16[512,384]{1,0:T(8,128)(2,1)}, u32[]{:S(2)}, u32[]{:S(2)}) collective-permute-start(bf16[512,384]{1,0:T(8,128)(2,1)} %convolution_convert_fusion), channel_id=1, source_target_pairs={{0,2},{1,3},{2,0},{3,1},{4,6},{5,7},{6,4},{7,5},{8,10},{9,11},{10,... | collective-permute-start | bytes 1179656 | tf_op jit(solution)/shard_map/ppermute | solution.py:22
  75.3 21.4 %copy-start.8 = (bf16[2,2,512,384]{3,2,1,0:T(8,128)(2,1)S(1)}, bf16[2,2,512,384]{3,2,1,0:T(8,128)(2,1)}, u32[]{:S(2)}) copy-start(bf16[2,2,512,384]{3,2,1,0:T(8,128)(2,1)} %copy-done.7) | copy-start | bytes 4718596

commit v7 on v4

--- a/solution.py
+++ b/solution.py
@@ -203,16 +203,15 @@
     cands = (from_left2, partner_own, relay_to_odd, relay_to_even, from_right2)
     attn, grad_q, self_term, near, far = attention(sel, queries, keys, values, cands, grad_attn, shot_ids)
     attn_out = project_out(attn, out_weight)
-    got_a = even_to_odd(near, "seq")
-    got_b = odd_to_even(near, "seq")
-    up_plus = (far[1].astype(jnp.float32) + got_b[1].astype(jnp.float32)).astype(jnp.bfloat16)
-    up_minus = (far[0].astype(jnp.float32) + got_a[0].astype(jnp.float32)).astype(jnp.bfloat16)
+    got = partner_swap(near, "seq").astype(jnp.float32)
+    odd = parity == 1
+    up_plus = (far[1].astype(jnp.float32) + jnp.where(odd, 0.0, got[1])).astype(jnp.bfloat16)
+    up_minus = (far[0].astype(jnp.float32) + jnp.where(odd, got[0], 0.0)).astype(jnp.bfloat16)
     got_from_left = shifted(up_plus, "seq", 2)
     got_from_right = shifted(up_minus, "seq", -2)
     total = (
         self_term
-        + got_a[1].astype(jnp.float32)
-        + got_b[0].astype(jnp.float32)
+        + jnp.where(odd, got[1], got[0])
         + got_from_left.astype(jnp.float32)
         + got_from_right.astype(jnp.float32)
     )

time: 101 us -> 99.6 us (0.986)
  starting transfers between devices: 33.6 us -> 30 us
  other arithmetic: 6.16 us -> 7.51 us
  local copies, waits for them, and re-layouts: 1.16 us -> 2.27 us
    ppermute x2 -> x1, starting transfers between devices: 4.55 us -> 1.33 us  [even_to_odd(): lax.ppermute(block, axis, [(i, i + 1) for i in range(0, size - 1, 2)])]
    ppermute x2 -> x1, starting transfers between devices: 2.7 us -> 1.29 us  [odd_to_even(): return lax.ppermute(block, axis, [(i, i - 1) for i in range(1, size, 2)])]
    unnamed x24 -> x20, local copies, waits for them, and re-layouts: 0.06 us -> 1.17 us
    convert_element_type x1 -> x2, other arithmetic: 1.63 us -> 2.12 us  [the longest x1 1.91 us: on_device(): (far[1].astype(jnp.float32) + jnp.where(odd, 0.0, got[1])).astype(jnp.bfl...]
  transfers between devices with their start and end apart: 15 -> 14, of which waited for: 6 -> 6; matrix products, arithmetic and copies ran while one was open for 12% -> 12% of each run, Pallas kernels for 0% -> 0%
where the time goes in v7:
time: 99.6 us; the launch traced here: 98.7 us
  waiting for transfers between devices  30.4 us (31%)
  starting transfers between devices  30 us (30%)
  Pallas kernels  16.1 us (16%)
  matrix products  11.4 us (11%)
  other arithmetic  7.51 us (8%)
  local copies, waits for them, and re-layouts  2.27 us (2%)
    ppermute x6, waiting for transfers between devices, ring_shift(): lax.ppermute(block, axis, [(i, (i + distance) % size) for i in range(size)])  28.1 us
    ppermute x4, starting transfers between devices, shifted(): return lax.ppermute(block, axis, route)  18.6 us
    pallas_call x1, Pallas kernels, attention(): pl.pallas_call(attn_kernel, grid_spec=grid_spec, out_shape=out_shape, com...  16.1 us
    ppermute x6, starting transfers between devices, ring_shift(): lax.ppermute(block, axis, [(i, (i + distance) % size) for i in range(size)])  8.14 us
    dot_general x4, matrix products, fold_cotangent(): lax.dot_general(piece, w_cols, nt, preferred_element_type=jnp.float32)  5.62 us
    dot_general x3, matrix products, part(): jnp.dot(attn, w_cols, preferred_element_type=jnp.float32)  3.43 us
    convert_element_type x1, other arithmetic, on_device(): rounded = total.astype(jnp.bfloat16)  2.95 us
    dot_general x1, matrix products, project_out(): jnp.dot(attn, head_slice(out_weight, me, width), preferred_element_type=j...  2.34 us
  transfers between devices with their start and end apart: 14, of which 6 were waited for; matrix products, arithmetic and copies ran while one was open for 12% of the time, Pallas kernels for 0%

profile of v7, /device:TPU:126, one launch (start us, length us, event | category | flops | bytes accessed | tf_op | source)
XLA Modules:
  0.0 98.7 jit_solution(18437200956660313172)
XLA Ops:
  0.7 2.2 %pad_maximum_fusion = bf16[2,512,384]{2,1,0:T(8,128)(2,1)} fusion(bf16[1,512,384]{2,1,0:T(8,128)(2,1)} %bitcast.31, bf16[1,512,384]{2,1,0:T(8,128)(2,1)} %bitcast.30), kind=kLoop, calls=%fused_computation.20 | loop fusion | flops 393216 | bytes 1572864 | tf_op jit(solution)/shard_map/stack | solution.py:192
  2.8 2.7 %collective-permute-start.2 = (bf16[2,512,384]{2,1,0:T(8,128)(2,1)}, bf16[2,512,384]{2,1,0:T(8,128)(2,1)S(1)}, u32[]{:S(2)}, u32[]{:S(2)}) collective-permute-start(bf16[2,512,384]{2,1,0:T(8,128)(2,1)} %pad_maximum_fusion), channel_id=1, source_target_pairs={{8,0},{12,4},{16,8},{20,12},{24,16},{28,20},{32,24},{36,28},{40,32... | collective-permute-start | bytes 2359304 | tf_op jit(solution)/shard_map/ppermute | solution.py:17
  5.6 6.4 %collective-permute-start = (bf16[2,512,384]{2,1,0:T(8,128)(2,1)}, bf16[2,512,384]{2,1,0:T(8,128)(2,1)S(1)}, u32[]{:S(2)}, u32[]{:S(2)}) collective-permute-start(bf16[2,512,384]{2,1,0:T(8,128)(2,1)} %pad_maximum_fusion), channel_id=1, source_target_pairs={{0,8},{4,12},{8,16},{12,20},{16,24},{20,28},{24,32},{28,36},{32,40... | collective-permute-start | bytes 2359304 | tf_op jit(solution)/shard_map/ppermute | solution.py:17
  12.0 0.3 collective-permute-start.5
  12.3 2.6 %collective-permute-start.7 = (bf16[512,384]{1,0:T(8,128)(2,1)}, bf16[512,384]{1,0:T(8,128)(2,1)}, u32[]{:S(2)}, u32[]{:S(2)}) collective-permute-start(bf16[512,384]{1,0:T(8,128)(2,1)} %param.11), channel_id=1, source_target_pairs={{0,2},{1,3},{2,0},{3,1},{4,6},{5,7},{6,4},{7,5},{8,10},{9,11},{10,... | collective-permute-start | bytes 1179656 | tf_op jit(solution)/shard_map/ppermute | solution.py:22
  14.9 2.4 %fusion.12 = f32[384,512]{0,1:T(8,128)} fusion(bf16[512,384]{1,0:T(8,128)(2,1)} %param.11, bf16[384,1536]{1,0:T(8,128)(2,1)S(1)} %copy-done, s32[]{:T(128)S(6)} %select_n.97), kind=kOutput, calls=%fused_computation.24 | convolution fusion | flops 150994944 | bytes 1474564 | tf_op jit(solution)/shard_map/dot_general | solution.py:40
  17.8 8.4 %collective-permute-done.7 = bf16[512,384]{1,0:T(8,128)(2,1)} collective-permute-done((bf16[512,384]{1,0:T(8,128)(2,1)}, bf16[512,384]{1,0:T(8,128)(2,1)}, u32[]{:S(2)}, u32[]{:S(2)}) %collective-permute-start.7) | collective-permute-done | bytes 393248 | tf_op jit(solution)/shard_map/ppermute | solution.py:22
  26.2 1.4 %collective-permute-done.2.refs_8_.refs_9_ = bf16[2,512,384]{2,1,0:T(8,128)(2,1)S(1)} collective-permute-done((bf16[2,512,384]{2,1,0:T(8,128)(2,1)}, bf16[2,512,384]{2,1,0:T(8,128)(2,1)S(1)}, u32[]{:S(2)}, u32[]{:S(2)}) %collective-permute-start.2) | collective-permute-done | bytes 786464 | tf_op jit(solution)/shard_map/ppermute | solution.py:17
  27.5 1.3 %collective-permute-start.3 = (bf16[2,512,384]{2,1,0:T(8,128)(2,1)S(1)}, bf16[2,512,384]{2,1,0:T(8,128)(2,1)S(1)}, u32[]{:S(2)}, u32[]{:S(2)}) collective-permute-start(bf16[2,512,384]{2,1,0:T(8,128)(2,1)S(1)} %collective-permute-done.2.refs_8_.refs_9_), channel_id=1, source_target_pairs={{0,4},{8,12},{16,20},{24,28},{32,36},{40,44},{48,52},{56,60},{64,6... | collective-permute-start | bytes 2359304 | tf_op jit(solution)/shard_map/ppermute | solution.py:76
  28.9 1.3 %collective-permute-start.4 = (bf16[2,512,384]{2,1,0:T(8,128)(2,1)S(1)}, bf16[2,512,384]{2,1,0:T(8,128)(2,1)S(1)}, u32[]{:S(2)}, u32[]{:S(2)}) collective-permute-start(bf16[2,512,384]{2,1,0:T(8,128)(2,1)S(1)} %collective-permute-done.refs_0_.refs_1_), channel_id=1, source_target_pairs={{4,0},{12,8},{20,16},{28,24},{36,32},{44,40},{52,48},{60,56},{68,6... | collective-permute-start | bytes 2359304 | tf_op jit(solution)/shard_map/ppermute | solution.py:81
  30.2 1.4 %fusion.15 = f32[384,512]{0,1:T(8,128)S(1)} fusion(bf16[512,384]{1,0:T(8,128)(2,1)} %collective-permute-done.7, bf16[384,1536]{1,0:T(8,128)(2,1)S(1)} %copy-done, s32[]{:T(128)S(6)} %select_n.103), kind=kOutput, calls=%fused_computation.27 | convolution fusion | flops 150994944 | bytes 1474564 | tf_op jit(solution)/shard_map/dot_general | solution.py:40
  31.6 0.4 convolution_add_fusion.2
  32.1 0.7 collective-permute-done.6
  32.7 1.4 %fusion.8.refs_10_ = bf16[512,384]{1,0:T(8,128)(2,1)S(1)} fusion(f32[384,512]{0,1:T(8,128)S(1)} %fusion.15, f32[384,512]{0,1:T(8,128)S(1)} %convolution_add_fusion.2, bf16[512,384]{1,0:T(8,128)(2,1)} %collective-permute-done.6, bf16[384,1536]{1,0:T(8,128)(2,1)S(1)} %copy-done, s32[]{:T(128)S(6)} %select_n.101), kind=kOutput, calls=%fused_computation.17 | convolution fusion | flops 151584768 | bytes 2654212 | tf_op jit(solution)/shard_map/dot_general | solution.py:40
  34.2 16.1 %shard_map.102 = (bf16[512,384]{1,0:T(8,128)(2,1)S(1)}, bf16[512,384]{1,0:T(8,128)(2,1)}, f32[2,512,384]{2,1,0:T(8,128)}, bf16[2,2,512,384]{3,2,1,0:T(8,128)(2,1)}, bf16[2,2,512,384]{3,2,1,0:T(8,128)(2,1)}) custom-call(s32[5]{0:T(128)S(1)} %pad_add_fusion.sel_ref, bf16[512,384]{1,0:T(8,128)(2,1)S(1)} %copy-done.3, bf16[512,384]{1,0:T(8,128)(2,1)S(1)} %copy-done.1, ...), custom_call_target="tpu_custom_call" | custom-call | tf_op jit(solution)/shard_map/pallas_call | solution.py:179
  50.4 0.6 collective-permute-start.11
  51.0 1.1 %convolution_convert_fusion = bf16[512,384]{1,0:T(8,128)(2,1)} fusion(bf16[512,384]{1,0:T(8,128)(2,1)S(1)} %get-tuple-element.9, bf16[384,1536]{1,0:T(8,128)(2,1)S(1)} %copy-done, s32[]{:T(128)S(6)} %select_n.103), kind=kOutput, calls=%fused_computation.14 | convolution fusion | flops 151191552 | bytes 1081348 | tf_op jit(solution)/shard_map/dot_general | solution.py:52
  52.1 1.1 %convolution_convert_fusion.1 = bf16[512,384]{1,0:T(8,128)(2,1)} fusion(bf16[512,384]{1,0:T(8,128)(2,1)S(1)} %get-tuple-element.9, bf16[384,1536]{1,0:T(8,128)(2,1)S(1)} %copy-done, s32[]{:T(128)S(6)} %select_n.99), kind=kOutput, calls=%fused_computation.15 | convolution fusion | flops 151191552 | bytes 1081348 | tf_op jit(solution)/shard_map/dot_general | solution.py:52
  53.3 1.0 collective-permute-done.11
  54.4 0.2 copy-done.7
  54.7 1.9 %fusion.9 = (bf16[2,512,384]{2,1,0:T(8,128)(2,1)}, bf16[2,512,384]{2,1,0:T(8,128)(2,1)}) fusion(f32[2,2,512,384]{3,2,1,0:T(8,128)S(1)} %convert_element_type.67, bf16[2,2,512,384]{3,2,1,0:T(8,128)(2,1)S(1)} %copy-done.7, pred[]{:T(512)S(6)} %eq.29), kind=kLoop, calls=%fused_computation.18 | loop fusion | flops 3145728 | bytes 6291457 | tf_op jit(solution)/shard_map/convert_element_type | solution.py:208
  56.6 7.5 %collective-permute-start.12 = (bf16[2,512,384]{2,1,0:T(8,128)(2,1)}, bf16[2,512,384]{2,1,0:T(8,128)(2,1)S(1)}, u32[]{:S(2)}, u32[]{:S(2)}) collective-permute-start(bf16[2,512,384]{2,1,0:T(8,128)(2,1)} %get-tuple-element.14), channel_id=1, source_target_pairs={{0,8},{4,12},{8,16},{12,20},{16,24},{20,28},{24,32},{28,36},{32,40... | collective-permute-start | bytes 2359304 | tf_op jit(solution)/shard_map/ppermute | solution.py:17
  64.1 1.9 %collective-permute-start.13 = (bf16[2,512,384]{2,1,0:T(8,128)(2,1)}, bf16[2,512,384]{2,1,0:T(8,128)(2,1)S(1)}, u32[]{:S(2)}, u32[]{:S(2)}) collective-permute-start(bf16[2,512,384]{2,1,0:T(8,128)(2,1)} %get-tuple-element.15), channel_id=1, source_target_pairs={{8,0},{12,4},{16,8},{20,12},{24,16},{28,20},{32,24},{36,28},{40,32... | collective-permute-start | bytes 2359304 | tf_op jit(solution)/shard_map/ppermute | solution.py:17
  66.0 1.1 %convolution_convert_fusion.2 = bf16[512,384]{1,0:T(8,128)(2,1)} fusion(bf16[512,384]{1,0:T(8,128)(2,1)S(1)} %get-tuple-element.9, bf16[384,1536]{1,0:T(8,128)(2,1)S(1)} %copy-done, s32[]{:T(128)S(6)} %select_n.101), kind=kOutput, calls=%fused_computation.16 | convolution fusion | flops 151191552 | bytes 1081348 | tf_op jit(solution)/shard_map/dot_general | solution.py:52
  67.2 3.8 %collective-permute-start.8 = (bf16[512,384]{1,0:T(8,128)(2,1)}, bf16[512,384]{1,0:T(8,128)(2,1)S(1)}, u32[]{:S(2)}, u32[]{:S(2)}) collective-permute-start(bf16[512,384]{1,0:T(8,128)(2,1)} %convolution_convert_fusion.2), channel_id=1, source_target_pairs={{0,1},{1,2},{2,3},{3,0},{4,5},{5,6},{6,7},{7,4},{8,9},{9,10},{10,1... | collective-permute-start | bytes 1179656 | tf_op jit(solution)/shard_map/ppermute | solution.py:22
  71.0 1.5 %collective-permute-start.10 = (bf16[512,384]{1,0:T(8,128)(2,1)}, bf16[512,384]{1,0:T(8,128)(2,1)}, u32[]{:S(2)}, u32[]{:S(2)}) collective-permute-start(bf16[512,384]{1,0:T(8,128)(2,1)} %convolution_convert_fusion), channel_id=1, source_target_pairs={{0,2},{1,3},{2,0},{3,1},{4,6},{5,7},{6,4},{7,5},{8,10},{9,11},{10,... | collective-permute-start | bytes 1179656 | tf_op jit(solution)/shard_map/ppermute | solution.py:22
  72.4 15.7 %collective-permute-done.8 = bf16[512,384]{1,0:T(8,128)(2,1)S(1)} collective-permute-done((bf16[512,384]{1,0:T(8,128)(2,1)}, bf16[512,384]{1,0:T(8,128)(2,1)S(1)}, u32[]{:S(2)}, u32[]{:S(2)}) %collective-permute-start.8) | collective-permute-done | bytes 393248 | tf_op jit(solution)/shard_map/ppermute | solution.py:22
  88.1 3.4 %collective-permute-done.9 = bf16[512,384]{1,0:T(8,128)(2,1)} collective-permute-done((bf16[512,384]{1,0:T(8,128)(2,1)}, bf16[512,384]{1,0:T(8,128)(2,1)}, u32[]{:S(2)}, u32[]{:S(2)}) %collective-permute-start.9) | collective-permute-done | bytes 393248 | tf_op jit(solution)/shard_map/ppermute | solution.py:22
  91.5 2.3 %fusion.6 = bf16[512,384]{1,0:T(8,128)(2,1)} fusion(bf16[512,384]{1,0:T(8,128)(2,1)S(1)} %get-tuple-element.9, bf16[512,384]{1,0:T(8,128)(2,1)} %collective-permute-done.10, bf16[512,384]{1,0:T(8,128)(2,1)} %collective-permute-done.9, bf16[512,384]{1,0:T(8,128)(2,1)S(1)} %collective-permute-done.8, bf16[384,1536]{1,0:T(8,128)(2,1)S(1)} %copy-done, ...), kind=kOutput, calls=%fused_computation.12 | convolution fusion | flops 152371200 | bytes 2260996 | tf_op jit(solution)/shard_map/dot_general | solution.py:61
  93.9 0.9 copy-done.8
  94.8 3.0 %fusion.2 = bf16[2,512,384]{2,1,0:T(8,128)(2,1)S(1)} fusion(f32[2,512,384]{2,1,0:T(8,128)} %get-tuple-element.11, bf16[2,512,384]{2,1,0:T(8,128)(2,1)} %copy-done.8, bf16[2,512,384]{2,1,0:T(8,128)(2,1)S(1)} %collective-permute-done.12, f32[2,2,512,384]{3,2,1,0:T(8,128)} %copy-done.5, pred[]{:T(512)S(6)} %eq.29), kind=kLoop, calls=%fused_computation.3 | loop fusion | flops 2752512 | bytes 7077889 | tf_op jit(solution)/shard_map/convert_element_type | solution.py:218
  97.7 1.0 slice_bitcast_fusion
  (34 shorter events, 0.7 us)
Async XLA Ops:
  0.6 14.3 %copy-start = (bf16[384,1536]{1,0:T(8,128)(2,1)S(1)}, bf16[384,1536]{1,0:T(8,128)(2,1)}, u32[]{:S(2)}) copy-start(bf16[384,1536]{1,0:T(8,128)(2,1)} %param.10) | copy-start | bytes 3538948
  0.6 16.6 %copy-start.9 = (s32[64,2]{0,1:T(2,128)S(1)}, s32[64,2]{0,1:T(2,128)}, u32[]{:S(2)}) copy-start(s32[64,2]{0,1:T(2,128)} %param.12) | copy-start | bytes 1540
  0.7 16.9 %copy-start.4 = (s32[512]{0:T(512)S(1)}, s32[512]{0:T(512)}, u32[]{:S(2)}) copy-start(s32[512]{0:T(512)} %param.13) | copy-start | bytes 6148
  2.8 24.7 %collective-permute-start.2 = (bf16[2,512,384]{2,1,0:T(8,128)(2,1)}, bf16[2,512,384]{2,1,0:T(8,128)(2,1)S(1)}, u32[]{:S(2)}, u32[]{:S(2)}) collective-permute-start(bf16[2,512,384]{2,1,0:T(8,128)(2,1)} %pad_maximum_fusion), channel_id=1, source_target_pairs={{8,0},{12,4},{16,8},{20,12},{24,16},{28,20},{32,24},{36,28},{40,32... | collective-permute-start | bytes 2359304 | tf_op jit(solution)/shard_map/ppermute | solution.py:17
  5.6 23.3 %collective-permute-start = (bf16[2,512,384]{2,1,0:T(8,128)(2,1)}, bf16[2,512,384]{2,1,0:T(8,128)(2,1)S(1)}, u32[]{:S(2)}, u32[]{:S(2)}) collective-permute-start(bf16[2,512,384]{2,1,0:T(8,128)(2,1)} %pad_maximum_fusion), channel_id=1, source_target_pairs={{0,8},{4,12},{8,16},{12,20},{16,24},{20,28},{24,32},{28,36},{32,40... | collective-permute-start | bytes 2359304 | tf_op jit(solution)/shard_map/ppermute | solution.py:17
  12.0 19.6 %collective-permute-start.5 = (bf16[512,384]{1,0:T(8,128)(2,1)}, bf16[512,384]{1,0:T(8,128)(2,1)S(1)}, u32[]{:S(2)}, u32[]{:S(2)}) collective-permute-start(bf16[512,384]{1,0:T(8,128)(2,1)} %param.11), channel_id=1, source_target_pairs={{0,1},{1,2},{2,3},{3,0},{4,5},{5,6},{6,7},{7,4},{8,9},{9,10},{10,1... | collective-permute-start | bytes 1179656 | tf_op jit(solution)/shard_map/ppermute | solution.py:22
  12.3 13.9 %collective-permute-start.7 = (bf16[512,384]{1,0:T(8,128)(2,1)}, bf16[512,384]{1,0:T(8,128)(2,1)}, u32[]{:S(2)}, u32[]{:S(2)}) collective-permute-start(bf16[512,384]{1,0:T(8,128)(2,1)} %param.11), channel_id=1, source_target_pairs={{0,2},{1,3},{2,0},{3,1},{4,6},{5,7},{6,4},{7,5},{8,10},{9,11},{10,... | collective-permute-start | bytes 1179656 | tf_op jit(solution)/shard_map/ppermute | solution.py:22
  14.9 17.8 %collective-permute-start.6 = (bf16[512,384]{1,0:T(8,128)(2,1)}, bf16[512,384]{1,0:T(8,128)(2,1)}, u32[]{:S(2)}, u32[]{:S(2)}) collective-permute-start(bf16[512,384]{1,0:T(8,128)(2,1)} %param.11), channel_id=1, source_target_pairs={{0,3},{1,0},{2,1},{3,2},{4,7},{5,4},{6,5},{7,6},{8,11},{9,8},{10,9... | collective-permute-start | bytes 1179656 | tf_op jit(solution)/shard_map/ppermute | solution.py:22
  17.7 13.9 %copy-start.6 = (f32[384,512]{0,1:T(8,128)S(1)}, f32[384,512]{0,1:T(8,128)}, u32[]{:S(2)}) copy-start(f32[384,512]{0,1:T(8,128)} %fusion.12) | copy-start | bytes 2359300
  26.2 8.0 %collective-permute-start.1 = (bf16[2,512,384]{2,1,0:T(8,128)(2,1)}, bf16[2,512,384]{2,1,0:T(8,128)(2,1)S(1)}, u32[]{:S(2)}, u32[]{:S(2)}) collective-permute-start(bf16[2,512,384]{2,1,0:T(8,128)(2,1)} %pad_maximum_fusion), channel_id=1, source_target_pairs={{0,4},{4,0},{8,12},{12,8},{16,20},{20,16},{24,28},{28,24},{32,36},... | collective-permute-start | bytes 2359304 | tf_op jit(solution)/shard_map/ppermute | solution.py:71
  27.5 6.6 %collective-permute-start.3 = (bf16[2,512,384]{2,1,0:T(8,128)(2,1)S(1)}, bf16[2,512,384]{2,1,0:T(8,128)(2,1)S(1)}, u32[]{:S(2)}, u32[]{:S(2)}) collective-permute-start(bf16[2,512,384]{2,1,0:T(8,128)(2,1)S(1)} %collective-permute-done.2.refs_8_.refs_9_), channel_id=1, source_target_pairs={{0,4},{8,12},{16,20},{24,28},{32,36},{40,44},{48,52},{56,60},{64,6... | collective-permute-start | bytes 2359304 | tf_op jit(solution)/shard_map/ppermute | solution.py:76
  28.9 5.3 %collective-permute-start.4 = (bf16[2,512,384]{2,1,0:T(8,128)(2,1)S(1)}, bf16[2,512,384]{2,1,0:T(8,128)(2,1)S(1)}, u32[]{:S(2)}, u32[]{:S(2)}) collective-permute-start(bf16[2,512,384]{2,1,0:T(8,128)(2,1)S(1)} %collective-permute-done.refs_0_.refs_1_), channel_id=1, source_target_pairs={{4,0},{12,8},{20,16},{28,24},{36,32},{44,40},{52,48},{60,56},{68,6... | collective-permute-start | bytes 2359304 | tf_op jit(solution)/shard_map/ppermute | solution.py:81
  32.0 2.1 %copy-start.1 = (bf16[512,384]{1,0:T(8,128)(2,1)S(1)}, bf16[512,384]{1,0:T(8,128)(2,1)}, u32[]{:S(2)}) copy-start(bf16[512,384]{1,0:T(8,128)(2,1)} %k0_ref.1) | copy-start | bytes 1179652
  32.1 2.1 %copy-start.2 = (bf16[512,384]{1,0:T(8,128)(2,1)S(1)}, bf16[512,384]{1,0:T(8,128)(2,1)}, u32[]{:S(2)}) copy-start(bf16[512,384]{1,0:T(8,128)(2,1)} %v0_ref.1) | copy-start | bytes 1179652
  32.1 2.1 %copy-start.3 = (bf16[512,384]{1,0:T(8,128)(2,1)S(1)}, bf16[512,384]{1,0:T(8,128)(2,1)}, u32[]{:S(2)}) copy-start(bf16[512,384]{1,0:T(8,128)(2,1)} %q_ref.1) | copy-start | bytes 1179652
  50.4 3.9 %collective-permute-start.11 = (bf16[2,2,512,384]{3,2,1,0:T(8,128)(2,1)}, bf16[2,2,512,384]{3,2,1,0:T(8,128)(2,1)S(1)}, u32[]{:S(2)}, u32[]{:S(2)}) collective-permute-start(bf16[2,2,512,384]{3,2,1,0:T(8,128)(2,1)} %get-tuple-element.12), channel_id=1, source_target_pairs={{0,4},{4,0},{8,12},{12,8},{16,20},{20,16},{24,28},{28,24},{32,36},... | collective-permute-start | bytes 4718600 | tf_op jit(solution)/shard_map/ppermute | solution.py:71
  53.3 1.4 %copy-start.7 = (bf16[2,2,512,384]{3,2,1,0:T(8,128)(2,1)S(1)}, bf16[2,2,512,384]{3,2,1,0:T(8,128)(2,1)}, u32[]{:S(2)}) copy-start(bf16[2,2,512,384]{3,2,1,0:T(8,128)(2,1)} %get-tuple-element.13) | copy-start | bytes 4718596
  54.4 2.1 %copy-start.5 = (f32[2,2,512,384]{3,2,1,0:T(8,128)}, f32[2,2,512,384]{3,2,1,0:T(8,128)S(1)}, u32[]{:S(2)}) copy-start(f32[2,2,512,384]{3,2,1,0:T(8,128)S(1)} %convert_element_type.67) | copy-start | bytes 9437188
  56.6 37.3 %collective-permute-start.12 = (bf16[2,512,384]{2,1,0:T(8,128)(2,1)}, bf16[2,512,384]{2,1,0:T(8,128)(2,1)S(1)}, u32[]{:S(2)}, u32[]{:S(2)}) collective-permute-start(bf16[2,512,384]{2,1,0:T(8,128)(2,1)} %get-tuple-element.14), channel_id=1, source_target_pairs={{0,8},{4,12},{8,16},{12,20},{16,24},{20,28},{24,32},{28,36},{32,40... | collective-permute-start | bytes 2359304 | tf_op jit(solution)/shard_map/ppermute | solution.py:17
  64.1 29.7 %collective-permute-start.13 = (bf16[2,512,384]{2,1,0:T(8,128)(2,1)}, bf16[2,512,384]{2,1,0:T(8,128)(2,1)S(1)}, u32[]{:S(2)}, u32[]{:S(2)}) collective-permute-start(bf16[2,512,384]{2,1,0:T(8,128)(2,1)} %get-tuple-element.15), channel_id=1, source_target_pairs={{8,0},{12,4},{16,8},{20,12},{24,16},{28,20},{32,24},{36,28},{40,32... | collective-permute-start | bytes 2359304 | tf_op jit(solution)/shard_map/ppermute | solution.py:17
  67.2 20.9 %collective-permute-start.8 = (bf16[512,384]{1,0:T(8,128)(2,1)}, bf16[512,384]{1,0:T(8,128)(2,1)S(1)}, u32[]{:S(2)}, u32[]{:S(2)}) collective-permute-start(bf16[512,384]{1,0:T(8,128)(2,1)} %convolution_convert_fusion.2), channel_id=1, source_target_pairs={{0,1},{1,2},{2,3},{3,0},{4,5},{5,6},{6,7},{7,4},{8,9},{9,10},{10,1... | collective-permute-start | bytes 1179656 | tf_op jit(solution)/shard_map/ppermute | solution.py:22
  71.0 20.5 %collective-permute-start.9 = (bf16[512,384]{1,0:T(8,128)(2,1)}, bf16[512,384]{1,0:T(8,128)(2,1)}, u32[]{:S(2)}, u32[]{:S(2)}) collective-permute-start(bf16[512,384]{1,0:T(8,128)(2,1)} %convolution_convert_fusion.1), channel_id=1, source_target_pairs={{0,3},{1,0},{2,1},{3,2},{4,7},{5,4},{6,5},{7,6},{8,11},{9,8},{10,9... | collective-permute-start | bytes 1179656 | tf_op jit(solution)/shard_map/ppermute | solution.py:22
  71.0 20.5 %collective-permute-start.10 = (bf16[512,384]{1,0:T(8,128)(2,1)}, bf16[512,384]{1,0:T(8,128)(2,1)}, u32[]{:S(2)}, u32[]{:S(2)}) collective-permute-start(bf16[512,384]{1,0:T(8,128)(2,1)} %convolution_convert_fusion), channel_id=1, source_target_pairs={{0,2},{1,3},{2,0},{3,1},{4,6},{5,7},{6,4},{7,5},{8,10},{9,11},{10,... | collective-permute-start | bytes 1179656 | tf_op jit(solution)/shard_map/ppermute | solution.py:22
  93.8 0.9 copy-start.8

commit v8 on v6

--- a/solution.py
+++ b/solution.py
@@ -203,18 +203,17 @@
     cands = (from_left2, partner_own, relay_to_odd, relay_to_even, from_right2)
     attn, grad_q, self_term, near, far = attention(sel, queries, keys, values, cands, grad_attn, shot_ids)
     attn_out = project_out(attn, out_weight)
-    got_a = even_to_odd(near, "seq")
-    got_b = odd_to_even(near, "seq")
-    up_plus = (far[1].astype(jnp.float32) + got_b[1].astype(jnp.float32)).astype(jnp.bfloat16)
-    up_minus = (far[0].astype(jnp.float32) + got_a[0].astype(jnp.float32)).astype(jnp.bfloat16)
+    got = partner_swap(near, "seq").astype(jnp.float32)
+    odd = parity == 1
+    up_plus = (far[1].astype(jnp.float32) + jnp.where(odd, 0.0, got[1])).astype(jnp.bfloat16)
+    up_minus = (far[0].astype(jnp.float32) + jnp.where(odd, got[0], 0.0)).astype(jnp.bfloat16)
     got_from_left = shifted(up_plus, "seq", 2)
     got_from_right = shifted(up_minus, "seq", -2)
 
     def summed(part):
         total = (
             self_term[part]
-            + got_a[1, part].astype(jnp.float32)
-            + got_b[0, part].astype(jnp.float32)
+            + jnp.where(odd, got[1, part], got[0, part])
             + got_from_left[part].astype(jnp.float32)
             + got_from_right[part].astype(jnp.float32)
         )

time: 101 us -> 98.5 us (0.975)
  starting transfers between devices: 33.6 us -> 30.1 us
  other arithmetic: 7 us -> 8.06 us
    ppermute x2 -> x1, starting transfers between devices: 4.55 us -> 1.33 us  [even_to_odd(): lax.ppermute(block, axis, [(i, i + 1) for i in range(0, size - 1, 2)])]
    ppermute x2 -> x1, starting transfers between devices: 2.7 us -> 1.29 us  [odd_to_even(): return lax.ppermute(block, axis, [(i, i - 1) for i in range(1, size, 2)])]
    convert_element_type x1 -> x2, other arithmetic: 1.63 us -> 2.09 us  [the longest x1 1.89 us: on_device(): (far[1].astype(jnp.float32) + jnp.where(odd, 0.0, got[1])).astype(jnp.bfl...]
  transfers between devices with their start and end apart: 15 -> 14, of which waited for: 6 -> 6; matrix products, arithmetic and copies ran while one was open for 12% -> 12% of each run, Pallas kernels for 0% -> 0%
where the time goes in v8:
time: 98.5 us; the launch traced here: 97.5 us
  waiting for transfers between devices  30.4 us (31%)
  starting transfers between devices  30.1 us (31%)
  Pallas kernels  16.1 us (16%)
  matrix products  11.4 us (12%)
  other arithmetic  8.06 us (8%)
    ppermute x6, waiting for transfers between devices, ring_shift(): lax.ppermute(block, axis, [(i, (i + distance) % size) for i in range(size)])  28 us
    ppermute x4, starting transfers between devices, shifted(): return lax.ppermute(block, axis, route)  18.7 us
    pallas_call x1, Pallas kernels, attention(): pl.pallas_call(attn_kernel, grid_spec=grid_spec, out_shape=out_shape, com...  16.1 us
    ppermute x6, starting transfers between devices, ring_shift(): lax.ppermute(block, axis, [(i, (i + distance) % size) for i in range(size)])  8.14 us
    dot_general x4, matrix products, fold_cotangent(): lax.dot_general(piece, w_cols, nt, preferred_element_type=jnp.float32)  5.62 us
    convert_element_type x1, other arithmetic, summed(): return total.astype(jnp.bfloat16)  3.52 us
    dot_general x3, matrix products, part(): jnp.dot(attn, w_cols, preferred_element_type=jnp.float32)  3.43 us
    dot_general x1, matrix products, project_out(): jnp.dot(attn, head_slice(out_weight, me, width), preferred_element_type=j...  2.34 us
  transfers between devices with their start and end apart: 14, of which 6 were waited for; matrix products, arithmetic and copies ran while one was open for 12% of the time, Pallas kernels for 0%

profile of v8, /device:TPU:126, one launch (start us, length us, event | category | flops | bytes accessed | tf_op | source)
XLA Modules:
  0.0 97.5 jit_solution(5427116059884761997)
XLA Ops:
  0.7 2.2 %pad_maximum_fusion = bf16[2,512,384]{2,1,0:T(8,128)(2,1)} fusion(bf16[1,512,384]{2,1,0:T(8,128)(2,1)} %bitcast.63, bf16[1,512,384]{2,1,0:T(8,128)(2,1)} %bitcast.62), kind=kLoop, calls=%fused_computation.32 | loop fusion | flops 393216 | bytes 1572864 | tf_op jit(solution)/shard_map/stack | solution.py:192
  2.8 2.7 %collective-permute-start.2 = (bf16[2,512,384]{2,1,0:T(8,128)(2,1)}, bf16[2,512,384]{2,1,0:T(8,128)(2,1)S(1)}, u32[]{:S(2)}, u32[]{:S(2)}) collective-permute-start(bf16[2,512,384]{2,1,0:T(8,128)(2,1)} %pad_maximum_fusion), channel_id=1, source_target_pairs={{8,0},{12,4},{16,8},{20,12},{24,16},{28,20},{32,24},{36,28},{40,32... | collective-permute-start | bytes 2359304 | tf_op jit(solution)/shard_map/ppermute | solution.py:17
  5.6 6.4 %collective-permute-start = (bf16[2,512,384]{2,1,0:T(8,128)(2,1)}, bf16[2,512,384]{2,1,0:T(8,128)(2,1)S(1)}, u32[]{:S(2)}, u32[]{:S(2)}) collective-permute-start(bf16[2,512,384]{2,1,0:T(8,128)(2,1)} %pad_maximum_fusion), channel_id=1, source_target_pairs={{0,8},{4,12},{8,16},{12,20},{16,24},{20,28},{24,32},{28,36},{32,40... | collective-permute-start | bytes 2359304 | tf_op jit(solution)/shard_map/ppermute | solution.py:17
  12.0 0.3 collective-permute-start.5
  12.3 2.6 %collective-permute-start.7 = (bf16[512,384]{1,0:T(8,128)(2,1)}, bf16[512,384]{1,0:T(8,128)(2,1)}, u32[]{:S(2)}, u32[]{:S(2)}) collective-permute-start(bf16[512,384]{1,0:T(8,128)(2,1)} %param.11), channel_id=1, source_target_pairs={{0,2},{1,3},{2,0},{3,1},{4,6},{5,7},{6,4},{7,5},{8,10},{9,11},{10,... | collective-permute-start | bytes 1179656 | tf_op jit(solution)/shard_map/ppermute | solution.py:22
  14.9 2.4 %fusion.23 = f32[384,512]{0,1:T(8,128)} fusion(bf16[512,384]{1,0:T(8,128)(2,1)} %param.11, bf16[384,1536]{1,0:T(8,128)(2,1)S(1)} %copy-done, s32[]{:T(128)S(6)} %select_n.106), kind=kOutput, calls=%fused_computation.38 | convolution fusion | flops 150994944 | bytes 1474564 | tf_op jit(solution)/shard_map/dot_general | solution.py:40
  17.3 0.2 fusion.41
  17.8 8.4 %collective-permute-done.7 = bf16[512,384]{1,0:T(8,128)(2,1)} collective-permute-done((bf16[512,384]{1,0:T(8,128)(2,1)}, bf16[512,384]{1,0:T(8,128)(2,1)}, u32[]{:S(2)}, u32[]{:S(2)}) %collective-permute-start.7) | collective-permute-done | bytes 393248 | tf_op jit(solution)/shard_map/ppermute | solution.py:22
  26.2 1.4 %collective-permute-done.2.refs_8_.refs_9_ = bf16[2,512,384]{2,1,0:T(8,128)(2,1)S(1)} collective-permute-done((bf16[2,512,384]{2,1,0:T(8,128)(2,1)}, bf16[2,512,384]{2,1,0:T(8,128)(2,1)S(1)}, u32[]{:S(2)}, u32[]{:S(2)}) %collective-permute-start.2) | collective-permute-done | bytes 786464 | tf_op jit(solution)/shard_map/ppermute | solution.py:17
  27.5 1.3 %collective-permute-start.3 = (bf16[2,512,384]{2,1,0:T(8,128)(2,1)S(1)}, bf16[2,512,384]{2,1,0:T(8,128)(2,1)S(1)}, u32[]{:S(2)}, u32[]{:S(2)}) collective-permute-start(bf16[2,512,384]{2,1,0:T(8,128)(2,1)S(1)} %collective-permute-done.2.refs_8_.refs_9_), channel_id=1, source_target_pairs={{0,4},{8,12},{16,20},{24,28},{32,36},{40,44},{48,52},{56,60},{64,6... | collective-permute-start | bytes 2359304 | tf_op jit(solution)/shard_map/ppermute | solution.py:76
  28.9 1.3 %collective-permute-start.4 = (bf16[2,512,384]{2,1,0:T(8,128)(2,1)S(1)}, bf16[2,512,384]{2,1,0:T(8,128)(2,1)S(1)}, u32[]{:S(2)}, u32[]{:S(2)}) collective-permute-start(bf16[2,512,384]{2,1,0:T(8,128)(2,1)S(1)} %collective-permute-done.refs_0_.refs_1_), channel_id=1, source_target_pairs={{4,0},{12,8},{20,16},{28,24},{36,32},{44,40},{52,48},{60,56},{68,6... | collective-permute-start | bytes 2359304 | tf_op jit(solution)/shard_map/ppermute | solution.py:81
  30.2 1.4 %fusion.26 = f32[384,512]{0,1:T(8,128)S(1)} fusion(bf16[512,384]{1,0:T(8,128)(2,1)} %collective-permute-done.7, bf16[384,1536]{1,0:T(8,128)(2,1)S(1)} %copy-done, s32[]{:T(128)S(6)} %select_n.112), kind=kOutput, calls=%fused_computation.41 | convolution fusion | flops 150994944 | bytes 1474564 | tf_op jit(solution)/shard_map/dot_general | solution.py:40
  31.6 0.4 convolution_add_fusion.2
  32.1 0.7 collective-permute-done.6
  32.7 1.4 %fusion.9.refs_10_ = bf16[512,384]{1,0:T(8,128)(2,1)S(1)} fusion(f32[384,512]{0,1:T(8,128)S(1)} %fusion.26, f32[384,512]{0,1:T(8,128)S(1)} %convolution_add_fusion.2, bf16[512,384]{1,0:T(8,128)(2,1)} %collective-permute-done.6, bf16[384,1536]{1,0:T(8,128)(2,1)S(1)} %copy-done, s32[]{:T(128)S(6)} %select_n.110), kind=kOutput, calls=%fused_computation.17 | convolution fusion | flops 151584768 | bytes 2654212 | tf_op jit(solution)/shard_map/dot_general | solution.py:40
  34.2 16.1 %shard_map.102 = (bf16[512,384]{1,0:T(8,128)(2,1)S(1)}, bf16[512,384]{1,0:T(8,128)(2,1)}, f32[2,512,384]{2,1,0:T(8,128)}, bf16[2,2,512,384]{3,2,1,0:T(8,128)(2,1)}, bf16[2,2,512,384]{3,2,1,0:T(8,128)(2,1)}) custom-call(s32[5]{0:T(128)S(1)} %pad_add_fusion.sel_ref, bf16[512,384]{1,0:T(8,128)(2,1)S(1)} %copy-done.3, bf16[512,384]{1,0:T(8,128)(2,1)S(1)} %copy-done.1, ...), custom_call_target="tpu_custom_call" | custom-call | tf_op jit(solution)/shard_map/pallas_call | solution.py:179
  50.4 0.6 collective-permute-start.11
  51.0 1.1 %convolution_convert_fusion = bf16[512,384]{1,0:T(8,128)(2,1)} fusion(bf16[512,384]{1,0:T(8,128)(2,1)S(1)} %get-tuple-element.9, bf16[384,1536]{1,0:T(8,128)(2,1)S(1)} %copy-done, s32[]{:T(128)S(6)} %select_n.112), kind=kOutput, calls=%fused_computation.14 | convolution fusion | flops 151191552 | bytes 1081348 | tf_op jit(solution)/shard_map/dot_general | solution.py:52
  52.1 1.1 %convolution_convert_fusion.1 = bf16[512,384]{1,0:T(8,128)(2,1)} fusion(bf16[512,384]{1,0:T(8,128)(2,1)S(1)} %get-tuple-element.9, bf16[384,1536]{1,0:T(8,128)(2,1)S(1)} %copy-done, s32[]{:T(128)S(6)} %select_n.108), kind=kOutput, calls=%fused_computation.15 | convolution fusion | flops 151191552 | bytes 1081348 | tf_op jit(solution)/shard_map/dot_general | solution.py:52
  53.3 1.0 collective-permute-done.11
  54.2 0.2 convert_element_type.88
  54.4 0.2 copy-done.8
  54.7 1.9 %fusion.10 = (bf16[2,512,384]{2,1,0:T(8,128)(2,1)}, bf16[2,512,384]{2,1,0:T(8,128)(2,1)}) fusion(f32[2,2,512,384]{3,2,1,0:T(8,128)S(1)} %convert_element_type.88, bf16[2,2,512,384]{3,2,1,0:T(8,128)(2,1)S(1)} %copy-done.8, pred[]{:T(512)S(6)} %eq.29), kind=kLoop, calls=%fused_computation.18 | loop fusion | flops 3145728 | bytes 6291457 | tf_op jit(solution)/shard_map/convert_element_type | solution.py:208
  56.6 7.5 %collective-permute-start.12 = (bf16[2,512,384]{2,1,0:T(8,128)(2,1)}, bf16[2,512,384]{2,1,0:T(8,128)(2,1)}, u32[]{:S(2)}, u32[]{:S(2)}) collective-permute-start(bf16[2,512,384]{2,1,0:T(8,128)(2,1)} %get-tuple-element.16), channel_id=1, source_target_pairs={{0,8},{4,12},{8,16},{12,20},{16,24},{20,28},{24,32},{28,36},{32,40... | collective-permute-start | bytes 2359304 | tf_op jit(solution)/shard_map/ppermute | solution.py:17
  64.1 2.1 %collective-permute-start.13 = (bf16[2,512,384]{2,1,0:T(8,128)(2,1)}, bf16[2,512,384]{2,1,0:T(8,128)(2,1)}, u32[]{:S(2)}, u32[]{:S(2)}) collective-permute-start(bf16[2,512,384]{2,1,0:T(8,128)(2,1)} %get-tuple-element.17), channel_id=1, source_target_pairs={{8,0},{12,4},{16,8},{20,12},{24,16},{28,20},{32,24},{36,28},{40,32... | collective-permute-start | bytes 2359304 | tf_op jit(solution)/shard_map/ppermute | solution.py:17
  66.2 1.1 %convolution_convert_fusion.2 = bf16[512,384]{1,0:T(8,128)(2,1)} fusion(bf16[512,384]{1,0:T(8,128)(2,1)S(1)} %get-tuple-element.9, bf16[384,1536]{1,0:T(8,128)(2,1)S(1)} %copy-done, s32[]{:T(128)S(6)} %select_n.110), kind=kOutput, calls=%fused_computation.16 | convolution fusion | flops 151191552 | bytes 1081348 | tf_op jit(solution)/shard_map/dot_general | solution.py:52
  67.3 3.8 %collective-permute-start.8 = (bf16[512,384]{1,0:T(8,128)(2,1)}, bf16[512,384]{1,0:T(8,128)(2,1)S(1)}, u32[]{:S(2)}, u32[]{:S(2)}) collective-permute-start(bf16[512,384]{1,0:T(8,128)(2,1)} %convolution_convert_fusion.2), channel_id=1, source_target_pairs={{0,1},{1,2},{2,3},{3,0},{4,5},{5,6},{6,7},{7,4},{8,9},{9,10},{10,1... | collective-permute-start | bytes 1179656 | tf_op jit(solution)/shard_map/ppermute | solution.py:22
  71.1 1.5 %collective-permute-start.10 = (bf16[512,384]{1,0:T(8,128)(2,1)}, bf16[512,384]{1,0:T(8,128)(2,1)}, u32[]{:S(2)}, u32[]{:S(2)}) collective-permute-start(bf16[512,384]{1,0:T(8,128)(2,1)} %convolution_convert_fusion), channel_id=1, source_target_pairs={{0,2},{1,3},{2,0},{3,1},{4,6},{5,7},{6,4},{7,5},{8,10},{9,11},{10,... | collective-permute-start | bytes 1179656 | tf_op jit(solution)/shard_map/ppermute | solution.py:22
  72.6 15.6 %collective-permute-done.8 = bf16[512,384]{1,0:T(8,128)(2,1)S(1)} collective-permute-done((bf16[512,384]{1,0:T(8,128)(2,1)}, bf16[512,384]{1,0:T(8,128)(2,1)S(1)}, u32[]{:S(2)}, u32[]{:S(2)}) %collective-permute-start.8) | collective-permute-done | bytes 393248 | tf_op jit(solution)/shard_map/ppermute | solution.py:22
  88.2 3.4 %collective-permute-done.9 = bf16[512,384]{1,0:T(8,128)(2,1)} collective-permute-done((bf16[512,384]{1,0:T(8,128)(2,1)}, bf16[512,384]{1,0:T(8,128)(2,1)}, u32[]{:S(2)}, u32[]{:S(2)}) %collective-permute-start.9) | collective-permute-done | bytes 393248 | tf_op jit(solution)/shard_map/ppermute | solution.py:22
  91.6 2.3 %fusion.7 = bf16[512,384]{1,0:T(8,128)(2,1)} fusion(bf16[512,384]{1,0:T(8,128)(2,1)S(1)} %get-tuple-element.9, bf16[512,384]{1,0:T(8,128)(2,1)} %collective-permute-done.10, bf16[512,384]{1,0:T(8,128)(2,1)} %collective-permute-done.9, bf16[512,384]{1,0:T(8,128)(2,1)S(1)} %collective-permute-done.8, bf16[384,1536]{1,0:T(8,128)(2,1)S(1)} %copy-done, ...), kind=kOutput, calls=%fused_computation.12 | convolution fusion | flops 152371200 | bytes 2260996 | tf_op jit(solution)/shard_map/dot_general | solution.py:61
  93.9 3.5 %fusion.16 = (bf16[512,384]{1,0:T(8,128)(2,1)}, bf16[512,384]{1,0:T(8,128)(2,1)}) fusion(f32[2,2,512,384]{3,2,1,0:T(8,128)} %copy-done.5, f32[2,512,384]{2,1,0:T(8,128)S(1)} %copy-done.7, bf16[2,512,384]{2,1,0:T(8,128)(2,1)} %collective-permute-done.13, bf16[2,512,384]{2,1,0:T(8,128)(2,1)} %collective-permute-done.12, pred[]{:T(512)S(6)} %eq.29), kind=kLoop, calls=%fused_computation.25 | loop fusion | flops 2752512 | bytes 7077889 | tf_op jit(solution)/shard_map/convert_element_type | solution.py:220
  (33 shorter events, 0.3 us)
Async XLA Ops:
  0.6 14.3 %copy-start = (bf16[384,1536]{1,0:T(8,128)(2,1)S(1)}, bf16[384,1536]{1,0:T(8,128)(2,1)}, u32[]{:S(2)}) copy-start(bf16[384,1536]{1,0:T(8,128)(2,1)} %param.10) | copy-start | bytes 3538948
  0.6 16.6 %copy-start.9 = (s32[64,2]{0,1:T(2,128)S(1)}, s32[64,2]{0,1:T(2,128)}, u32[]{:S(2)}) copy-start(s32[64,2]{0,1:T(2,128)} %param.12) | copy-start | bytes 1540
  0.7 16.9 %copy-start.4 = (s32[512]{0:T(512)S(1)}, s32[512]{0:T(512)}, u32[]{:S(2)}) copy-start(s32[512]{0:T(512)} %param.13) | copy-start | bytes 6148
  2.8 24.7 %collective-permute-start.2 = (bf16[2,512,384]{2,1,0:T(8,128)(2,1)}, bf16[2,512,384]{2,1,0:T(8,128)(2,1)S(1)}, u32[]{:S(2)}, u32[]{:S(2)}) collective-permute-start(bf16[2,512,384]{2,1,0:T(8,128)(2,1)} %pad_maximum_fusion), channel_id=1, source_target_pairs={{8,0},{12,4},{16,8},{20,12},{24,16},{28,20},{32,24},{36,28},{40,32... | collective-permute-start | bytes 2359304 | tf_op jit(solution)/shard_map/ppermute | solution.py:17
  5.6 23.3 %collective-permute-start = (bf16[2,512,384]{2,1,0:T(8,128)(2,1)}, bf16[2,512,384]{2,1,0:T(8,128)(2,1)S(1)}, u32[]{:S(2)}, u32[]{:S(2)}) collective-permute-start(bf16[2,512,384]{2,1,0:T(8,128)(2,1)} %pad_maximum_fusion), channel_id=1, source_target_pairs={{0,8},{4,12},{8,16},{12,20},{16,24},{20,28},{24,32},{28,36},{32,40... | collective-permute-start | bytes 2359304 | tf_op jit(solution)/shard_map/ppermute | solution.py:17
  12.0 19.6 %collective-permute-start.5 = (bf16[512,384]{1,0:T(8,128)(2,1)}, bf16[512,384]{1,0:T(8,128)(2,1)S(1)}, u32[]{:S(2)}, u32[]{:S(2)}) collective-permute-start(bf16[512,384]{1,0:T(8,128)(2,1)} %param.11), channel_id=1, source_target_pairs={{0,1},{1,2},{2,3},{3,0},{4,5},{5,6},{6,7},{7,4},{8,9},{9,10},{10,1... | collective-permute-start | bytes 1179656 | tf_op jit(solution)/shard_map/ppermute | solution.py:22
  12.3 13.9 %collective-permute-start.7 = (bf16[512,384]{1,0:T(8,128)(2,1)}, bf16[512,384]{1,0:T(8,128)(2,1)}, u32[]{:S(2)}, u32[]{:S(2)}) collective-permute-start(bf16[512,384]{1,0:T(8,128)(2,1)} %param.11), channel_id=1, source_target_pairs={{0,2},{1,3},{2,0},{3,1},{4,6},{5,7},{6,4},{7,5},{8,10},{9,11},{10,... | collective-permute-start | bytes 1179656 | tf_op jit(solution)/shard_map/ppermute | solution.py:22
  14.9 17.8 %collective-permute-start.6 = (bf16[512,384]{1,0:T(8,128)(2,1)}, bf16[512,384]{1,0:T(8,128)(2,1)}, u32[]{:S(2)}, u32[]{:S(2)}) collective-permute-start(bf16[512,384]{1,0:T(8,128)(2,1)} %param.11), channel_id=1, source_target_pairs={{0,3},{1,0},{2,1},{3,2},{4,7},{5,4},{6,5},{7,6},{8,11},{9,8},{10,9... | collective-permute-start | bytes 1179656 | tf_op jit(solution)/shard_map/ppermute | solution.py:22
  17.7 13.9 %copy-start.6 = (f32[384,512]{0,1:T(8,128)S(1)}, f32[384,512]{0,1:T(8,128)}, u32[]{:S(2)}) copy-start(f32[384,512]{0,1:T(8,128)} %fusion.23) | copy-start | bytes 2359300
  26.2 8.0 %collective-permute-start.1 = (bf16[2,512,384]{2,1,0:T(8,128)(2,1)}, bf16[2,512,384]{2,1,0:T(8,128)(2,1)S(1)}, u32[]{:S(2)}, u32[]{:S(2)}) collective-permute-start(bf16[2,512,384]{2,1,0:T(8,128)(2,1)} %pad_maximum_fusion), channel_id=1, source_target_pairs={{0,4},{4,0},{8,12},{12,8},{16,20},{20,16},{24,28},{28,24},{32,36},... | collective-permute-start | bytes 2359304 | tf_op jit(solution)/shard_map/ppermute | solution.py:71
  27.5 6.6 %collective-permute-start.3 = (bf16[2,512,384]{2,1,0:T(8,128)(2,1)S(1)}, bf16[2,512,384]{2,1,0:T(8,128)(2,1)S(1)}, u32[]{:S(2)}, u32[]{:S(2)}) collective-permute-start(bf16[2,512,384]{2,1,0:T(8,128)(2,1)S(1)} %collective-permute-done.2.refs_8_.refs_9_), channel_id=1, source_target_pairs={{0,4},{8,12},{16,20},{24,28},{32,36},{40,44},{48,52},{56,60},{64,6... | collective-permute-start | bytes 2359304 | tf_op jit(solution)/shard_map/ppermute | solution.py:76
  28.9 5.3 %collective-permute-start.4 = (bf16[2,512,384]{2,1,0:T(8,128)(2,1)S(1)}, bf16[2,512,384]{2,1,0:T(8,128)(2,1)S(1)}, u32[]{:S(2)}, u32[]{:S(2)}) collective-permute-start(bf16[2,512,384]{2,1,0:T(8,128)(2,1)S(1)} %collective-permute-done.refs_0_.refs_1_), channel_id=1, source_target_pairs={{4,0},{12,8},{20,16},{28,24},{36,32},{44,40},{52,48},{60,56},{68,6... | collective-permute-start | bytes 2359304 | tf_op jit(solution)/shard_map/ppermute | solution.py:81
  32.0 2.1 %copy-start.1 = (bf16[512,384]{1,0:T(8,128)(2,1)S(1)}, bf16[512,384]{1,0:T(8,128)(2,1)}, u32[]{:S(2)}) copy-start(bf16[512,384]{1,0:T(8,128)(2,1)} %k0_ref.1) | copy-start | bytes 1179652
  32.1 2.1 %copy-start.2 = (bf16[512,384]{1,0:T(8,128)(2,1)S(1)}, bf16[512,384]{1,0:T(8,128)(2,1)}, u32[]{:S(2)}) copy-start(bf16[512,384]{1,0:T(8,128)(2,1)} %v0_ref.1) | copy-start | bytes 1179652
  32.1 2.1 %copy-start.3 = (bf16[512,384]{1,0:T(8,128)(2,1)S(1)}, bf16[512,384]{1,0:T(8,128)(2,1)}, u32[]{:S(2)}) copy-start(bf16[512,384]{1,0:T(8,128)(2,1)} %q_ref.1) | copy-start | bytes 1179652
  50.4 3.9 %collective-permute-start.11 = (bf16[2,2,512,384]{3,2,1,0:T(8,128)(2,1)}, bf16[2,2,512,384]{3,2,1,0:T(8,128)(2,1)S(1)}, u32[]{:S(2)}, u32[]{:S(2)}) collective-permute-start(bf16[2,2,512,384]{3,2,1,0:T(8,128)(2,1)} %get-tuple-element.12), channel_id=1, source_target_pairs={{0,4},{4,0},{8,12},{12,8},{16,20},{20,16},{24,28},{28,24},{32,36},... | collective-permute-start | bytes 4718600 | tf_op jit(solution)/shard_map/ppermute | solution.py:71
  53.3 1.4 %copy-start.8 = (bf16[2,2,512,384]{3,2,1,0:T(8,128)(2,1)S(1)}, bf16[2,2,512,384]{3,2,1,0:T(8,128)(2,1)}, u32[]{:S(2)}) copy-start(bf16[2,2,512,384]{3,2,1,0:T(8,128)(2,1)} %get-tuple-element.13) | copy-start | bytes 4718596
  54.4 2.1 %copy-start.5 = (f32[2,2,512,384]{3,2,1,0:T(8,128)}, f32[2,2,512,384]{3,2,1,0:T(8,128)S(1)}, u32[]{:S(2)}) copy-start(f32[2,2,512,384]{3,2,1,0:T(8,128)S(1)} %convert_element_type.88) | copy-start | bytes 9437188
  56.6 37.4 %collective-permute-start.12 = (bf16[2,512,384]{2,1,0:T(8,128)(2,1)}, bf16[2,512,384]{2,1,0:T(8,128)(2,1)}, u32[]{:S(2)}, u32[]{:S(2)}) collective-permute-start(bf16[2,512,384]{2,1,0:T(8,128)(2,1)} %get-tuple-element.16), channel_id=1, source_target_pairs={{0,8},{4,12},{8,16},{12,20},{16,24},{20,28},{24,32},{28,36},{32,40... | collective-permute-start | bytes 2359304 | tf_op jit(solution)/shard_map/ppermute | solution.py:17
  64.1 29.9 %copy-start.7 = (f32[2,512,384]{2,1,0:T(8,128)S(1)}, f32[2,512,384]{2,1,0:T(8,128)}, u32[]{:S(2)}) copy-start(f32[2,512,384]{2,1,0:T(8,128)} %get-tuple-element.11) | copy-start | bytes 4718596
  64.1 29.8 %collective-permute-start.13 = (bf16[2,512,384]{2,1,0:T(8,128)(2,1)}, bf16[2,512,384]{2,1,0:T(8,128)(2,1)}, u32[]{:S(2)}, u32[]{:S(2)}) collective-permute-start(bf16[2,512,384]{2,1,0:T(8,128)(2,1)} %get-tuple-element.17), channel_id=1, source_target_pairs={{8,0},{12,4},{16,8},{20,12},{24,16},{28,20},{32,24},{36,28},{40,32... | collective-permute-start | bytes 2359304 | tf_op jit(solution)/shard_map/ppermute | solution.py:17
  67.3 20.9 %collective-permute-start.8 = (bf16[512,384]{1,0:T(8,128)(2,1)}, bf16[512,384]{1,0:T(8,128)(2,1)S(1)}, u32[]{:S(2)}, u32[]{:S(2)}) collective-permute-start(bf16[512,384]{1,0:T(8,128)(2,1)} %convolution_convert_fusion.2), channel_id=1, source_target_pairs={{0,1},{1,2},{2,3},{3,0},{4,5},{5,6},{6,7},{7,4},{8,9},{9,10},{10,1... | collective-permute-start | bytes 1179656 | tf_op jit(solution)/shard_map/ppermute | solution.py:22
  71.1 20.5 %collective-permute-start.9 = (bf16[512,384]{1,0:T(8,128)(2,1)}, bf16[512,384]{1,0:T(8,128)(2,1)}, u32[]{:S(2)}, u32[]{:S(2)}) collective-permute-start(bf16[512,384]{1,0:T(8,128)(2,1)} %convolution_convert_fusion.1), channel_id=1, source_target_pairs={{0,3},{1,0},{2,1},{3,2},{4,7},{5,4},{6,5},{7,6},{8,11},{9,8},{10,9... | collective-permute-start | bytes 1179656 | tf_op jit(solution)/shard_map/ppermute | solution.py:22
  71.1 20.5 %collective-permute-start.10 = (bf16[512,384]{1,0:T(8,128)(2,1)}, bf16[512,384]{1,0:T(8,128)(2,1)}, u32[]{:S(2)}, u32[]{:S(2)}) collective-permute-start(bf16[512,384]{1,0:T(8,128)(2,1)} %convolution_convert_fusion), channel_id=1, source_target_pairs={{0,2},{1,3},{2,0},{3,1},{4,6},{5,7},{6,4},{7,5},{8,10},{9,11},{10,... | collective-permute-start | bytes 1179656 | tf_op jit(solution)/shard_map/ppermute | solution.py:22
